TPU v7x, 256 devices: a whole 4x4x8 slice. The times are simulated.
256 devices in a mesh: dp: 4 (over y), head: 4 (over x), seq: 16 (over z, core).
Axes of the slice: x: 4, y: 4, z: 8, core: 2. Of those that a mesh axis runs over, the one named last changes fastest.
Arguments:
- q_dense: bfloat16 [32768, 8, 128], P(('dp', 'seq'), 'head'), parts along dimension 0, may hold values from -108 to 108
- k_dense: bfloat16 [32768, 8, 128], P(('dp', 'seq'), 'head'), parts along dimension 0, may hold values from -4 to 4
- v_dense: bfloat16 [32768, 8, 128], P(('dp', 'seq'), 'head'), parts along dimension 0, may hold values from -4 to 4
- q_expert: bfloat16 [32768, 12, 128], P(('dp', 'seq'), 'head'), parts along dimension 0, may hold values from -108 to 108
- k_expert: bfloat16 [32768, 12, 128], P(('dp', 'seq'), 'head'), parts along dimension 0, may hold values from -4 to 4
- v_expert: bfloat16 [32768, 12, 128], P(('dp', 'seq'), 'head'), parts along dimension 0, may hold values from -4 to 4
- gate_logit: bfloat16 [12, 32768], P('head', ('dp', 'seq')), parts along dimension 1, may hold values from -8 to 8
- selection: int32 [12, 2048], P('head', 'dp'), parts along dimension 1, may hold values from 0 to 8191, as said below
Outputs:
- dense_out: bfloat16 [32768, 8, 128], P(('dp', 'seq'), 'head'), parts along dimension 0
- expert_out: bfloat16 [32768, 12, 128], P(('dp', 'seq'), 'head'), parts along dimension 0
There are 4 independent parts, one for each index of `dp`. A program takes and returns all parts, laid end to end along the dimension named above; each array names one. Nothing has to cross between parts.
Inputs may be any that keep to these rules, and one draw needn't show every extreme that they name: `selection`: each row lists 512 distinct token positions in increasing order; every row holds the first and the last token.
All inputs are finite; a program needn't handle non-finite values.
Results may differ from a plain program's by a relative error of at most 0.0055.
Values may be sent and summed in bfloat16 or wider, within the bound.
No kernel may reach another device: no remote copies, remote signals or barrier semaphores. Data moves between devices by JAX's collectives and lax.ppermute only.
A program may use at most 64 MiB of HBM per device.

v0:
```python
import math

import jax
import jax.numpy as jnp
from jax import lax
from jax.sharding import PartitionSpec as P

NEGATIVE = -1e30


def plain_rows(rows, tok_rows, count):
    return rows


def online_update(state, queries, query_pos, keys, values, key_pos, scale):
    leading, total, summed = state
    scores = jnp.einsum("qhd,khd->qhk", queries, keys, preferred_element_type=jnp.float32) * scale
    visible = key_pos[None, None, :] <= query_pos[:, None, None]
    scores = jnp.where(visible, scores, NEGATIVE)
    new_leading = jnp.maximum(leading, jnp.max(scores, axis=2))
    shrink = jnp.exp(leading - new_leading)
    weights = jnp.where(visible, jnp.exp(scores - new_leading[:, :, None]), 0.0)
    total = total * shrink + jnp.sum(weights, axis=2)
    moved = jnp.einsum(
        "qhk,khd->qhd", weights.astype(jnp.bfloat16), values, preferred_element_type=jnp.float32
    )
    return (new_leading, total, summed * shrink[:, :, None] + moved)


def dense_heads(queries, keys, values, position_map):
    tok_rows, heads, width = queries.shape
    count = lax.axis_size("seq")
    half_rows = tok_rows // 2
    own_rows = lax.axis_index("seq") * tok_rows + jnp.arange(tok_rows, dtype=jnp.int32)
    query_pos = position_map(own_rows, tok_rows, count).reshape(2, half_rows)
    groups = queries.reshape(2, half_rows, heads, width)
    scale = 1.0 / math.sqrt(width)
    blank = (
        jnp.full((half_rows, heads), NEGATIVE, jnp.float32),
        jnp.zeros((half_rows, heads), jnp.float32),
        jnp.zeros((half_rows, heads, width), jnp.float32),
    )
    key_rows = lax.all_gather(keys, "seq", axis=0, tiled=True)
    value_rows = lax.all_gather(values, "seq", axis=0, tiled=True)
    length = key_rows.shape[0]
    block = math.gcd(length, 512)
    count_blocks = length // block
    key_pos = position_map(jnp.arange(length, dtype=jnp.int32), tok_rows, count).reshape(
        count_blocks, block
    )
    key_blocks = key_rows.reshape(count_blocks, block, heads, width)
    value_blocks = value_rows.reshape(count_blocks, block, heads, width)

    def advance(state, item):
        key_block, value_block, block_pos = item
        result = []
        for group in range(2):
            seen = jnp.min(block_pos) <= jnp.max(query_pos[group])
            result.append(
                lax.cond(
                    seen,
                    lambda inner, member=group: online_update(
                        inner,
                        groups[member],
                        query_pos[member],
                        key_block,
                        value_block,
                        block_pos,
                        scale,
                    ),
                    lambda inner: inner,
                    state[group],
                )
            )
        return (tuple(result), None)

    final_state, unused = lax.scan(advance, (blank, blank), (key_blocks, value_blocks, key_pos))
    outputs = [
        (summed / total[:, :, None]).astype(jnp.bfloat16) for leading, total, summed in final_state
    ]
    return jnp.concatenate(outputs, axis=0)


def attend_ranked(query_rows, query_ranks, keys, values, gate_rows):
    heads, rows, width = query_rows.shape
    block = math.gcd(rows, 512)
    scale = 1.0 / math.sqrt(width)
    key_ranks = jnp.arange(keys.shape[1], dtype=jnp.int32)

    def one_block(index):
        scores = (
            jnp.einsum("erd,ekd->erk", query_rows, keys, preferred_element_type=jnp.float32) * scale
        )
        visible = key_ranks[None, None, :] <= query_ranks[:, :, None]
        scores = jnp.where(visible, scores, NEGATIVE)
        leading = jnp.max(scores, axis=2, keepdims=True)
        weights = jnp.where(visible, jnp.exp(scores - leading), 0.0)
        total = jnp.sum(weights, axis=2, keepdims=True)
        mixed = (
            jnp.einsum(
                "erk,ekd->erd",
                weights.astype(jnp.bfloat16),
                values,
                preferred_element_type=jnp.float32,
            )
            / total
        )
        return (mixed * jax.nn.sigmoid(gate_rows.astype(jnp.float32))[:, :, None]).astype(
            jnp.bfloat16
        )

    blocks = lax.map(one_block, jnp.arange(rows // block, dtype=jnp.int32))
    return jnp.moveaxis(blocks, 0, 1).reshape(heads, rows, width)


def sparse_heads(queries, keys, values, gate_logit, selection):
    tok_rows, heads, width = queries.shape
    chosen = selection.shape[1]
    start = lax.axis_index("seq") * tok_rows
    positions = start + jnp.arange(tok_rows, dtype=jnp.int32)
    matches = selection[:, :, None] == positions[None, None, :]
    one_hot = matches.astype(jnp.bfloat16)

    def pick(source):
        return jnp.einsum(
            "ent,ted->end", one_hot, source, preferred_element_type=jnp.float32
        ).astype(jnp.bfloat16)

    gate_rows = jnp.einsum("ent,et->en", one_hot, gate_logit, preferred_element_type=jnp.float32)
    gathered = (
        lax.psum(pick(queries), "seq").astype(jnp.float32),
        lax.psum(pick(keys), "seq").astype(jnp.float32),
        lax.psum(pick(values), "seq").astype(jnp.float32),
        lax.psum(gate_rows.astype(jnp.bfloat16), "seq").astype(jnp.float32),
    )
    picked_q, picked_k, picked_v, picked_gate = [member.astype(jnp.bfloat16) for member in gathered]
    all_ranks = jnp.broadcast_to(jnp.arange(chosen, dtype=jnp.int32)[None, :], (heads, chosen))
    results = attend_ranked(picked_q, all_ranks, picked_k, picked_v, picked_gate)
    return jnp.einsum("ent,end->ted", one_hot, results, preferred_element_type=jnp.float32).astype(
        jnp.bfloat16
    )


def local(q_dense, k_dense, v_dense, q_expert, k_expert, v_expert, gate_logit, selection):
    dense_out = dense_heads(q_dense, k_dense, v_dense, plain_rows)
    expert_out = sparse_heads(q_expert, k_expert, v_expert, gate_logit, selection)
    return (dense_out, expert_out)


def solution(mesh):
    placed = (
        P(("dp", "seq"), "head", None),
        P(("dp", "seq"), "head", None),
        P(("dp", "seq"), "head", None),
        P(("dp", "seq"), "head", None),
        P(("dp", "seq"), "head", None),
        P(("dp", "seq"), "head", None),
        P("head", ("dp", "seq")),
        P("head", "dp"),
    )
    return jax.shard_map(
        local,
        mesh=mesh,
        in_specs=placed,
        out_specs=(P(("dp", "seq"), "head", None), P(("dp", "seq"), "head", None)),
        check_vma=False,
    )
```

profile of v0, /device:TPU:225, one launch (start us, length us, event | category | flops | bytes accessed | tf_op | source)
XLA Modules:
  0.0 332.1 jit_solution(16076033150022781153)
XLA Ops:
  8.2 2.1 fusion.67
  10.3 2.5 fusion.61
  12.7 1.4 fusion.64
  16.6 23.1 %psum.31 = bf16[3,512]{1,0:T(4,128)(2,1)S(1)} all-reduce(bf16[3,512]{1,0:T(4,128)(2,1)S(1)} %bitcast.68), channel_id=1, replica_groups=mesh['dp'=4,'head'=4,'seq'=16] {'seq'}, use_global_device_ids=true, to_apply=%region_18.19 | all-reduce | flops 1536 | bytes 6144 | tf_op jit(solution)/shard_map/psum | solution.py:134
  40.3 87.0 %all-reduce.3.cloned.1.call-done = (bf16[3,512,128]{2,1,0:T(8,128)(2,1)}, bf16[3,512,128]{2,1,0:T(8,128)(2,1)}, bf16[3,512,128]{2,1,0:T(8,128)(2,1)}) async-done(((bf16[3,512,128]{2,1,0:T(8,128)(2,1)}, bf16[3,512,128]{2,1,0:T(8,128)(2,1)}, bf16[3,512,128]{2,1,0:T(8,128)(2,1)}), (bf16[3,512,128]{2,1,0:T(8,128)(2,1)}, bf16[3,512,128]{2,1,0:T(8,128)(2,1)}, ...) | async-done | bytes 1179664 | tf_op jit(solution)/shard_map/psum | solution.py:133
  127.3 2.1 fusion.90
  129.5 1.6 fusion.73
  132.0 39.2 %all-gather.3.cloned.1.call-done = bf16[8192,2,128]{2,0,1:T(8,128)(2,1)} async-done(((bf16[512,2,128]{2,0,1:T(8,128)(2,1)}), bf16[8192,2,128]{2,0,1:T(8,128)(2,1)}) %all-gather.3.cloned.1.call-update) | async-done | bytes 4194320 | tf_op jit(solution)/shard_map/all_gather | solution.py:43
  171.2 42.6 %all-gather.5.cloned.1.call-done = bf16[8192,2,128]{2,0,1:T(8,128)(2,1)} async-done(((bf16[512,2,128]{2,0,1:T(8,128)(2,1)}), bf16[8192,2,128]{2,0,1:T(8,128)(2,1)}) %all-gather.5.cloned.1.call-update) | async-done | bytes 4194320 | tf_op jit(solution)/shard_map/all_gather | solution.py:44
  213.9 109.1 %while.26 = (s32[]{:T(128)}, f32[256,2]{0,1:T(2,128)S(1)}, f32[256,2]{0,1:T(2,128)S(1)}, f32[256,2,128]{2,0,1:T(8,128)S(1)}, f32[256,2]{0,1:T(2,128)S(1)}, /*ind...) while((s32[]{:T(128)}, f32[256,2]{0,1:T(2,128)S(1)}, ...), condition=%wide.region_12.13_spmd.clone, body=%wide.region_2.12_spmd.clone.sunk | while | flops 273682432 | bytes 10830257 | solution.py:77
  215.9 1.1 dynamic-slice_bitcast_fusion.3
  217.0 1.3 conditional.6
  219.4 1.3 conditional.7
  222.7 1.1 dynamic-slice_bitcast_fusion.3
  223.8 1.3 conditional.6
  226.3 1.3 conditional.7
  229.5 1.1 dynamic-slice_bitcast_fusion.3
  230.6 1.3 conditional.6
  233.1 1.3 conditional.7
  236.3 1.1 dynamic-slice_bitcast_fusion.3
  237.4 1.3 conditional.6
  239.9 1.3 conditional.7
  244.2 1.3 conditional.6
  246.7 1.3 conditional.7
  250.0 1.1 dynamic-slice_bitcast_fusion.3
  251.0 1.3 conditional.6
  253.5 1.3 conditional.7
  257.9 1.3 conditional.6
  260.3 1.3 conditional.7
  264.7 1.3 conditional.6
  267.2 1.3 conditional.7
  271.5 1.3 conditional.6
  274.0 1.3 conditional.7
  278.3 1.3 conditional.6
  280.8 1.3 conditional.7
  285.1 1.3 conditional.6
  287.6 1.3 conditional.7
  291.9 1.3 conditional.6
  294.4 1.3 conditional.7
  298.8 1.3 conditional.6
  301.2 1.3 conditional.7
  305.6 1.3 conditional.6
  308.1 1.3 conditional.7
  312.4 1.3 conditional.6
  314.9 1.3 conditional.7
  319.2 1.3 conditional.6
  321.7 1.3 conditional.7
  323.3 1.2 fusion.82
  (341 shorter events, 67.6 us)
Async XLA Ops:
  7.2 1.0 copy-start
  7.2 5.6 %copy-start.6 = (s32[3,512]{1,0:T(4,128)S(1)}, s32[3,512]{1,0:T(4,128)}, u32[]{:S(2)}) copy-start(s32[3,512]{1,0:T(4,128)} %param.21) | copy-start | bytes 18436
  7.2 5.5 %copy-start.4 = (bf16[512,3,128]{2,0,1:T(8,128)(2,1)S(1)}, bf16[512,3,128]{2,0,1:T(8,128)(2,1)}, u32[]{:S(2)}) copy-start(bf16[512,3,128]{2,0,1:T(8,128)(2,1)} %param.18) | copy-start | bytes 1179652
  7.2 120.1 %all-reduce.3.cloned.1.call-start = ((), (), s32[]{:S(2)}) async-start(), calls=%async_computation.2 | async-start | bytes 2359296 | tf_op jit(solution)/shard_map/psum | solution.py:133
  10.3 4.0 %copy-start.1 = (bf16[512,2,128]{2,1,0:T(2,128)(2,1)S(1)}, bf16[512,2,128]{2,1,0:T(2,128)(2,1)}, u32[]{:S(2)}) copy-start(bf16[512,2,128]{2,1,0:T(2,128)(2,1)} %param.15) | copy-start | bytes 786436
  10.3 4.8 %copy-start.2 = (bf16[512,2,128]{2,1,0:T(2,128)(2,1)S(1)}, bf16[512,2,128]{2,1,0:T(2,128)(2,1)}, u32[]{:S(2)}) copy-start(bf16[512,2,128]{2,1,0:T(2,128)(2,1)} %param.16) | copy-start | bytes 786436
  10.3 5.6 %copy-start.3 = (bf16[512,2,128]{2,1,0:T(2,128)(2,1)S(1)}, bf16[512,2,128]{2,1,0:T(2,128)(2,1)}, u32[]{:S(2)}) copy-start(bf16[512,2,128]{2,1,0:T(2,128)(2,1)} %param.14) | copy-start | bytes 786436
  12.7 3.2 copy-start.7
  14.2 157.1 %all-gather.3.cloned.1.call-start = ((), (), s32[]{:S(2)}) async-start(), calls=%async_computation | async-start | bytes 4456448 | tf_op jit(solution)/shard_map/all_gather | solution.py:43
  15.0 198.9 %all-gather.5.cloned.1.call-start = ((), (), s32[]{:S(2)}) async-start(), calls=%async_computation.1 | async-start | bytes 4456448 | tf_op jit(solution)/shard_map/all_gather | solution.py:44
  127.3 2.1 copy-start.5
Sparse Core Ops, SparseCore 0:
  14.3 113.0 all-reduce.2
  129.8 41.4 all-gather.2
  173.1 40.6 all-gather.4
where the time goes:
time: 333 us; the launch traced here: 332 us
  waiting for transfers between devices  169 us (51%)
  loops' own time  42.3 us (13%)
  matrix products  36.9 us (11%)
  other arithmetic  25.7 us (8%)
  blocking collectives  23.1 us (7%)
  local copies, waits for them, and re-layouts  21.1 us (6%)
  between operations  13.9 us (4%)
    psum x1, waiting for transfers between devices, sparse_heads(): lax.psum(pick(values), 'seq').astype(jnp.float32)  87 us
    all_gather x1, waiting for transfers between devices, dense_heads(): value_rows = lax.all_gather(values, 'seq', axis=0, tiled=True)  42.6 us
    another operation x1, loops' own time, dense_heads(): lax.scan(advance, (blank, blank), (key_blocks, value_blocks, key_pos))  40.4 us
    all_gather x1, waiting for transfers between devices, dense_heads(): key_rows = lax.all_gather(keys, 'seq', axis=0, tiled=True)  39.2 us
    psum x1, blocking collectives, sparse_heads(): lax.psum(gate_rows.astype(jnp.bfloat16), 'seq').astype(jnp.float32)  23.1 us
    squeeze x16, local copies, waits for them, and re-layouts, dense_heads(): lax.scan(advance, (blank, blank), (key_blocks, value_blocks, key_pos))  17.2 us
    dot_general x32, matrix products, online_update(): jnp.einsum('qhk,khd->qhd', weights.astype(jnp.bfloat16), values, preferre...  16.5 us
    reduce_min x16, other arithmetic, advance(): seen = jnp.min(block_pos) <= jnp.max(query_pos[group])  10.3 us
  transfers between devices with their start and end apart: 3, of which 3 were waited for; matrix products, arithmetic and copies ran while one was open for 2% of the time, Pallas kernels for 0%

commit v1 on v0

v1 whole, which is shorter than its diff:
```python
import functools
import math

import jax
import jax.numpy as jnp
from jax import lax
from jax.experimental import pallas as pl
from jax.experimental.pallas import tpu as pltpu
from jax.sharding import PartitionSpec as P

NEGATIVE = -1e30


def flash_kernel(count_ref, q_ref, k_ref, v_ref, o_ref, m_ref, l_ref, acc_ref, *, scale, blocks):
    step = pl.program_id(1)
    last = count_ref[0]

    @pl.when(step == 0)
    def _():
        m_ref[...] = jnp.full(m_ref.shape, NEGATIVE, jnp.float32)
        l_ref[...] = jnp.zeros(l_ref.shape, jnp.float32)
        acc_ref[...] = jnp.zeros(acc_ref.shape, jnp.float32)

    @pl.when(step <= last)
    def _():
        q = q_ref[0]
        k = k_ref[0]
        scores = lax.dot_general(
            q, k, (((1,), (1,)), ((), ())), preferred_element_type=jnp.float32
        ) * scale
        rows = lax.broadcasted_iota(jnp.int32, scores.shape, 0)
        cols = lax.broadcasted_iota(jnp.int32, scores.shape, 1)
        visible = (cols <= rows) | (step < last)
        scores = jnp.where(visible, scores, NEGATIVE)
        m_prev = m_ref[:, :1]
        m_new = jnp.maximum(m_prev, jnp.max(scores, axis=1, keepdims=True))
        shrink = jnp.exp(m_prev - m_new)
        weights = jnp.where(visible, jnp.exp(scores - m_new), 0.0)
        l_new = l_ref[:, :1] * shrink + jnp.sum(weights, axis=1, keepdims=True)
        moved = jnp.dot(weights.astype(jnp.bfloat16), v_ref[0], preferred_element_type=jnp.float32)
        acc_ref[...] = acc_ref[...] * shrink + moved
        m_ref[...] = jnp.broadcast_to(m_new, m_ref.shape)
        l_ref[...] = jnp.broadcast_to(l_new, l_ref.shape)

    @pl.when(step == blocks - 1)
    def _():
        o_ref[0] = (acc_ref[...] / l_ref[:, :1]).astype(o_ref.dtype)


def dense_flash(count, queries, keys, values):
    heads, rows, width = queries.shape
    blocks = keys.shape[1] // rows
    scale = 1.0 / math.sqrt(width)

    def kv_map(h, j, c):
        return (h, jnp.minimum(j, c[0]), 0)

    return pl.pallas_call(
        functools.partial(flash_kernel, scale=scale, blocks=blocks),
        out_shape=jax.ShapeDtypeStruct((heads, rows, width), jnp.bfloat16),
        grid_spec=pltpu.PrefetchScalarGridSpec(
            num_scalar_prefetch=1,
            grid=(heads, blocks),
            in_specs=[
                pl.BlockSpec((1, rows, width), lambda h, j, c: (h, 0, 0)),
                pl.BlockSpec((1, rows, width), kv_map),
                pl.BlockSpec((1, rows, width), kv_map),
            ],
            out_specs=pl.BlockSpec((1, rows, width), lambda h, j, c: (h, 0, 0)),
            scratch_shapes=[
                pltpu.VMEM((rows, 128), jnp.float32),
                pltpu.VMEM((rows, 128), jnp.float32),
                pltpu.VMEM((rows, width), jnp.float32),
            ],
        ),
        compiler_params=pltpu.CompilerParams(dimension_semantics=("arbitrary", "arbitrary")),
        cost_estimate=pl.CostEstimate(
            flops=4 * heads * rows * keys.shape[1] * width,
            transcendentals=heads * rows * keys.shape[1],
            bytes_accessed=2 * (2 * keys.size + 2 * queries.size),
        ),
    )(count, queries, keys, values)


def dense_heads(queries, keys, values):
    tok_rows, heads, width = queries.shape
    stacked = jnp.stack([jnp.swapaxes(keys, 0, 1), jnp.swapaxes(values, 0, 1)], axis=0)
    gathered = lax.all_gather(stacked, "seq", axis=2, tiled=True)
    count = lax.axis_index("seq").astype(jnp.int32).reshape(1)
    out = dense_flash(count, jnp.swapaxes(queries, 0, 1), gathered[0], gathered[1])
    return jnp.swapaxes(out, 0, 1)


def attend_ranked(query_rows, keys, values, gate_rows):
    heads, rows, width = query_rows.shape
    scale = 1.0 / math.sqrt(width)
    ranks = jnp.arange(rows, dtype=jnp.int32)
    scores = jnp.einsum("erd,ekd->erk", query_rows, keys, preferred_element_type=jnp.float32) * scale
    visible = ranks[None, None, :] <= ranks[None, :, None]
    scores = jnp.where(visible, scores, NEGATIVE)
    leading = jnp.max(scores, axis=2, keepdims=True)
    weights = jnp.where(visible, jnp.exp(scores - leading), 0.0)
    total = jnp.sum(weights, axis=2, keepdims=True)
    mixed = (
        jnp.einsum("erk,ekd->erd", weights.astype(jnp.bfloat16), values, preferred_element_type=jnp.float32)
        / total
    )
    return (mixed * jax.nn.sigmoid(gate_rows)[:, :, None]).astype(jnp.bfloat16)


def sparse_heads(queries, keys, values, gate_logit, selection):
    tok_rows, heads, width = queries.shape
    start = lax.axis_index("seq") * tok_rows
    positions = start + jnp.arange(tok_rows, dtype=jnp.int32)
    one_hot = (selection[:, :, None] == positions[None, None, :]).astype(jnp.bfloat16)

    def pick(source):
        return jnp.einsum("ent,ted->end", one_hot, source, preferred_element_type=jnp.float32).astype(
            jnp.bfloat16
        )

    local_kv = jnp.stack([pick(keys), pick(values)], axis=0)
    picked_kv = lax.psum(local_kv, "seq")
    picked_q = pick(queries)
    gate_rows = jnp.einsum("ent,et->en", one_hot, gate_logit, preferred_element_type=jnp.float32)
    results = attend_ranked(picked_q, picked_kv[0], picked_kv[1], gate_rows)
    return jnp.einsum("ent,end->ted", one_hot, results, preferred_element_type=jnp.float32).astype(
        jnp.bfloat16
    )


def local(q_dense, k_dense, v_dense, q_expert, k_expert, v_expert, gate_logit, selection):
    dense_out = dense_heads(q_dense, k_dense, v_dense)
    expert_out = sparse_heads(q_expert, k_expert, v_expert, gate_logit, selection)
    return (dense_out, expert_out)


def solution(mesh):
    rows = P(("dp", "seq"), "head", None)
    placed = (rows, rows, rows, rows, rows, rows, P("head", ("dp", "seq")), P("head", "dp"))
    return jax.shard_map(
        local,
        mesh=mesh,
        in_specs=placed,
        out_specs=(rows, rows),
        check_vma=False,
    )
```

time: 333 us -> 253 us (0.76)
  Pallas kernels: 0 us -> 58.3 us
  loops' own time: 42.3 us -> 0 us
  matrix products: 36.9 us -> 8.58 us
  blocking collectives: 23.1 us -> 0 us
  other arithmetic: 25.7 us -> 8.07 us
  waiting for transfers between devices: 169 us -> 154 us
  local copies, waits for them, and re-layouts: 21.1 us -> 9.38 us
    pallas_call x0 -> x1, Pallas kernels: none -> 58.3 us  [dense_flash(): pl.pallas_call(functools.partial(flash_kernel, scale=scale, blocks=blocks...]
    another operation x33 -> x0, loops' own time: 42.3 us -> none  [the longest x1 40.4 us: dense_heads(): lax.scan(advance, (blank, blank), (key_blocks, value_blocks, key_pos))]
    all_gather x2 -> x1, waiting for transfers between devices: 81.8 us -> 46.4 us  [dense_heads(): gathered = lax.all_gather(stacked, 'seq', axis=2, tiled=True)]
    dot_general x64 -> x1, matrix products: 26.5 us -> 2.05 us  [attend_ranked(): jnp.einsum('erd,ekd->erk', query_rows, keys, preferred_element_type=jnp.f...]
    psum x1 -> x0, blocking collectives: 23.1 us -> none  [sparse_heads(): lax.psum(gate_rows.astype(jnp.bfloat16), 'seq').astype(jnp.float32)]
    psum x1, waiting for transfers between devices: 87 us -> 107 us  [sparse_heads(): picked_kv = lax.psum(local_kv, 'seq')]
    squeeze x16 -> x1, local copies, waits for them, and re-layouts: 17.2 us -> 5.69 us  [dense_heads(): gathered[1]]
    reduce_min x16 -> x0, other arithmetic: 10.3 us -> none  [advance(): seen = jnp.min(block_pos) <= jnp.max(query_pos[group])]
  transfers between devices with their start and end apart: 3 -> 2, of which waited for: 3 -> 2; matrix products, arithmetic and copies ran while one was open for 2% -> 6% of each run, Pallas kernels for 0% -> 0%
where the time goes in v1:
time: 253 us; the launch traced here: 252 us
  waiting for transfers between devices  154 us (61%)
  Pallas kernels  58.3 us (23%)
  between operations  14.2 us (6%)
  local copies, waits for them, and re-layouts  9.38 us (4%)
  matrix products  8.58 us (3%)
  other arithmetic  8.07 us (3%)
    psum x1, waiting for transfers between devices, sparse_heads(): picked_kv = lax.psum(local_kv, 'seq')  107 us
    pallas_call x1, Pallas kernels, dense_flash(): pl.pallas_call(functools.partial(flash_kernel, scale=scale, blocks=blocks...  58.3 us
    all_gather x1, waiting for transfers between devices, dense_heads(): gathered = lax.all_gather(stacked, 'seq', axis=2, tiled=True)  46.4 us
    squeeze x1, local copies, waits for them, and re-layouts, dense_heads(): gathered[1]  5.69 us
  transfers between devices with their start and end apart: 2, of which 2 were waited for; matrix products, arithmetic and copies ran while one was open for 6% of the time, Pallas kernels for 0%

profile of v1, /device:TPU:225, one launch (start us, length us, event | category | flops | bytes accessed | tf_op | source)
XLA Modules:
  0.0 252.4 jit_solution(9630605575272115055)
XLA Ops:
  7.2 0.0 copy-start
  7.2 0.0 all-reduce.2.cloned.1.call-start
  7.2 0.0 copy-start.2
  7.3 0.0 copy-start.3
  7.3 1.7 fusion.51
  9.0 0.0 copy-start.1
  9.0 1.7 fusion.54
  10.7 0.0 copy-start.4
  10.7 0.0 copy-start.5
  10.7 1.0 pad_maximum_fusion
  11.7 0.0 all-reduce.2.cloned.1.call-update
  11.8 0.0 all-gather.2.cloned.1.call-start
  11.8 0.0 copy-done.2
  11.8 0.0 copy-done.3
  11.8 0.1 copy_bitcast_fusion
  11.9 0.9 pad_maximum_fusion.1
  12.8 0.0 all-gather.2.cloned.1.call-update
  12.8 0.0 copy-done.1
  12.8 0.7 copy.23
  13.5 0.8 iota_compare_fusion
  14.3 0.0 copy-done.4
  14.3 0.0 copy-done.5
  14.3 0.6 fusion.3
  15.0 0.6 fusion.66
  15.6 107.4 %all-reduce.2.cloned.1.call-done = bf16[2,3,512,128]{3,2,1,0:T(8,128)(2,1)} async-done(((bf16[2,3,512,128]{3,2,1,0:T(8,128)(2,1)}), bf16[2,3,512,128]{3,2,1,0:T(8,128)(2,1)}) %all-reduce.2.cloned.1.call-update) | async-done | bytes 786448 | tf_op jit(solution)/shard_map/psum | solution.py:123
  123.0 0.0 copy-done
  123.0 2.0 fusion.58
  125.1 4.8 %fusion.70 = (f32[3,512]{1,0:T(4,128)}, bf16[3,512,512]{1,2,0:T(8,128)(2,1)}) fusion(f32[3,512,512]{1,2,0:T(8,128)S(1)} %fusion.58, pred[512,512]{0,1:T(8,128)(4,1)} %iota_compare_fusion), kind=kOutput, calls=%fused_computation.60 | output fusion | flops 6291967 | bytes 4986880 | tf_op jit(solution)/shard_map/sub | solution.py:102
  129.9 2.5 fusion.48
  132.3 0.9 copy.14
  133.3 46.4 %all-gather.2.cloned.1.call-done = bf16[2,2,8192,128]{3,2,1,0:T(8,128)(2,1)} async-done(((bf16[2,2,512,128]{3,2,1,0:T(8,128)(2,1)}), bf16[2,2,8192,128]{3,2,1,0:T(8,128)(2,1)}) %all-gather.2.cloned.1.call-update) | async-done | bytes 8388624 | tf_op jit(solution)/shard_map/all_gather | solution.py:88
  179.7 5.7 %slice_bitcast_fusion = (bf16[2,8192,128]{2,1,0:T(8,128)(2,1)}, bf16[2,8192,128]{2,1,0:T(8,128)(2,1)}) fusion(bf16[2,2,8192,128]{3,2,1,0:T(8,128)(2,1)} %all-gather.2.cloned.1.call-done), kind=kLoop, calls=%fused_computation.11 | loop fusion | bytes 16777216 | tf_op jit(solution)/shard_map/squeeze | solution.py:90
  185.3 58.3 %shard_map.95 = bf16[2,512,128]{2,1,0:T(8,128)(2,1)} custom-call(s32[1]{0:T(128)} %bitcast.count_ref, bf16[2,512,128]{2,1,0:T(8,128)(2,1)} %bitcast.43, bf16[2,8192,128]{2,1,0:T(8,128)(2,1)} %get-tuple-element.5.k_ref, bf16[2,8192,128]{2,1,0:T(8,128)(2,1)} %get-tuple-element.4.v_ref), custom_call_target="tpu_custom_call" | custom-call | flops 4294967296 | bytes 8912896 | tf_op jit(solution)/shard_map/pallas_call | solution.py:58
  243.7 1.9 copy.13
  (1 shorter events, 0.0 us)
Async XLA Ops:
  7.2 115.8 %copy-start = (bf16[512,3,128]{2,0,1:T(8,128)(2,1)S(1)}, bf16[512,3,128]{2,0,1:T(8,128)(2,1)}, u32[]{:S(2)}) copy-start(bf16[512,3,128]{2,0,1:T(8,128)(2,1)} %param.11) | copy-start | bytes 1179652
  7.2 115.8 %all-reduce.2.cloned.1.call-start = ((), (), s32[]{:S(2)}) async-start(), calls=%async_computation.1 | async-start | bytes 1572864 | tf_op jit(solution)/shard_map/psum | solution.py:123
  7.2 4.6 %copy-start.2 = (bf16[512,2,128]{2,1,0:T(2,128)(2,1)S(1)}, bf16[512,2,128]{2,1,0:T(2,128)(2,1)}, u32[]{:S(2)}) copy-start(bf16[512,2,128]{2,1,0:T(2,128)(2,1)} %param.10) | copy-start | bytes 786436
  7.3 4.6 %copy-start.3 = (bf16[512,2,128]{2,1,0:T(2,128)(2,1)S(1)}, bf16[512,2,128]{2,1,0:T(2,128)(2,1)}, u32[]{:S(2)}) copy-start(bf16[512,2,128]{2,1,0:T(2,128)(2,1)} %param.9) | copy-start | bytes 786436
  9.0 3.8 %copy-start.1 = (bf16[512,2,128]{2,1,0:T(2,128)(2,1)S(1)}, bf16[512,2,128]{2,1,0:T(2,128)(2,1)}, u32[]{:S(2)}) copy-start(bf16[512,2,128]{2,1,0:T(2,128)(2,1)} %param.8) | copy-start | bytes 786436
  10.7 3.6 %copy-start.4 = (s32[3,512]{1,0:T(4,128)S(1)}, s32[3,512]{1,0:T(4,128)}, u32[]{:S(2)}) copy-start(s32[3,512]{1,0:T(4,128)} %param.15) | copy-start | bytes 18436
  10.7 3.6 %copy-start.5 = (bf16[3,512]{1,0:T(4,128)(2,1)S(1)}, bf16[3,512]{1,0:T(4,128)(2,1)}, u32[]{:S(2)}) copy-start(bf16[3,512]{1,0:T(4,128)(2,1)} %param.14) | copy-start | bytes 9220
  11.8 167.9 %all-gather.2.cloned.1.call-start = ((), (), s32[]{:S(2)}) async-start(), calls=%async_computation | async-start | bytes 8912896 | tf_op jit(solution)/shard_map/all_gather | solution.py:88
Sparse Core Ops, SparseCore 0:
  11.9 111.0 all-reduce.1
  125.0 54.6 all-gather.1

commit v2 on v1

--- a/solution.py
+++ b/solution.py
@@ -47,13 +47,14 @@
         o_ref[0] = (acc_ref[...] / l_ref[:, :1]).astype(o_ref.dtype)
 
 
-def dense_flash(count, queries, keys, values):
+def dense_flash(count, queries, stacked):
     heads, rows, width = queries.shape
-    blocks = keys.shape[1] // rows
+    length = stacked.shape[2]
+    blocks = length // rows
     scale = 1.0 / math.sqrt(width)
 
-    def kv_map(h, j, c):
-        return (h, jnp.minimum(j, c[0]), 0)
+    def kv_map(which):
+        return lambda h, j, c: (which, h, jnp.minimum(j, c[0]), 0)
 
     return pl.pallas_call(
         functools.partial(flash_kernel, scale=scale, blocks=blocks),
@@ -63,8 +64,8 @@
             grid=(heads, blocks),
             in_specs=[
                 pl.BlockSpec((1, rows, width), lambda h, j, c: (h, 0, 0)),
-                pl.BlockSpec((1, rows, width), kv_map),
-                pl.BlockSpec((1, rows, width), kv_map),
+                pl.BlockSpec((None, 1, rows, width), kv_map(0)),
+                pl.BlockSpec((None, 1, rows, width), kv_map(1)),
             ],
             out_specs=pl.BlockSpec((1, rows, width), lambda h, j, c: (h, 0, 0)),
             scratch_shapes=[
@@ -75,11 +76,11 @@
         ),
         compiler_params=pltpu.CompilerParams(dimension_semantics=("arbitrary", "arbitrary")),
         cost_estimate=pl.CostEstimate(
-            flops=4 * heads * rows * keys.shape[1] * width,
-            transcendentals=heads * rows * keys.shape[1],
-            bytes_accessed=2 * (2 * keys.size + 2 * queries.size),
+            flops=4 * heads * rows * length * width,
+            transcendentals=heads * rows * length,
+            bytes_accessed=2 * (stacked.size + 2 * queries.size),
         ),
-    )(count, queries, keys, values)
+    )(count, queries, stacked, stacked)
 
 
 def dense_heads(queries, keys, values):
@@ -87,7 +88,7 @@
     stacked = jnp.stack([jnp.swapaxes(keys, 0, 1), jnp.swapaxes(values, 0, 1)], axis=0)
     gathered = lax.all_gather(stacked, "seq", axis=2, tiled=True)
     count = lax.axis_index("seq").astype(jnp.int32).reshape(1)
-    out = dense_flash(count, jnp.swapaxes(queries, 0, 1), gathered[0], gathered[1])
+    out = dense_flash(count, jnp.swapaxes(queries, 0, 1), gathered)
     return jnp.swapaxes(out, 0, 1)
 
 
@@ -119,8 +120,13 @@
             jnp.bfloat16
         )
 
+    count = lax.axis_size("seq")
     local_kv = jnp.stack([pick(keys), pick(values)], axis=0)
-    picked_kv = lax.psum(local_kv, "seq")
+    kinds, heads_, chosen, width_ = local_kv.shape
+    pieces = local_kv.reshape(kinds, heads_, count, chosen // count, width_)
+    arrived = lax.all_to_all(pieces, "seq", 2, 2, tiled=True)
+    own = jnp.sum(arrived.astype(jnp.float32), axis=2).astype(jnp.bfloat16)
+    picked_kv = lax.all_gather(own, "seq", axis=2, tiled=True)
     picked_q = pick(queries)
     gate_rows = jnp.einsum("ent,et->en", one_hot, gate_logit, preferred_element_type=jnp.float32)
     results = attend_ranked(picked_q, picked_kv[0], picked_kv[1], gate_rows)

time: 253 us -> 151 us (0.60)
  the two profiles are of different devices: /device:TPU:225 before, /device:TPU:231 now
where the time goes in v2:
time: 151 us
  Pallas kernels  58.4 us (39%)
  waiting for transfers between devices  27.4 us (18%)
  blocking collectives  24.3 us (16%)
  between operations  14.1 us (9%)
  matrix products  7.47 us (5%)
  other arithmetic  7.27 us (5%)
  starting transfers between devices  6.21 us (4%)
  local copies, waits for them, and re-layouts  5.82 us (4%)
    pallas_call x1, Pallas kernels, dense_flash(): pl.pallas_call(functools.partial(flash_kernel, scale=scale, blocks=blocks...  58.4 us
    all_gather x1, blocking collectives, sparse_heads(): picked_kv = lax.all_gather(own, 'seq', axis=2, tiled=True)  24.3 us
    all_to_all x1, waiting for transfers between devices, sparse_heads(): arrived = lax.all_to_all(pieces, 'seq', 2, 2, tiled=True)  22.9 us
    all_to_all x1, starting transfers between devices, sparse_heads(): arrived = lax.all_to_all(pieces, 'seq', 2, 2, tiled=True)  6.18 us
    sub x1, other arithmetic, attend_ranked(): weights = jnp.where(visible, jnp.exp(scores - leading), 0.0)  4.83 us
    all_gather x1, waiting for transfers between devices, dense_heads(): gathered = lax.all_gather(stacked, 'seq', axis=2, tiled=True)  4.45 us
    unnamed x13, local copies, waits for them, and re-layouts  3.61 us
  transfers between devices with their start and end apart: 2, of which 2 were waited for; matrix products, arithmetic and copies ran while one was open for 11% of the time, Pallas kernels for 0%

profile of v2, /device:TPU:231, one launch (start us, length us, event | category | flops | bytes accessed | tf_op | source)
XLA Modules:
  0.0 151.0 jit_solution(8491914449792114672)
XLA Ops:
  7.2 0.0 copy-start
  7.2 0.0 copy-start.2
  7.2 0.0 copy-start.3
  7.2 0.0 all-gather.2.cloned.1.call-start
  7.2 1.2 copy_bitcast_fusion
  8.4 0.8 pad_maximum_fusion.1
  9.3 0.0 all-gather.2.cloned.1.call-update
  9.3 1.7 %fusion.42 = bf16[3,512,128]{2,1,0:T(8,128)(2,1)S(1)} fusion(bf16[512,3,128]{2,0,1:T(8,128)(2,1)} %param.13, s32[512]{0:T(512)S(1)} %iota_add_fusion, s32[3,512]{1,0:T(4,128)} %param.15), kind=kOutput, calls=%fused_computation.34 | convolution fusion | flops 202309632 | bytes 794624 | tf_op jit(solution)/shard_map/ent,ted->end/dot_general | solution.py:119
  11.0 0.0 copy-done.2
  11.0 0.0 copy-done.3
  11.0 0.0 copy-start.1
  11.0 0.6 fusion.39
  11.7 0.0 copy-start.4
  11.7 0.1 pad_maximum_fusion
  11.8 1.0 copy.24
  12.8 6.2 %all-to-all-start = ((bf16[2,3,16,32,128]{4,3,1,0,2:T(8,128)(2,1)}), bf16[2,3,16,32,128]{4,3,1,0,2:T(8,128)(2,1)S(1)}, u32[]{:S(2)}, u32[]{:S(2)}) async-start(bf16[2,3,16,32,128]{4,3,1,0,2:T(8,128)(2,1)} %copy.24), calls=%async_computation | async-start | bytes 1572864 | tf_op jit(solution)/shard_map/all_to_all | solution.py:127
  19.0 0.0 copy-done.1
  19.0 0.7 copy.31
  19.7 0.8 iota_compare_fusion
  20.5 0.0 copy-done.4
  20.5 0.7 fusion.3
  21.1 0.6 fusion.60
  21.8 22.9 %all-to-all-done = bf16[2,3,16,32,128]{4,3,1,0,2:T(8,128)(2,1)S(1)} async-done(((bf16[2,3,16,32,128]{4,3,1,0,2:T(8,128)(2,1)}), bf16[2,3,16,32,128]{4,3,1,0,2:T(8,128)(2,1)S(1)}, u32[]{:S(2)}, u32[]{:S(2)}) %all-to-all-start) | async-done | bytes 786464 | tf_op jit(solution)/shard_map/all_to_all | solution.py:127
  44.6 0.1 reduce_sum.21
  44.8 24.3 %all_gather.7 = bf16[2,3,512,128]{3,2,1,0:T(8,128)(2,1)} all-gather(bf16[2,3,32,128]{3,2,1,0:T(8,128)(2,1)S(1)} %reduce_sum.21), channel_id=1, replica_groups=mesh['dp'=4,'head'=4,'seq'=16] {'seq'}, dimensions={2}, use_global_device_ids=true | all-gather | bytes 835584 | tf_op jit(solution)/shard_map/all_gather | solution.py:129
  69.1 0.0 copy-done
  69.1 2.0 %fusion.52 = f32[3,512,512]{1,2,0:T(8,128)S(1)} fusion(bf16[512,3,128]{2,0,1:T(8,128)(2,1)S(1)} %copy-done, s32[512]{0:T(512)S(1)} %iota_add_fusion, s32[3,512]{1,0:T(4,128)S(1)} %copy-done.2, bf16[2,3,512,128]{3,2,1,0:T(8,128)(2,1)} %all_gather.7), kind=kOutput, calls=%fused_computation.37 | convolution fusion | flops 403636224 | bytes 3940352 | tf_op jit(solution)/shard_map/erd,ekd->erk/dot_general | solution.py:99
  71.2 4.8 %fusion.64 = (f32[3,512]{1,0:T(4,128)}, bf16[3,512,512]{1,2,0:T(8,128)(2,1)}) fusion(f32[3,512,512]{1,2,0:T(8,128)S(1)} %fusion.52, pred[512,512]{0,1:T(8,128)(4,1)} %iota_compare_fusion), kind=kOutput, calls=%fused_computation.56 | output fusion | flops 6291967 | bytes 4986880 | tf_op jit(solution)/shard_map/sub | solution.py:103
  76.0 2.5 %fusion.48 = bf16[512,3,128]{0,2,1:T(8,128)(2,1)S(1)} fusion(s32[512]{0:T(512)S(1)} %iota_add_fusion, s32[3,512]{1,0:T(4,128)S(1)} %copy-done.2, bf16[3,512,512]{1,2,0:T(8,128)(2,1)} %get-tuple-element.7, bf16[2,3,512,128]{3,2,1,0:T(8,128)(2,1)} %all_gather.7, f32[3,512]{1,0:T(4,128)} %fusion.60, f32[3,512]{1,0:T(4,128)} %get-tuple-element.6), kind=kOutput, calls=%fused_computation.36 | convolution fusion | flops 404226048 | bytes 2383872 | tf_op jit(solution)/shard_map/ent,end->ted/dot_general | solution.py:133
  78.5 0.9 copy.21
  79.4 4.5 %all-gather.2.cloned.1.call-done.k_ref.v_ref = bf16[2,2,8192,128]{3,2,1,0:T(8,128)(2,1)} async-done(((bf16[2,2,512,128]{3,2,1,0:T(8,128)(2,1)}), bf16[2,2,8192,128]{3,2,1,0:T(8,128)(2,1)}) %all-gather.2.cloned.1.call-update) | async-done | bytes 8388624 | tf_op jit(solution)/shard_map/all_gather | solution.py:89
  83.8 58.4 %shard_map.95 = bf16[2,512,128]{2,1,0:T(8,128)(2,1)} custom-call(s32[1]{0:T(128)} %bitcast.count_ref, bf16[2,512,128]{2,1,0:T(8,128)(2,1)} %bitcast.37, bf16[2,2,8192,128]{3,2,1,0:T(8,128)(2,1)} %all-gather.2.cloned.1.call-done.k_ref.v_ref, bf16[2,2,8192,128]{3,2,1,0:T(8,128)(2,1)} %all-gather.2.cloned.1.call-done.k_ref.v_ref), custom_call_target="tpu_custom_call" | custom-call | flops 4294967296 | bytes 8912896 | tf_op jit(solution)/shard_map/pallas_call | solution.py:59
  142.2 1.9 %copy.20 = bf16[512,2,128]{2,1,0:T(2,128)(2,1)} copy(bf16[512,2,128]{2,0,1:T(8,128)(2,1)} %bitcast.38) | data formatting | bytes 524288
  (1 shorter events, 0.0 us)
Async XLA Ops:
  7.2 61.9 %copy-start = (bf16[512,3,128]{2,0,1:T(8,128)(2,1)S(1)}, bf16[512,3,128]{2,0,1:T(8,128)(2,1)}, u32[]{:S(2)}) copy-start(bf16[512,3,128]{2,0,1:T(8,128)(2,1)} %param.11) | copy-start | bytes 1179652
  7.2 3.8 %copy-start.2 = (s32[3,512]{1,0:T(4,128)S(1)}, s32[3,512]{1,0:T(4,128)}, u32[]{:S(2)}) copy-start(s32[3,512]{1,0:T(4,128)} %param.15) | copy-start | bytes 18436
  7.2 3.8 %copy-start.3 = (bf16[512,3,128]{2,0,1:T(8,128)(2,1)S(1)}, bf16[512,3,128]{2,0,1:T(8,128)(2,1)}, u32[]{:S(2)}) copy-start(bf16[512,3,128]{2,0,1:T(8,128)(2,1)} %param.12) | copy-start | bytes 1179652
  7.2 76.6 %all-gather.2.cloned.1.call-start = ((), (), s32[]{:S(2)}) async-start(), calls=%async_computation.1 | async-start | bytes 8912896 | tf_op jit(solution)/shard_map/all_gather | solution.py:89
  11.0 8.0 %copy-start.1 = (bf16[512,2,128]{2,1,0:T(2,128)(2,1)S(1)}, bf16[512,2,128]{2,1,0:T(2,128)(2,1)}, u32[]{:S(2)}) copy-start(bf16[512,2,128]{2,1,0:T(2,128)(2,1)} %param.8) | copy-start | bytes 786436
  11.7 8.8 %copy-start.4 = (bf16[3,512]{1,0:T(4,128)(2,1)S(1)}, bf16[3,512]{1,0:T(4,128)(2,1)}, u32[]{:S(2)}) copy-start(bf16[3,512]{1,0:T(4,128)(2,1)} %param.14) | copy-start | bytes 9220
  12.8 31.9 %all-to-all-start = ((bf16[2,3,16,32,128]{4,3,1,0,2:T(8,128)(2,1)}), bf16[2,3,16,32,128]{4,3,1,0,2:T(8,128)(2,1)S(1)}, u32[]{:S(2)}, u32[]{:S(2)}) async-start(bf16[2,3,16,32,128]{4,3,1,0,2:T(8,128)(2,1)} %copy.24), calls=%async_computation | async-start | bytes 1572864 | tf_op jit(solution)/shard_map/all_to_all | solution.py:127
Sparse Core Ops, SparseCore 0:
  9.9 73.8 all-gather.1

commit v3 on v2

--- a/solution.py
+++ b/solution.py
@@ -11,9 +11,11 @@
 NEGATIVE = -1e30
 
 
-def flash_kernel(count_ref, q_ref, k_ref, v_ref, o_ref, m_ref, l_ref, acc_ref, *, scale, blocks):
-    step = pl.program_id(1)
-    last = count_ref[0]
+def flash_kernel(info_ref, q_ref, k_ref, v_ref, o_ref, m_ref, l_ref, acc_ref, *, scale, blocks):
+    part = pl.program_id(1)
+    step = pl.program_id(2)
+    last = info_ref[part]
+    offset = info_ref[2 + part]
 
     @pl.when(step == 0)
     def _():
@@ -21,75 +23,93 @@
         l_ref[...] = jnp.zeros(l_ref.shape, jnp.float32)
         acc_ref[...] = jnp.zeros(acc_ref.shape, jnp.float32)
 
-    @pl.when(step <= last)
-    def _():
-        q = q_ref[0]
-        k = k_ref[0]
+    def update(masked):
         scores = lax.dot_general(
-            q, k, (((1,), (1,)), ((), ())), preferred_element_type=jnp.float32
+            q_ref[0, 0], k_ref[0], (((1,), (1,)), ((), ())), preferred_element_type=jnp.float32
         ) * scale
-        rows = lax.broadcasted_iota(jnp.int32, scores.shape, 0)
-        cols = lax.broadcasted_iota(jnp.int32, scores.shape, 1)
-        visible = (cols <= rows) | (step < last)
-        scores = jnp.where(visible, scores, NEGATIVE)
+        if masked:
+            rows = lax.broadcasted_iota(jnp.int32, scores.shape, 0) + offset
+            cols = lax.broadcasted_iota(jnp.int32, scores.shape, 1)
+            scores = jnp.where(cols <= rows, scores, NEGATIVE)
         m_prev = m_ref[:, :1]
         m_new = jnp.maximum(m_prev, jnp.max(scores, axis=1, keepdims=True))
         shrink = jnp.exp(m_prev - m_new)
-        weights = jnp.where(visible, jnp.exp(scores - m_new), 0.0)
+        weights = jnp.exp(scores - m_new)
         l_new = l_ref[:, :1] * shrink + jnp.sum(weights, axis=1, keepdims=True)
         moved = jnp.dot(weights.astype(jnp.bfloat16), v_ref[0], preferred_element_type=jnp.float32)
         acc_ref[...] = acc_ref[...] * shrink + moved
         m_ref[...] = jnp.broadcast_to(m_new, m_ref.shape)
         l_ref[...] = jnp.broadcast_to(l_new, l_ref.shape)
 
+    @pl.when(step < last)
+    def _():
+        update(False)
+
+    @pl.when(step == last)
+    def _():
+        update(True)
+
     @pl.when(step == blocks - 1)
     def _():
-        o_ref[0] = (acc_ref[...] / l_ref[:, :1]).astype(o_ref.dtype)
+        o_ref[0, 0] = (acc_ref[...] / l_ref[:, :1]).astype(o_ref.dtype)
 
 
-def dense_flash(count, queries, stacked):
-    heads, rows, width = queries.shape
+def dense_flash(info, queries, stacked):
+    parts, heads, rows, width = queries.shape
     length = stacked.shape[2]
-    blocks = length // rows
+    block = 512
+    blocks = length // block
     scale = 1.0 / math.sqrt(width)
 
     def kv_map(which):
-        return lambda h, j, c: (which, h, jnp.minimum(j, c[0]), 0)
+        return lambda h, p, j, c: (which, h, jnp.minimum(j, c[p]), 0)
 
     return pl.pallas_call(
         functools.partial(flash_kernel, scale=scale, blocks=blocks),
-        out_shape=jax.ShapeDtypeStruct((heads, rows, width), jnp.bfloat16),
+        out_shape=jax.ShapeDtypeStruct((parts, heads, rows, width), jnp.bfloat16),
         grid_spec=pltpu.PrefetchScalarGridSpec(
             num_scalar_prefetch=1,
-            grid=(heads, blocks),
+            grid=(heads, parts, blocks),
             in_specs=[
-                pl.BlockSpec((1, rows, width), lambda h, j, c: (h, 0, 0)),
-                pl.BlockSpec((None, 1, rows, width), kv_map(0)),
-                pl.BlockSpec((None, 1, rows, width), kv_map(1)),
+                pl.BlockSpec((1, 1, rows, width), lambda h, p, j, c: (p, h, 0, 0)),
+                pl.BlockSpec((None, 1, block, width), kv_map(0)),
+                pl.BlockSpec((None, 1, block, width), kv_map(1)),
             ],
-            out_specs=pl.BlockSpec((1, rows, width), lambda h, j, c: (h, 0, 0)),
+            out_specs=pl.BlockSpec((1, 1, rows, width), lambda h, p, j, c: (p, h, 0, 0)),
             scratch_shapes=[
                 pltpu.VMEM((rows, 128), jnp.float32),
                 pltpu.VMEM((rows, 128), jnp.float32),
                 pltpu.VMEM((rows, width), jnp.float32),
             ],
         ),
-        compiler_params=pltpu.CompilerParams(dimension_semantics=("arbitrary", "arbitrary")),
+        compiler_params=pltpu.CompilerParams(
+            dimension_semantics=("arbitrary", "arbitrary", "arbitrary")
+        ),
         cost_estimate=pl.CostEstimate(
-            flops=4 * heads * rows * length * width,
-            transcendentals=heads * rows * length,
-            bytes_accessed=2 * (stacked.size + 2 * queries.size),
+            flops=2 * heads * rows * length * width,
+            transcendentals=heads * rows * length // 2,
+            bytes_accessed=stacked.size + 4 * queries.size,
         ),
-    )(count, queries, stacked, stacked)
+    )(info, queries, stacked, stacked)
 
 
 def dense_heads(queries, keys, values):
     tok_rows, heads, width = queries.shape
+    count = lax.axis_size("seq")
+    me = lax.axis_index("seq").astype(jnp.int32)
+    partner = count - 1 - me
+    half = tok_rows // 2
+    swap = [(i, count - 1 - i) for i in range(count)]
     stacked = jnp.stack([jnp.swapaxes(keys, 0, 1), jnp.swapaxes(values, 0, 1)], axis=0)
     gathered = lax.all_gather(stacked, "seq", axis=2, tiled=True)
-    count = lax.axis_index("seq").astype(jnp.int32).reshape(1)
-    out = dense_flash(count, jnp.swapaxes(queries, 0, 1), gathered)
-    return jnp.swapaxes(out, 0, 1)
+    rows_first = jnp.swapaxes(queries, 0, 1)
+    lent = lax.ppermute(rows_first[:, half:], "seq", swap)
+    both = jnp.stack([rows_first[:, :half], lent], axis=0)
+    info = jnp.stack([me, partner, jnp.int32(0), jnp.int32(half)])
+    out = dense_flash(info, both, gathered)
+    returned = lax.ppermute(out[1], "seq", swap)
+    mine = jnp.concatenate([out[0], returned], axis=1)
+    return jnp.swapaxes(mine, 0, 1)
 
 
 def attend_ranked(query_rows, keys, values, gate_rows):

time: 151 us -> 148 us (0.980)
  the two profiles are of different devices: /device:TPU:231 before, /device:TPU:1 now
where the time goes in v3:
time: 148 us; the launch traced here: 147 us
  waiting for transfers between devices  40.3 us (27%)
  Pallas kernels  34.9 us (24%)
  blocking collectives  23.4 us (16%)
  between operations  14.2 us (10%)
  starting transfers between devices  13.2 us (9%)
  other arithmetic  8.61 us (6%)
  matrix products  7.35 us (5%)
  local copies, waits for them, and re-layouts  5.2 us (4%)
    pallas_call x1, Pallas kernels, dense_flash(): pl.pallas_call(functools.partial(flash_kernel, scale=scale, blocks=blocks...  34.9 us
    ppermute x1, waiting for transfers between devices, dense_heads(): lent = lax.ppermute(rows_first[:, half:], 'seq', swap)  29.4 us
    all_gather x1, blocking collectives, sparse_heads(): picked_kv = lax.all_gather(own, 'seq', axis=2, tiled=True)  23.4 us
    all_to_all x1, starting transfers between devices, sparse_heads(): arrived = lax.all_to_all(pieces, 'seq', 2, 2, tiled=True)  9.98 us
    all_gather x1, waiting for transfers between devices, dense_heads(): gathered = lax.all_gather(stacked, 'seq', axis=2, tiled=True)  5.78 us
    ppermute x1, waiting for transfers between devices, dense_heads(): returned = lax.ppermute(out[1], 'seq', swap)  5.14 us
    sub x1, other arithmetic, attend_ranked(): weights = jnp.where(visible, jnp.exp(scores - leading), 0.0)  4.73 us
  transfers between devices with their start and end apart: 4, of which 3 were waited for; matrix products, arithmetic and copies ran while one was open for 12% of the time, Pallas kernels for 0%

profile of v3, /device:TPU:1, one launch (start us, length us, event | category | flops | bytes accessed | tf_op | source)
XLA Modules:
  0.0 147.2 jit_solution(15592931140789400276)
XLA Ops:
  7.2 0.0 copy-start
  7.2 0.0 copy-start.3
  7.2 0.0 copy-start.5
  7.2 0.0 all-gather.2.cloned.1.call-start
  7.2 1.2 copy_bitcast_fusion
  8.4 0.9 pad_maximum_fusion.1
  9.3 0.0 all-gather.2.cloned.1.call-update
  9.3 1.7 %fusion.42 = bf16[3,512,128]{2,1,0:T(8,128)(2,1)S(1)} fusion(bf16[512,3,128]{2,0,1:T(8,128)(2,1)} %param.13, s32[512]{0:T(512)S(1)} %iota_add_fusion, s32[3,512]{1,0:T(4,128)} %param.15), kind=kOutput, calls=%fused_computation.34 | convolution fusion | flops 202309632 | bytes 794624 | tf_op jit(solution)/shard_map/ent,ted->end/dot_general | solution.py:139
  11.0 0.0 copy-done.3
  11.0 0.0 copy-done.5
  11.0 0.0 copy-start.2
  11.0 0.6 fusion.39
  11.7 0.0 copy-start.6
  11.7 0.1 pad_maximum_fusion
  11.8 1.0 copy.24
  12.8 10.0 %all-to-all-start = ((bf16[2,3,16,32,128]{4,3,1,0,2:T(8,128)(2,1)}), bf16[2,3,16,32,128]{4,3,1,0,2:T(8,128)(2,1)S(1)}, u32[]{:S(2)}, u32[]{:S(2)}) async-start(bf16[2,3,16,32,128]{4,3,1,0,2:T(8,128)(2,1)} %copy.24), calls=%async_computation | async-start | bytes 1572864 | tf_op jit(solution)/shard_map/all_to_all | solution.py:147
  22.8 0.0 copy-done.2
  22.9 2.9 %collective-permute-start = (bf16[2,256,128]{2,1,0:T(8,128)(2,1)S(1)}, bf16[2,256,128]{2,1,0:T(8,128)(2,1)S(1)}, u32[]{:S(2)}, u32[]{:S(2)}) collective-permute-start(bf16[2,256,128]{2,1,0:T(8,128)(2,1)S(1)} %get-tuple-element.9), channel_id=1, source_target_pairs={{0,15},{1,14},{2,13},{3,12},{4,11},{5,10},{6,9},{7,8},{8,7},{9,6},... | collective-permute-start | bytes 393224 | tf_op jit(solution)/shard_map/ppermute | solution.py:106
  25.8 0.0 copy-done.6
  25.8 0.6 fusion.3
  26.5 0.6 fusion.60
  27.1 0.7 pad_add_fusion.info_ref
  27.8 0.8 iota_compare_fusion
  28.5 29.4 %collective-permute-done = bf16[2,256,128]{2,1,0:T(8,128)(2,1)S(1)} collective-permute-done((bf16[2,256,128]{2,1,0:T(8,128)(2,1)S(1)}, bf16[2,256,128]{2,1,0:T(8,128)(2,1)S(1)}, u32[]{:S(2)}, u32[]{:S(2)}) %collective-permute-start) | collective-permute-done | bytes 131104 | tf_op jit(solution)/shard_map/ppermute | solution.py:106
  57.9 0.7 pad_maximum_fusion.2.q_ref
  58.6 0.0 all-to-all-done
  58.6 0.1 reduce_sum.21
  58.8 23.4 %all_gather.7 = bf16[2,3,512,128]{3,2,1,0:T(8,128)(2,1)} all-gather(bf16[2,3,32,128]{3,2,1,0:T(8,128)(2,1)S(1)} %reduce_sum.21), channel_id=1, replica_groups=mesh['dp'=4,'head'=4,'seq'=16] {'seq'}, dimensions={2}, use_global_device_ids=true | all-gather | bytes 835584 | tf_op jit(solution)/shard_map/all_gather | solution.py:149
  82.1 0.0 copy-done
  82.1 2.1 %fusion.52 = f32[3,512,512]{1,2,0:T(8,128)S(1)} fusion(bf16[512,3,128]{2,0,1:T(8,128)(2,1)S(1)} %copy-done, s32[512]{0:T(512)S(1)} %iota_add_fusion, s32[3,512]{1,0:T(4,128)S(1)} %copy-done.3, bf16[2,3,512,128]{3,2,1,0:T(8,128)(2,1)} %all_gather.7), kind=kOutput, calls=%fused_computation.37 | convolution fusion | flops 403636224 | bytes 3940352 | tf_op jit(solution)/shard_map/erd,ekd->erk/dot_general | solution.py:119
  84.2 4.7 %fusion.64 = (f32[3,512]{1,0:T(4,128)}, bf16[3,512,512]{1,2,0:T(8,128)(2,1)}) fusion(f32[3,512,512]{1,2,0:T(8,128)S(1)} %fusion.52, pred[512,512]{0,1:T(8,128)(4,1)} %iota_compare_fusion), kind=kOutput, calls=%fused_computation.62 | output fusion | flops 6291967 | bytes 4986880 | tf_op jit(solution)/shard_map/sub | solution.py:123
  88.9 0.0 copy-start.1
  88.9 0.0 copy-start.4
  88.9 0.0 copy-start.7
  88.9 5.8 %all-gather.2.cloned.1.call-done.k_ref.v_ref = bf16[2,2,8192,128]{3,2,1,0:T(8,128)(2,1)} async-done(((bf16[2,2,512,128]{3,2,1,0:T(8,128)(2,1)}), bf16[2,2,8192,128]{3,2,1,0:T(8,128)(2,1)}) %all-gather.2.cloned.1.call-update) | async-done | bytes 8388624 | tf_op jit(solution)/shard_map/all_gather | solution.py:104
  94.7 34.9 %shard_map.95 = bf16[2,2,256,128]{3,2,1,0:T(8,128)(2,1)} custom-call(s32[4]{0:T(128)} %pad_add_fusion.info_ref, bf16[2,2,256,128]{3,2,1,0:T(8,128)(2,1)} %pad_maximum_fusion.2.q_ref, bf16[2,2,8192,128]{3,2,1,0:T(8,128)(2,1)} %all-gather.2.cloned.1.call-done.k_ref.v_ref, bf16[2,2,8192,128]{3,2,1,0:T(8,128)(2,1)} %all-gather.2.cloned.1.call-done.k_ref.v_ref), custom_call_target="tpu_custom_call" | custom-call | flops 1073741824 | bytes 4718592 | tf_op jit(solution)/shard_map/pallas_call | solution.py:67
  129.7 1.0 slice_bitcast_fusion.6
  130.6 0.3 collective-permute-start.1
  130.9 0.0 copy-done.1
  130.9 0.0 copy-done.4
  130.9 0.0 copy-done.7
  130.9 2.3 %fusion.48 = bf16[512,3,128]{0,2,1:T(8,128)(2,1)S(1)} fusion(s32[512]{0:T(512)S(1)} %iota_add_fusion, s32[3,512]{1,0:T(4,128)S(1)} %copy-done.3, bf16[3,512,512]{1,2,0:T(8,128)(2,1)} %get-tuple-element.11, bf16[2,3,512,128]{3,2,1,0:T(8,128)(2,1)S(1)} %copy-done.1, f32[3,512]{1,0:T(4,128)S(1)} %copy-done.4, f32[3,512]{1,0:T(4,128)S(1)} %copy-done.7), kind=kOutput, calls=%fused_computation.36 | convolution fusion | flops 404226048 | bytes 2385920 | tf_op jit(solution)/shard_map/ent,end->ted/dot_general | solution.py:153
  133.3 0.9 copy.21
  134.2 5.1 %collective-permute-done.1 = bf16[2,256,128]{2,1,0:T(8,128)(2,1)S(1)} collective-permute-done((bf16[2,256,128]{2,1,0:T(8,128)(2,1)S(1)}, bf16[2,256,128]{2,1,0:T(8,128)(2,1)S(1)}, u32[]{:S(2)}, u32[]{:S(2)}) %collective-permute-start.1) | collective-permute-done | bytes 131104 | tf_op jit(solution)/shard_map/ppermute | solution.py:110
  139.4 1.0 copy.20
  (4 shorter events, 0.1 us)
Async XLA Ops:
  7.2 75.0 %copy-start = (bf16[512,3,128]{2,0,1:T(8,128)(2,1)S(1)}, bf16[512,3,128]{2,0,1:T(8,128)(2,1)}, u32[]{:S(2)}) copy-start(bf16[512,3,128]{2,0,1:T(8,128)(2,1)} %param.11) | copy-start | bytes 1179652
  7.2 3.8 %copy-start.3 = (s32[3,512]{1,0:T(4,128)S(1)}, s32[3,512]{1,0:T(4,128)}, u32[]{:S(2)}) copy-start(s32[3,512]{1,0:T(4,128)} %param.15) | copy-start | bytes 18436
  7.2 3.8 %copy-start.5 = (bf16[512,3,128]{2,0,1:T(8,128)(2,1)S(1)}, bf16[512,3,128]{2,0,1:T(8,128)(2,1)}, u32[]{:S(2)}) copy-start(bf16[512,3,128]{2,0,1:T(8,128)(2,1)} %param.12) | copy-start | bytes 1179652
  7.2 87.5 %all-gather.2.cloned.1.call-start = ((), (), s32[]{:S(2)}) async-start(), calls=%async_computation.1 | async-start | bytes 8912896 | tf_op jit(solution)/shard_map/all_gather | solution.py:104
  11.0 11.8 %copy-start.2 = (bf16[512,2,128]{2,1,0:T(2,128)(2,1)S(1)}, bf16[512,2,128]{2,1,0:T(2,128)(2,1)}, u32[]{:S(2)}) copy-start(bf16[512,2,128]{2,1,0:T(2,128)(2,1)} %param.8) | copy-start | bytes 786436
  11.7 14.1 %copy-start.6 = (bf16[3,512]{1,0:T(4,128)(2,1)S(1)}, bf16[3,512]{1,0:T(4,128)(2,1)}, u32[]{:S(2)}) copy-start(bf16[3,512]{1,0:T(4,128)(2,1)} %param.14) | copy-start | bytes 9220
  12.8 45.8 %all-to-all-start = ((bf16[2,3,16,32,128]{4,3,1,0,2:T(8,128)(2,1)}), bf16[2,3,16,32,128]{4,3,1,0,2:T(8,128)(2,1)S(1)}, u32[]{:S(2)}, u32[]{:S(2)}) async-start(bf16[2,3,16,32,128]{4,3,1,0,2:T(8,128)(2,1)} %copy.24), calls=%async_computation | async-start | bytes 1572864 | tf_op jit(solution)/shard_map/all_to_all | solution.py:147
  22.9 35.0 %collective-permute-start = (bf16[2,256,128]{2,1,0:T(8,128)(2,1)S(1)}, bf16[2,256,128]{2,1,0:T(8,128)(2,1)S(1)}, u32[]{:S(2)}, u32[]{:S(2)}) collective-permute-start(bf16[2,256,128]{2,1,0:T(8,128)(2,1)S(1)} %get-tuple-element.9), channel_id=1, source_target_pairs={{0,15},{1,14},{2,13},{3,12},{4,11},{5,10},{6,9},{7,8},{8,7},{9,6},... | collective-permute-start | bytes 393224 | tf_op jit(solution)/shard_map/ppermute | solution.py:106
  88.9 42.0 %copy-start.1 = (bf16[2,3,512,128]{3,2,1,0:T(8,128)(2,1)S(1)}, bf16[2,3,512,128]{3,2,1,0:T(8,128)(2,1)}, u32[]{:S(2)}) copy-start(bf16[2,3,512,128]{3,2,1,0:T(8,128)(2,1)} %all_gather.7) | copy-start | bytes 2359300
  88.9 42.0 %copy-start.4 = (f32[3,512]{1,0:T(4,128)S(1)}, f32[3,512]{1,0:T(4,128)}, u32[]{:S(2)}) copy-start(f32[3,512]{1,0:T(4,128)} %fusion.60) | copy-start | bytes 18436
  88.9 42.0 %copy-start.7 = (f32[3,512]{1,0:T(4,128)S(1)}, f32[3,512]{1,0:T(4,128)}, u32[]{:S(2)}) copy-start(f32[3,512]{1,0:T(4,128)} %get-tuple-element.10) | copy-start | bytes 18436
  130.6 8.7 %collective-permute-start.1 = (bf16[2,256,128]{2,1,0:T(8,128)(2,1)S(1)}, bf16[2,256,128]{2,1,0:T(8,128)(2,1)S(1)}, u32[]{:S(2)}, u32[]{:S(2)}) collective-permute-start(bf16[2,256,128]{2,1,0:T(8,128)(2,1)S(1)} %get-tuple-element.7), channel_id=1, source_target_pairs={{0,15},{1,14},{2,13},{3,12},{4,11},{5,10},{6,9},{7,8},{8,7},{9,6},... | collective-permute-start | bytes 393224 | tf_op jit(solution)/shard_map/ppermute | solution.py:110
Sparse Core Ops, SparseCore 0:
  9.9 84.7 all-gather.1

commit v4 on v3

--- a/solution.py
+++ b/solution.py
@@ -11,19 +11,17 @@
 NEGATIVE = -1e30
 
 
-def flash_kernel(info_ref, q_ref, k_ref, v_ref, o_ref, m_ref, l_ref, acc_ref, *, scale, blocks):
+def flash_kernel(info_ref, q_ref, m_in, l_in, acc_in, *refs, scale, count):
+    kv_refs = refs[: 2 * count]
+    m_out, l_out, acc_out = refs[2 * count :]
     part = pl.program_id(1)
-    step = pl.program_id(2)
     last = info_ref[part]
     offset = info_ref[2 + part]
+    m_out[0, 0] = m_in[0, 0]
+    l_out[0, 0] = l_in[0, 0]
+    acc_out[0, 0] = acc_in[0, 0]
 
-    @pl.when(step == 0)
-    def _():
-        m_ref[...] = jnp.full(m_ref.shape, NEGATIVE, jnp.float32)
-        l_ref[...] = jnp.zeros(l_ref.shape, jnp.float32)
-        acc_ref[...] = jnp.zeros(acc_ref.shape, jnp.float32)
-
-    def update(masked):
+    def update(k_ref, v_ref, masked):
         scores = lax.dot_general(
             q_ref[0, 0], k_ref[0], (((1,), (1,)), ((), ())), preferred_element_type=jnp.float32
         ) * scale
@@ -31,82 +29,100 @@
             rows = lax.broadcasted_iota(jnp.int32, scores.shape, 0) + offset
             cols = lax.broadcasted_iota(jnp.int32, scores.shape, 1)
             scores = jnp.where(cols <= rows, scores, NEGATIVE)
-        m_prev = m_ref[:, :1]
+        m_prev = m_out[0, 0][:, :1]
         m_new = jnp.maximum(m_prev, jnp.max(scores, axis=1, keepdims=True))
         shrink = jnp.exp(m_prev - m_new)
         weights = jnp.exp(scores - m_new)
-        l_new = l_ref[:, :1] * shrink + jnp.sum(weights, axis=1, keepdims=True)
+        l_new = l_out[0, 0][:, :1] * shrink + jnp.sum(weights, axis=1, keepdims=True)
         moved = jnp.dot(weights.astype(jnp.bfloat16), v_ref[0], preferred_element_type=jnp.float32)
-        acc_ref[...] = acc_ref[...] * shrink + moved
-        m_ref[...] = jnp.broadcast_to(m_new, m_ref.shape)
-        l_ref[...] = jnp.broadcast_to(l_new, l_ref.shape)
+        acc_out[0, 0] = acc_out[0, 0] * shrink + moved
+        m_out[0, 0] = jnp.broadcast_to(m_new, m_out.shape[2:])
+        l_out[0, 0] = jnp.broadcast_to(l_new, l_out.shape[2:])
 
-    @pl.when(step < last)
-    def _():
-        update(False)
+    for b in range(count):
+        index = info_ref[4 + b]
 
-    @pl.when(step == last)
-    def _():
-        update(True)
+        @pl.when(index < last)
+        def _():
+            update(kv_refs[2 * b], kv_refs[2 * b + 1], False)
 
-    @pl.when(step == blocks - 1)
-    def _():
-        o_ref[0, 0] = (acc_ref[...] / l_ref[:, :1]).astype(o_ref.dtype)
+        @pl.when(index == last)
+        def _():
+            update(kv_refs[2 * b], kv_refs[2 * b + 1], True)
 
 
-def dense_flash(info, queries, stacked):
+def flash_round(info, queries, state, blocks):
     parts, heads, rows, width = queries.shape
-    length = stacked.shape[2]
-    block = 512
-    blocks = length // block
+    block = blocks[0].shape[2]
+    count = len(blocks)
     scale = 1.0 / math.sqrt(width)
-
-    def kv_map(which):
-        return lambda h, p, j, c: (which, h, jnp.minimum(j, c[p]), 0)
-
+    row_spec = pl.BlockSpec((1, 1, rows, width), lambda h, p, c: (p, h, 0, 0))
+    kv_specs = []
+    kv_args = []
+    for item in blocks:
+        for which in range(2):
+            kv_specs.append(pl.BlockSpec((None, 1, block, width), lambda h, p, c, w=which: (w, h, 0, 0)))
+            kv_args.append(item)
     return pl.pallas_call(
-        functools.partial(flash_kernel, scale=scale, blocks=blocks),
-        out_shape=jax.ShapeDtypeStruct((parts, heads, rows, width), jnp.bfloat16),
+        functools.partial(flash_kernel, scale=scale, count=count),
+        out_shape=[jax.ShapeDtypeStruct(x.shape, x.dtype) for x in state],
         grid_spec=pltpu.PrefetchScalarGridSpec(
             num_scalar_prefetch=1,
-            grid=(heads, parts, blocks),
-            in_specs=[
-                pl.BlockSpec((1, 1, rows, width), lambda h, p, j, c: (p, h, 0, 0)),
-                pl.BlockSpec((None, 1, block, width), kv_map(0)),
-                pl.BlockSpec((None, 1, block, width), kv_map(1)),
-            ],
-            out_specs=pl.BlockSpec((1, 1, rows, width), lambda h, p, j, c: (p, h, 0, 0)),
-            scratch_shapes=[
-                pltpu.VMEM((rows, 128), jnp.float32),
-                pltpu.VMEM((rows, 128), jnp.float32),
-                pltpu.VMEM((rows, width), jnp.float32),
-            ],
+            grid=(heads, parts),
+            in_specs=[row_spec, row_spec, row_spec, row_spec] + kv_specs,
+            out_specs=[row_spec, row_spec, row_spec],
         ),
-        compiler_params=pltpu.CompilerParams(
-            dimension_semantics=("arbitrary", "arbitrary", "arbitrary")
+        input_output_aliases={2: 0, 3: 1, 4: 2},
+        compiler_params=pltpu.CompilerParams(dimension_semantics=("arbitrary", "arbitrary")),
+        cost_estimate=pl.CostEstimate(
+            flops=4 * heads * parts * rows * block * width * count // 2,
+            transcendentals=heads * parts * rows * block * count // 2,
+            bytes_accessed=2 * count * blocks[0].size + 12 * queries.size,
         ),
-        cost_estimate=pl.CostEstimate(
-            flops=2 * heads * rows * length * width,
-            transcendentals=heads * rows * length // 2,
-            bytes_accessed=stacked.size + 4 * queries.size,
-        ),
-    )(info, queries, stacked, stacked)
+    )(info, queries, *state, *kv_args)
 
 
 def dense_heads(queries, keys, values):
     tok_rows, heads, width = queries.shape
     count = lax.axis_size("seq")
+    chips = count // 2
     me = lax.axis_index("seq").astype(jnp.int32)
     partner = count - 1 - me
     half = tok_rows // 2
     swap = [(i, count - 1 - i) for i in range(count)]
-    stacked = jnp.stack([jnp.swapaxes(keys, 0, 1), jnp.swapaxes(values, 0, 1)], axis=0)
-    gathered = lax.all_gather(stacked, "seq", axis=2, tiled=True)
+    up = [(i, (i + 2) % count) for i in range(count)]
+    down = [(i, (i - 2) % count) for i in range(count)]
+    sib = [(i, i ^ 1) for i in range(count)]
+    own = jnp.stack([jnp.swapaxes(keys, 0, 1), jnp.swapaxes(values, 0, 1)], axis=0)
     rows_first = jnp.swapaxes(queries, 0, 1)
     lent = lax.ppermute(rows_first[:, half:], "seq", swap)
     both = jnp.stack([rows_first[:, :half], lent], axis=0)
-    info = jnp.stack([me, partner, jnp.int32(0), jnp.int32(half)])
-    out = dense_flash(info, both, gathered)
+    head = jnp.stack([me, partner, jnp.int32(0), jnp.int32(half)])
+    state = (
+        jnp.full((2, heads, half, 128), NEGATIVE, jnp.float32),
+        jnp.zeros((2, heads, half, 128), jnp.float32),
+        jnp.zeros((2, heads, half, width), jnp.float32),
+    )
+
+    def run(state, items):
+        info = jnp.concatenate([head, jnp.stack([index for index, _ in items])])
+        return flash_round(info, both, state, [item for _, item in items])
+
+    pending = [(me ^ 1, lax.ppermute(own, "seq", sib))]
+    state = run(state, [(me, own)])
+    cur_up, cur_dn = own, own
+    for t in range(1, chips // 2 + 1):
+        cur_up = lax.ppermute(cur_up, "seq", up)
+        arrived = [((me - 2 * t) % count, cur_up)]
+        if 2 * t < chips:
+            cur_dn = lax.ppermute(cur_dn, "seq", down)
+            arrived.append(((me + 2 * t) % count, cur_dn))
+        sent = [(index ^ 1, lax.ppermute(item, "seq", sib)) for index, item in arrived]
+        state = run(state, pending + arrived)
+        pending = sent
+    state = run(state, pending)
+    m_final, l_final, acc_final = state
+    out = (acc_final / l_final[..., :1]).astype(jnp.bfloat16)
     returned = lax.ppermute(out[1], "seq", swap)
     mine = jnp.concatenate([out[0], returned], axis=1)
     return jnp.swapaxes(mine, 0, 1)

time: 148 us -> 163 us (1.10)
  starting transfers between devices: 13.2 us -> 27.7 us
  between operations: 14.2 us -> 0.9 us
  Pallas kernels: 34.9 us -> 44.7 us
  local copies, waits for them, and re-layouts: 5.2 us -> 12.5 us
  waiting for transfers between devices: 40.3 us -> 37.5 us
  blocking collectives: 23.4 us -> 20.7 us
    ppermute x0 -> x15, waiting for transfers between devices: none -> 27.2 us  [the longest x3 22 us: dense_heads(): cur_dn = lax.ppermute(cur_dn, 'seq', down)]
    ppermute x1, waiting for transfers between devices: 29.4 us -> 5.85 us  [dense_heads(): lent = lax.ppermute(rows_first[:, half:], 'seq', swap)]
    ppermute x0 -> x15, starting transfers between devices: none -> 13.7 us  [the longest x3 7.54 us: dense_heads(): cur_dn = lax.ppermute(cur_dn, 'seq', down)]
    pallas_call x1 -> x6, Pallas kernels: 34.9 us -> 44.7 us  [flash_round(): pl.pallas_call(functools.partial(flash_kernel, scale=scale, count=count),...]
    all_gather x1 -> x0, waiting for transfers between devices: 5.78 us -> none  [dense_heads(): gathered = lax.all_gather(stacked, 'seq', axis=2, tiled=True)]
    concatenate x0 -> x6, local copies, waits for them, and re-layouts: none -> 3.8 us  [run(): info = jnp.concatenate([head, jnp.stack([index for index, _ in items])])]
    all_gather x1, blocking collectives: 23.4 us -> 20.7 us  [sparse_heads(): picked_kv = lax.all_gather(own, 'seq', axis=2, tiled=True)]
    another operation x0 -> x2, local copies, waits for them, and re-layouts: none -> 1.73 us
  transfers between devices with their start and end apart: 4 -> 18, of which waited for: 3 -> 6; matrix products, arithmetic and copies ran while one was open for 12% -> 15% of each run, Pallas kernels for 0% -> 24%
where the time goes in v4:
time: 163 us; the launch traced here: 162 us
  Pallas kernels  44.7 us (27%)
  waiting for transfers between devices  37.5 us (23%)
  starting transfers between devices  27.7 us (17%)
  blocking collectives  20.7 us (13%)
  local copies, waits for them, and re-layouts  12.5 us (8%)
  other arithmetic  9.05 us (6%)
  matrix products  8.63 us (5%)
    pallas_call x6, Pallas kernels, flash_round(): pl.pallas_call(functools.partial(flash_kernel, scale=scale, count=count),...  44.7 us
    ppermute x3, waiting for transfers between devices, dense_heads(): cur_dn = lax.ppermute(cur_dn, 'seq', down)  22 us
    all_gather x1, blocking collectives, sparse_heads(): picked_kv = lax.all_gather(own, 'seq', axis=2, tiled=True)  20.7 us
    all_to_all x1, starting transfers between devices, sparse_heads(): arrived = lax.all_to_all(pieces, 'seq', 2, 2, tiled=True)  8.53 us
    ppermute x3, starting transfers between devices, dense_heads(): cur_dn = lax.ppermute(cur_dn, 'seq', down)  7.54 us
    ppermute x1, waiting for transfers between devices, dense_heads(): lent = lax.ppermute(rows_first[:, half:], 'seq', swap)  5.85 us
    ppermute x4, waiting for transfers between devices, dense_heads(): cur_up = lax.ppermute(cur_up, 'seq', up)  5.16 us
    sub x1, other arithmetic, attend_ranked(): weights = jnp.where(visible, jnp.exp(scores - leading), 0.0)  4.73 us
  transfers between devices with their start and end apart: 18, of which 6 were waited for; matrix products, arithmetic and copies ran while one was open for 15% of the time, Pallas kernels for 24%

profile of v4, /device:TPU:1, one launch (start us, length us, event | category | flops | bytes accessed | tf_op | source)
XLA Modules:
  0.0 161.7 jit_solution(8341434806163685217)
XLA Ops:
  0.7 1.2 copy_bitcast_fusion
  1.9 2.5 %collective-permute-start.2 = (bf16[2,2,512,128]{3,2,1,0:T(8,128)(2,1)S(1)}, bf16[2,2,512,128]{3,2,1,0:T(8,128)(2,1)S(1)}, u32[]{:S(2)}, u32[]{:S(2)}) collective-permute-start(bf16[2,2,512,128]{3,2,1,0:T(8,128)(2,1)S(1)} %pad_maximum_fusion.1.refs_0_.refs_1_), channel_id=1, source_target_pairs={{0,2},{1,3},{2,4},{3,5},{4,6},{5,7},{6,8},{7,9},{8,10},{9,11},{10,... | collective-permute-start | bytes 1572872 | tf_op jit(solution)/shard_map/ppermute | solution.py:115
  4.5 1.7 %fusion.39 = bf16[3,512,128]{2,1,0:T(8,128)(2,1)S(1)} fusion(bf16[512,3,128]{2,0,1:T(8,128)(2,1)} %param.12, s32[512]{0:T(512)S(1)} %iota_add_fusion, s32[3,512]{1,0:T(4,128)} %param.15), kind=kOutput, calls=%fused_computation.33 | convolution fusion | flops 202309632 | bytes 794624 | tf_op jit(solution)/shard_map/ent,ted->end/dot_general | solution.py:155
  6.1 0.6 fusion.42
  6.9 1.0 copy.51
  7.9 8.5 %all-to-all-start = ((bf16[2,3,16,32,128]{4,3,1,0,2:T(8,128)(2,1)}), bf16[2,3,16,32,128]{4,3,1,0,2:T(8,128)(2,1)S(1)}, u32[]{:S(2)}, u32[]{:S(2)}) async-start(bf16[2,3,16,32,128]{4,3,1,0,2:T(8,128)(2,1)} %copy.51), calls=%async_computation | async-start | bytes 1572864 | tf_op jit(solution)/shard_map/all_to_all | solution.py:163
  16.4 2.6 %collective-permute-start.3 = (bf16[2,2,512,128]{3,2,1,0:T(8,128)(2,1)S(1)}, bf16[2,2,512,128]{3,2,1,0:T(8,128)(2,1)S(1)}, u32[]{:S(2)}, u32[]{:S(2)}) collective-permute-start(bf16[2,2,512,128]{3,2,1,0:T(8,128)(2,1)S(1)} %pad_maximum_fusion.1.refs_0_.refs_1_), channel_id=1, source_target_pairs={{0,14},{1,15},{2,0},{3,1},{4,2},{5,3},{6,4},{7,5},{8,6},{9,7},{10,... | collective-permute-start | bytes 1572872 | tf_op jit(solution)/shard_map/ppermute | solution.py:118
  19.0 1.0 collective-permute-done.2.refs_2_.refs_3_
  20.1 4.5 %collective-permute-start = (bf16[2,256,128]{2,1,0:T(8,128)(2,1)S(1)}, bf16[2,256,128]{2,1,0:T(8,128)(2,1)S(1)}, u32[]{:S(2)}, u32[]{:S(2)}) collective-permute-start(bf16[2,256,128]{2,1,0:T(8,128)(2,1)S(1)} %get-tuple-element.45), channel_id=1, source_target_pairs={{0,15},{1,14},{2,13},{3,12},{4,11},{5,10},{6,9},{7,8},{8,7},{9,6},... | collective-permute-start | bytes 393224 | tf_op jit(solution)/shard_map/ppermute | solution.py:98
  24.6 0.5 collective-permute-start.4
  25.1 21.9 %collective-permute-done.3.refs_4_.refs_5_ = bf16[2,2,512,128]{3,2,1,0:T(8,128)(2,1)S(1)} collective-permute-done((bf16[2,2,512,128]{3,2,1,0:T(8,128)(2,1)S(1)}, bf16[2,2,512,128]{3,2,1,0:T(8,128)(2,1)S(1)}, u32[]{:S(2)}, u32[]{:S(2)}) %collective-permute-start.3) | collective-permute-done | bytes 524320 | tf_op jit(solution)/shard_map/ppermute | solution.py:118
  47.0 1.4 collective-permute-start.7
  48.4 5.8 %collective-permute-done = bf16[2,256,128]{2,1,0:T(8,128)(2,1)S(1)} collective-permute-done((bf16[2,256,128]{2,1,0:T(8,128)(2,1)S(1)}, bf16[2,256,128]{2,1,0:T(8,128)(2,1)S(1)}, u32[]{:S(2)}, u32[]{:S(2)}) %collective-permute-start) | collective-permute-done | bytes 131104 | tf_op jit(solution)/shard_map/ppermute | solution.py:98
  54.3 0.3 collective-permute-start.5
  54.6 1.3 fusion.3
  55.9 0.6 concatenate.33.info_ref
  56.5 0.7 concatenate.28.info_ref
  57.2 0.7 concatenate.32.info_ref
  57.9 0.7 concatenate.29.info_ref
  58.5 0.6 concatenate.31.info_ref
  59.1 0.6 concatenate.30.info_ref
  59.7 0.8 iota_compare_fusion
  60.5 1.3 fusion.60
  61.9 3.5 %collective-permute-start.11 = (bf16[2,2,512,128]{3,2,1,0:T(8,128)(2,1)}, bf16[2,2,512,128]{3,2,1,0:T(8,128)(2,1)}, u32[]{:S(2)}, u32[]{:S(2)}) collective-permute-start(bf16[2,2,512,128]{3,2,1,0:T(8,128)(2,1)} %collective-permute-done.7.refs_6_.refs_7_), channel_id=1, source_target_pairs={{0,14},{1,15},{2,0},{3,1},{4,2},{5,3},{6,4},{7,5},{8,6},{9,7},{10,... | collective-permute-start | bytes 1572872 | tf_op jit(solution)/shard_map/ppermute | solution.py:118
  65.4 4.1 %collective-permute-done.10.refs_4_.refs_5_ = bf16[2,2,512,128]{3,2,1,0:T(8,128)(2,1)} collective-permute-done((bf16[2,2,512,128]{3,2,1,0:T(8,128)(2,1)}, bf16[2,2,512,128]{3,2,1,0:T(8,128)(2,1)}, u32[]{:S(2)}, u32[]{:S(2)}) %collective-permute-start.10) | collective-permute-done | bytes 524320 | tf_op jit(solution)/shard_map/ppermute | solution.py:115
  69.5 0.7 pad_maximum_fusion.2.q_ref
  70.3 0.9 broadcast_3_l_in_acc_in.2.l_in
  71.1 0.9 broadcast_3_l_in_acc_in.2.clone.acc_in
  72.0 0.9 broadcast_in_dim.30.m_in
  72.9 5.9 %shard_map.95 = (f32[2,2,256,128]{3,2,1,0:T(8,128)}, f32[2,2,256,128]{3,2,1,0:T(8,128)}, f32[2,2,256,128]{3,2,1,0:T(8,128)}) custom-call(s32[5]{0:T(128)} %concatenate.33.info_ref, bf16[2,2,256,128]{3,2,1,0:T(8,128)(2,1)} %pad_maximum_fusion.2.q_ref, ...), custom_call_target="tpu_custom_call", output_to_operand_aliasing={{0}: (2, {}), {1}: (3, {}), {2}: (4, {})} | custom-call | flops 134217728 | bytes 2097152 | tf_op jit(solution)/shard_map/pallas_call | solution.py:66
  78.8 7.2 %shard_map.96 = (f32[2,2,256,128]{3,2,1,0:T(8,128)}, f32[2,2,256,128]{3,2,1,0:T(8,128)}, f32[2,2,256,128]{3,2,1,0:T(8,128)}) custom-call(s32[7]{0:T(128)} %concatenate.32.info_ref, bf16[2,2,256,128]{3,2,1,0:T(8,128)(2,1)} %pad_maximum_fusion.2.q_ref, ...), custom_call_target="tpu_custom_call", output_to_operand_aliasing={{0}: (2, {}), {1}: (3, {}), {2}: (4, {})} | custom-call | flops 402653184 | bytes 3145728 | tf_op jit(solution)/shard_map/pallas_call | solution.py:66
  85.9 1.8 %collective-permute-start.8 = (bf16[2,2,512,128]{3,2,1,0:T(8,128)(2,1)}, bf16[2,2,512,128]{3,2,1,0:T(8,128)(2,1)}, u32[]{:S(2)}, u32[]{:S(2)}) collective-permute-start(bf16[2,2,512,128]{3,2,1,0:T(8,128)(2,1)} %collective-permute-done.6.refs_4_.refs_5_), channel_id=1, source_target_pairs={{0,1},{1,0},{2,3},{3,2},{4,5},{5,4},{6,7},{7,6},{8,9},{9,8},{10,11... | collective-permute-start | bytes 1572872 | tf_op jit(solution)/shard_map/ppermute | solution.py:120
  87.9 0.7 copy-done.4
  88.5 9.2 %shard_map.97 = (f32[2,2,256,128]{3,2,1,0:T(8,128)}, f32[2,2,256,128]{3,2,1,0:T(8,128)}, f32[2,2,256,128]{3,2,1,0:T(8,128)}) custom-call(s32[8]{0:T(128)} %concatenate.31.info_ref, bf16[2,2,256,128]{3,2,1,0:T(8,128)(2,1)} %pad_maximum_fusion.2.q_ref, ...), custom_call_target="tpu_custom_call", output_to_operand_aliasing={{0}: (2, {}), {1}: (3, {}), {2}: (4, {})} | custom-call | flops 536870912 | bytes 3670016 | tf_op jit(solution)/shard_map/pallas_call | solution.py:66
  97.8 20.7 %all_gather.3 = bf16[2,3,512,128]{3,2,1,0:T(8,128)(2,1)} all-gather(bf16[2,3,32,128]{3,2,1,0:T(8,128)(2,1)S(1)} %reduce_sum.21), channel_id=1, replica_groups=mesh['dp'=4,'head'=4,'seq'=16] {'seq'}, dimensions={2}, use_global_device_ids=true | all-gather | bytes 835584 | tf_op jit(solution)/shard_map/all_gather | solution.py:165
  118.7 0.4 collective-permute-start.13
  119.4 2.0 %fusion.52 = f32[3,512,512]{1,2,0:T(8,128)S(1)} fusion(bf16[512,3,128]{2,0,1:T(8,128)(2,1)S(1)} %copy-done, s32[512]{0:T(512)S(1)} %iota_add_fusion, s32[3,512]{1,0:T(4,128)S(1)} %copy-done.7, bf16[2,3,512,128]{3,2,1,0:T(8,128)(2,1)} %all_gather.3), kind=kOutput, calls=%fused_computation.37 | convolution fusion | flops 403636224 | bytes 3940352 | tf_op jit(solution)/shard_map/erd,ekd->erk/dot_general | solution.py:135
  121.4 4.7 %fusion.64 = (f32[3,512]{1,0:T(4,128)}, bf16[3,512,512]{1,2,0:T(8,128)(2,1)}) fusion(f32[3,512,512]{1,2,0:T(8,128)S(1)} %fusion.52, pred[512,512]{0,1:T(8,128)(4,1)} %iota_compare_fusion), kind=kOutput, calls=%fused_computation.63 | output fusion | flops 6291967 | bytes 4986880 | tf_op jit(solution)/shard_map/sub | solution.py:139
  126.2 9.2 %shard_map.98 = (f32[2,2,256,128]{3,2,1,0:T(8,128)}, f32[2,2,256,128]{3,2,1,0:T(8,128)}, f32[2,2,256,128]{3,2,1,0:T(8,128)}) custom-call(s32[8]{0:T(128)} %concatenate.30.info_ref, bf16[2,2,256,128]{3,2,1,0:T(8,128)(2,1)} %pad_maximum_fusion.2.q_ref, ...), custom_call_target="tpu_custom_call", output_to_operand_aliasing={{0}: (2, {}), {1}: (3, {}), {2}: (4, {})} | custom-call | flops 536870912 | bytes 3670016 | tf_op jit(solution)/shard_map/pallas_call | solution.py:66
  135.4 7.9 %shard_map.99 = (f32[2,2,256,128]{3,2,1,0:T(8,128)}, f32[2,2,256,128]{3,2,1,0:T(8,128)}, f32[2,2,256,128]{3,2,1,0:T(8,128)}) custom-call(s32[7]{0:T(128)} %concatenate.29.info_ref, bf16[2,2,256,128]{3,2,1,0:T(8,128)(2,1)} %pad_maximum_fusion.2.q_ref, ...), custom_call_target="tpu_custom_call", output_to_operand_aliasing={{0}: (2, {}), {1}: (3, {}), {2}: (4, {})} | custom-call | flops 402653184 | bytes 3145728 | tf_op jit(solution)/shard_map/pallas_call | solution.py:66
  143.3 5.4 %shard_map.100 = (f32[2,2,256,128]{3,2,1,0:T(8,128)}, f32[2,2,256,128]{3,2,1,0:T(8,128)}, f32[2,2,256,128]{3,2,1,0:T(8,128)}) custom-call(s32[5]{0:T(128)} %concatenate.28.info_ref, bf16[2,2,256,128]{3,2,1,0:T(8,128)(2,1)} %pad_maximum_fusion.2.q_ref, ...), custom_call_target="tpu_custom_call", output_to_operand_aliasing={{0}: (2, {}), {1}: (3, {}), {2}: (4, {})} | custom-call | flops 134217728 | bytes 2097152 | tf_op jit(solution)/shard_map/pallas_call | solution.py:66
  148.7 1.2 slice_reduce_fusion
  150.0 1.3 divide_convert_fusion
  151.3 1.0 collective-permute-start.16
  152.3 3.0 %fusion.48 = bf16[512,3,128]{0,2,1:T(8,128)(2,1)S(1)} fusion(s32[512]{0:T(512)S(1)} %iota_add_fusion, s32[3,512]{1,0:T(4,128)S(1)} %copy-done.7, bf16[3,512,512]{1,2,0:T(8,128)(2,1)} %get-tuple-element.47, bf16[2,3,512,128]{3,2,1,0:T(8,128)(2,1)S(1)} %copy-done.5, f32[3,512]{1,0:T(4,128)S(1)} %copy-done.8, f32[3,512]{1,0:T(4,128)S(1)} %copy-done.11), kind=kOutput, calls=%fused_computation.36 | convolution fusion | flops 404226048 | bytes 2385920 | tf_op jit(solution)/shard_map/ent,end->ted/dot_general | solution.py:169
  155.3 0.9 copy.46
  156.2 4.5 %collective-permute-done.16 = bf16[2,256,128]{2,1,0:T(8,128)(2,1)S(1)} collective-permute-done((bf16[2,256,128]{2,1,0:T(8,128)(2,1)S(1)}, bf16[2,256,128]{2,1,0:T(8,128)(2,1)S(1)}, u32[]{:S(2)}, u32[]{:S(2)}) %collective-permute-start.16) | collective-permute-done | bytes 131104 | tf_op jit(solution)/shard_map/ppermute | solution.py:126
  160.7 1.0 copy.45
  (51 shorter events, 1.1 us)
Async XLA Ops:
  0.6 118.8 %copy-start = (bf16[512,3,128]{2,0,1:T(8,128)(2,1)S(1)}, bf16[512,3,128]{2,0,1:T(8,128)(2,1)}, u32[]{:S(2)}) copy-start(bf16[512,3,128]{2,0,1:T(8,128)(2,1)} %param.11) | copy-start | bytes 1179652
  0.6 5.5 %copy-start.7 = (s32[3,512]{1,0:T(4,128)S(1)}, s32[3,512]{1,0:T(4,128)}, u32[]{:S(2)}) copy-start(s32[3,512]{1,0:T(4,128)} %param.15) | copy-start | bytes 18436
  0.7 5.5 %copy-start.9 = (bf16[512,3,128]{2,0,1:T(8,128)(2,1)S(1)}, bf16[512,3,128]{2,0,1:T(8,128)(2,1)}, u32[]{:S(2)}) copy-start(bf16[512,3,128]{2,0,1:T(8,128)(2,1)} %param.13) | copy-start | bytes 1179652
  1.9 22.7 %copy-start.1 = (bf16[2,2,512,128]{3,2,1,0:T(8,128)(2,1)}, bf16[2,2,512,128]{3,2,1,0:T(8,128)(2,1)S(1)}, u32[]{:S(2)}) copy-start(bf16[2,2,512,128]{3,2,1,0:T(8,128)(2,1)S(1)} %pad_maximum_fusion.1.refs_0_.refs_1_) | copy-start | bytes 1572868
  1.9 18.1 %collective-permute-start.2 = (bf16[2,2,512,128]{3,2,1,0:T(8,128)(2,1)S(1)}, bf16[2,2,512,128]{3,2,1,0:T(8,128)(2,1)S(1)}, u32[]{:S(2)}, u32[]{:S(2)}) collective-permute-start(bf16[2,2,512,128]{3,2,1,0:T(8,128)(2,1)S(1)} %pad_maximum_fusion.1.refs_0_.refs_1_), channel_id=1, source_target_pairs={{0,2},{1,3},{2,4},{3,5},{4,6},{5,7},{6,8},{7,9},{8,10},{9,11},{10,... | collective-permute-start | bytes 1572872 | tf_op jit(solution)/shard_map/ppermute | solution.py:115
  6.1 13.9 %copy-start.6 = (bf16[512,2,128]{2,1,0:T(2,128)(2,1)S(1)}, bf16[512,2,128]{2,1,0:T(2,128)(2,1)}, u32[]{:S(2)}) copy-start(bf16[512,2,128]{2,1,0:T(2,128)(2,1)} %param.8) | copy-start | bytes 786436
  6.8 47.8 %copy-start.10 = (bf16[3,512]{1,0:T(4,128)(2,1)S(1)}, bf16[3,512]{1,0:T(4,128)(2,1)}, u32[]{:S(2)}) copy-start(bf16[3,512]{1,0:T(4,128)(2,1)} %param.14) | copy-start | bytes 9220
  7.9 89.8 %all-to-all-start = ((bf16[2,3,16,32,128]{4,3,1,0,2:T(8,128)(2,1)}), bf16[2,3,16,32,128]{4,3,1,0,2:T(8,128)(2,1)S(1)}, u32[]{:S(2)}, u32[]{:S(2)}) async-start(bf16[2,3,16,32,128]{4,3,1,0,2:T(8,128)(2,1)} %copy.51), calls=%async_computation | async-start | bytes 1572864 | tf_op jit(solution)/shard_map/all_to_all | solution.py:163
  16.4 30.6 %collective-permute-start.3 = (bf16[2,2,512,128]{3,2,1,0:T(8,128)(2,1)S(1)}, bf16[2,2,512,128]{3,2,1,0:T(8,128)(2,1)S(1)}, u32[]{:S(2)}, u32[]{:S(2)}) collective-permute-start(bf16[2,2,512,128]{3,2,1,0:T(8,128)(2,1)S(1)} %pad_maximum_fusion.1.refs_0_.refs_1_), channel_id=1, source_target_pairs={{0,14},{1,15},{2,0},{3,1},{4,2},{5,3},{6,4},{7,5},{8,6},{9,7},{10,... | collective-permute-start | bytes 1572872 | tf_op jit(solution)/shard_map/ppermute | solution.py:118
  20.0 58.7 %copy-start.2 = (bf16[2,2,512,128]{3,2,1,0:T(8,128)(2,1)}, bf16[2,2,512,128]{3,2,1,0:T(8,128)(2,1)S(1)}, u32[]{:S(2)}) copy-start(bf16[2,2,512,128]{3,2,1,0:T(8,128)(2,1)S(1)} %collective-permute-done.2.refs_2_.refs_3_) | copy-start | bytes 1572868
  20.0 34.6 %collective-permute-start.6 = (bf16[2,2,512,128]{3,2,1,0:T(8,128)(2,1)S(1)}, bf16[2,2,512,128]{3,2,1,0:T(8,128)(2,1)}, u32[]{:S(2)}, u32[]{:S(2)}) collective-permute-start(bf16[2,2,512,128]{3,2,1,0:T(8,128)(2,1)S(1)} %collective-permute-done.2.refs_2_.refs_3_), channel_id=1, source_target_pairs={{0,2},{1,3},{2,4},{3,5},{4,6},{5,7},{6,8},{7,9},{8,10},{9,11},{10,... | collective-permute-start | bytes 1572872 | tf_op jit(solution)/shard_map/ppermute | solution.py:115
  20.1 34.2 %collective-permute-start = (bf16[2,256,128]{2,1,0:T(8,128)(2,1)S(1)}, bf16[2,256,128]{2,1,0:T(8,128)(2,1)S(1)}, u32[]{:S(2)}, u32[]{:S(2)}) collective-permute-start(bf16[2,256,128]{2,1,0:T(8,128)(2,1)S(1)} %get-tuple-element.45), channel_id=1, source_target_pairs={{0,15},{1,14},{2,13},{3,12},{4,11},{5,10},{6,9},{7,8},{8,7},{9,6},... | collective-permute-start | bytes 393224 | tf_op jit(solution)/shard_map/ppermute | solution.py:98
  24.6 54.2 %collective-permute-start.1 = (bf16[2,2,512,128]{3,2,1,0:T(8,128)(2,1)S(1)}, bf16[2,2,512,128]{3,2,1,0:T(8,128)(2,1)}, u32[]{:S(2)}, u32[]{:S(2)}) collective-permute-start(bf16[2,2,512,128]{3,2,1,0:T(8,128)(2,1)S(1)} %pad_maximum_fusion.1.refs_0_.refs_1_), channel_id=1, source_target_pairs={{0,1},{1,0},{2,3},{3,2},{4,5},{5,4},{6,7},{7,6},{8,9},{9,8},{10,11... | collective-permute-start | bytes 1572872 | tf_op jit(solution)/shard_map/ppermute | solution.py:111
  24.6 63.1 %collective-permute-start.4 = (bf16[2,2,512,128]{3,2,1,0:T(8,128)(2,1)S(1)}, bf16[2,2,512,128]{3,2,1,0:T(8,128)(2,1)S(1)}, u32[]{:S(2)}, u32[]{:S(2)}) collective-permute-start(bf16[2,2,512,128]{3,2,1,0:T(8,128)(2,1)S(1)} %collective-permute-done.2.refs_2_.refs_3_), channel_id=1, source_target_pairs={{0,1},{1,0},{2,3},{3,2},{4,5},{5,4},{6,7},{7,6},{8,9},{9,8},{10,11... | collective-permute-start | bytes 1572872 | tf_op jit(solution)/shard_map/ppermute | solution.py:120
  47.0 31.7 %copy-start.3 = (bf16[2,2,512,128]{3,2,1,0:T(8,128)(2,1)}, bf16[2,2,512,128]{3,2,1,0:T(8,128)(2,1)S(1)}, u32[]{:S(2)}) copy-start(bf16[2,2,512,128]{3,2,1,0:T(8,128)(2,1)S(1)} %collective-permute-done.3.refs_4_.refs_5_) | copy-start | bytes 1572868
  47.0 14.9 %collective-permute-start.7 = (bf16[2,2,512,128]{3,2,1,0:T(8,128)(2,1)S(1)}, bf16[2,2,512,128]{3,2,1,0:T(8,128)(2,1)}, u32[]{:S(2)}, u32[]{:S(2)}) collective-permute-start(bf16[2,2,512,128]{3,2,1,0:T(8,128)(2,1)S(1)} %collective-permute-done.3.refs_4_.refs_5_), channel_id=1, source_target_pairs={{0,14},{1,15},{2,0},{3,1},{4,2},{5,3},{6,4},{7,5},{8,6},{9,7},{10,... | collective-permute-start | bytes 1572872 | tf_op jit(solution)/shard_map/ppermute | solution.py:118
  54.3 33.6 %collective-permute-start.5 = (bf16[2,2,512,128]{3,2,1,0:T(8,128)(2,1)S(1)}, bf16[2,2,512,128]{3,2,1,0:T(8,128)(2,1)}, u32[]{:S(2)}, u32[]{:S(2)}) collective-permute-start(bf16[2,2,512,128]{3,2,1,0:T(8,128)(2,1)S(1)} %collective-permute-done.3.refs_4_.refs_5_), channel_id=1, source_target_pairs={{0,1},{1,0},{2,3},{3,2},{4,5},{5,4},{6,7},{7,6},{8,9},{9,8},{10,11... | collective-permute-start | bytes 1572872 | tf_op jit(solution)/shard_map/ppermute | solution.py:120
  54.6 14.9 %collective-permute-start.10 = (bf16[2,2,512,128]{3,2,1,0:T(8,128)(2,1)}, bf16[2,2,512,128]{3,2,1,0:T(8,128)(2,1)}, u32[]{:S(2)}, u32[]{:S(2)}) collective-permute-start(bf16[2,2,512,128]{3,2,1,0:T(8,128)(2,1)} %collective-permute-done.6.refs_4_.refs_5_), channel_id=1, source_target_pairs={{0,2},{1,3},{2,4},{3,5},{4,6},{5,7},{6,8},{7,9},{8,10},{9,11},{10,... | collective-permute-start | bytes 1572872 | tf_op jit(solution)/shard_map/ppermute | solution.py:115
  61.9 56.8 %collective-permute-start.11 = (bf16[2,2,512,128]{3,2,1,0:T(8,128)(2,1)}, bf16[2,2,512,128]{3,2,1,0:T(8,128)(2,1)}, u32[]{:S(2)}, u32[]{:S(2)}) collective-permute-start(bf16[2,2,512,128]{3,2,1,0:T(8,128)(2,1)} %collective-permute-done.7.refs_6_.refs_7_), channel_id=1, source_target_pairs={{0,14},{1,15},{2,0},{3,1},{4,2},{5,3},{6,4},{7,5},{8,6},{9,7},{10,... | collective-permute-start | bytes 1572872 | tf_op jit(solution)/shard_map/ppermute | solution.py:118
  69.5 49.5 %collective-permute-start.14 = (bf16[2,2,512,128]{3,2,1,0:T(8,128)(2,1)}, bf16[2,2,512,128]{3,2,1,0:T(8,128)(2,1)}, u32[]{:S(2)}, u32[]{:S(2)}) collective-permute-start(bf16[2,2,512,128]{3,2,1,0:T(8,128)(2,1)} %collective-permute-done.10.refs_4_.refs_5_), channel_id=1, source_target_pairs={{0,2},{1,3},{2,4},{3,5},{4,6},{5,7},{6,8},{7,9},{8,10},{9,11},{10,... | collective-permute-start | bytes 1572872 | tf_op jit(solution)/shard_map/ppermute | solution.py:115
  85.9 40.2 %collective-permute-start.8 = (bf16[2,2,512,128]{3,2,1,0:T(8,128)(2,1)}, bf16[2,2,512,128]{3,2,1,0:T(8,128)(2,1)}, u32[]{:S(2)}, u32[]{:S(2)}) collective-permute-start(bf16[2,2,512,128]{3,2,1,0:T(8,128)(2,1)} %collective-permute-done.6.refs_4_.refs_5_), channel_id=1, source_target_pairs={{0,1},{1,0},{2,3},{3,2},{4,5},{5,4},{6,7},{7,6},{8,9},{9,8},{10,11... | collective-permute-start | bytes 1572872 | tf_op jit(solution)/shard_map/ppermute | solution.py:120
  87.7 0.8 copy-start.4
  87.7 38.4 %collective-permute-start.9 = (bf16[2,2,512,128]{3,2,1,0:T(8,128)(2,1)}, bf16[2,2,512,128]{3,2,1,0:T(8,128)(2,1)}, u32[]{:S(2)}, u32[]{:S(2)}) collective-permute-start(bf16[2,2,512,128]{3,2,1,0:T(8,128)(2,1)} %collective-permute-done.7.refs_6_.refs_7_), channel_id=1, source_target_pairs={{0,1},{1,0},{2,3},{3,2},{4,5},{5,4},{6,7},{7,6},{8,9},{9,8},{10,11... | collective-permute-start | bytes 1572872 | tf_op jit(solution)/shard_map/ppermute | solution.py:120
  118.6 16.8 %collective-permute-start.12 = (bf16[2,2,512,128]{3,2,1,0:T(8,128)(2,1)}, bf16[2,2,512,128]{3,2,1,0:T(8,128)(2,1)}, u32[]{:S(2)}, u32[]{:S(2)}) collective-permute-start(bf16[2,2,512,128]{3,2,1,0:T(8,128)(2,1)} %collective-permute-done.10.refs_4_.refs_5_), channel_id=1, source_target_pairs={{0,1},{1,0},{2,3},{3,2},{4,5},{5,4},{6,7},{7,6},{8,9},{9,8},{10,11... | collective-permute-start | bytes 1572872 | tf_op jit(solution)/shard_map/ppermute | solution.py:120
  118.7 16.6 %collective-permute-start.13 = (bf16[2,2,512,128]{3,2,1,0:T(8,128)(2,1)}, bf16[2,2,512,128]{3,2,1,0:T(8,128)(2,1)}, u32[]{:S(2)}, u32[]{:S(2)}) collective-permute-start(bf16[2,2,512,128]{3,2,1,0:T(8,128)(2,1)} %collective-permute-done.11.refs_6_.refs_7_), channel_id=1, source_target_pairs={{0,1},{1,0},{2,3},{3,2},{4,5},{5,4},{6,7},{7,6},{8,9},{9,8},{10,11... | collective-permute-start | bytes 1572872 | tf_op jit(solution)/shard_map/ppermute | solution.py:120
  119.1 24.2 %collective-permute-start.15 = (bf16[2,2,512,128]{3,2,1,0:T(8,128)(2,1)}, bf16[2,2,512,128]{3,2,1,0:T(8,128)(2,1)}, u32[]{:S(2)}, u32[]{:S(2)}) collective-permute-start(bf16[2,2,512,128]{3,2,1,0:T(8,128)(2,1)} %collective-permute-done.14.refs_4_.refs_5_), channel_id=1, source_target_pairs={{0,1},{1,0},{2,3},{3,2},{4,5},{5,4},{6,7},{7,6},{8,9},{9,8},{10,11... | collective-permute-start | bytes 1572872 | tf_op jit(solution)/shard_map/ppermute | solution.py:120
  143.3 9.0 %copy-start.5 = (bf16[2,3,512,128]{3,2,1,0:T(8,128)(2,1)S(1)}, bf16[2,3,512,128]{3,2,1,0:T(8,128)(2,1)}, u32[]{:S(2)}) copy-start(bf16[2,3,512,128]{3,2,1,0:T(8,128)(2,1)} %all_gather.3) | copy-start | bytes 2359300
  143.3 9.0 %copy-start.8 = (f32[3,512]{1,0:T(4,128)S(1)}, f32[3,512]{1,0:T(4,128)}, u32[]{:S(2)}) copy-start(f32[3,512]{1,0:T(4,128)} %fusion.60) | copy-start | bytes 18436
  143.3 9.0 %copy-start.11 = (f32[3,512]{1,0:T(4,128)S(1)}, f32[3,512]{1,0:T(4,128)}, u32[]{:S(2)}) copy-start(f32[3,512]{1,0:T(4,128)} %get-tuple-element.46) | copy-start | bytes 18436
  151.3 9.4 %collective-permute-start.16 = (bf16[2,256,128]{2,1,0:T(8,128)(2,1)S(1)}, bf16[2,256,128]{2,1,0:T(8,128)(2,1)S(1)}, u32[]{:S(2)}, u32[]{:S(2)}) collective-permute-start(bf16[2,256,128]{2,1,0:T(8,128)(2,1)S(1)} %get-tuple-element.43), channel_id=1, source_target_pairs={{0,15},{1,14},{2,13},{3,12},{4,11},{5,10},{6,9},{7,8},{8,7},{9,6},... | collective-permute-start | bytes 393224 | tf_op jit(solution)/shard_map/ppermute | solution.py:126

commit v5 on v3

--- a/solution.py
+++ b/solution.py
@@ -11,21 +11,18 @@
 NEGATIVE = -1e30
 
 
-def flash_kernel(info_ref, q_ref, k_ref, v_ref, o_ref, m_ref, l_ref, acc_ref, *, scale, blocks):
-    part = pl.program_id(1)
-    step = pl.program_id(2)
-    last = info_ref[part]
-    offset = info_ref[2 + part]
+def flash_kernel(info_ref, q_ref, k_ref, v_ref, o_ref, m_ref, l_ref, acc_ref, *, scale, block):
+    last = info_ref[0]
+    offset = info_ref[1]
+    m_ref[...] = jnp.full(m_ref.shape, NEGATIVE, jnp.float32)
+    l_ref[...] = jnp.zeros(l_ref.shape, jnp.float32)
+    acc_ref[...] = jnp.zeros(acc_ref.shape, jnp.float32)
 
-    @pl.when(step == 0)
-    def _():
-        m_ref[...] = jnp.full(m_ref.shape, NEGATIVE, jnp.float32)
-        l_ref[...] = jnp.zeros(l_ref.shape, jnp.float32)
-        acc_ref[...] = jnp.zeros(acc_ref.shape, jnp.float32)
-
-    def update(masked):
+    def update(j, masked):
+        first = pl.multiple_of(j * block, block)
         scores = lax.dot_general(
-            q_ref[0, 0], k_ref[0], (((1,), (1,)), ((), ())), preferred_element_type=jnp.float32
+            q_ref[0], k_ref[0, pl.ds(first, block), :], (((1,), (1,)), ((), ())),
+            preferred_element_type=jnp.float32,
         ) * scale
         if masked:
             rows = lax.broadcasted_iota(jnp.int32, scores.shape, 0) + offset
@@ -36,55 +33,47 @@
         shrink = jnp.exp(m_prev - m_new)
         weights = jnp.exp(scores - m_new)
         l_new = l_ref[:, :1] * shrink + jnp.sum(weights, axis=1, keepdims=True)
-        moved = jnp.dot(weights.astype(jnp.bfloat16), v_ref[0], preferred_element_type=jnp.float32)
+        moved = jnp.dot(
+            weights.astype(jnp.bfloat16), v_ref[0, pl.ds(first, block), :],
+            preferred_element_type=jnp.float32,
+        )
         acc_ref[...] = acc_ref[...] * shrink + moved
         m_ref[...] = jnp.broadcast_to(m_new, m_ref.shape)
         l_ref[...] = jnp.broadcast_to(l_new, l_ref.shape)
 
-    @pl.when(step < last)
-    def _():
-        update(False)
+    def body(j, carry):
+        update(j, False)
+        return carry
 
-    @pl.when(step == last)
-    def _():
-        update(True)
-
-    @pl.when(step == blocks - 1)
-    def _():
-        o_ref[0, 0] = (acc_ref[...] / l_ref[:, :1]).astype(o_ref.dtype)
+    lax.fori_loop(0, last, body, 0)
+    update(last, True)
+    o_ref[0] = (acc_ref[...] / l_ref[:, :1]).astype(o_ref.dtype)
 
 
 def dense_flash(info, queries, stacked):
-    parts, heads, rows, width = queries.shape
+    heads, rows, width = queries.shape
     length = stacked.shape[2]
     block = 512
-    blocks = length // block
     scale = 1.0 / math.sqrt(width)
-
-    def kv_map(which):
-        return lambda h, p, j, c: (which, h, jnp.minimum(j, c[p]), 0)
-
     return pl.pallas_call(
-        functools.partial(flash_kernel, scale=scale, blocks=blocks),
-        out_shape=jax.ShapeDtypeStruct((parts, heads, rows, width), jnp.bfloat16),
+        functools.partial(flash_kernel, scale=scale, block=block),
+        out_shape=jax.ShapeDtypeStruct((heads, rows, width), jnp.bfloat16),
         grid_spec=pltpu.PrefetchScalarGridSpec(
             num_scalar_prefetch=1,
-            grid=(heads, parts, blocks),
+            grid=(heads,),
             in_specs=[
-                pl.BlockSpec((1, 1, rows, width), lambda h, p, j, c: (p, h, 0, 0)),
-                pl.BlockSpec((None, 1, block, width), kv_map(0)),
-                pl.BlockSpec((None, 1, block, width), kv_map(1)),
+                pl.BlockSpec((1, rows, width), lambda h, c: (h, 0, 0)),
+                pl.BlockSpec((None, 1, length, width), lambda h, c: (0, h, 0, 0)),
+                pl.BlockSpec((None, 1, length, width), lambda h, c: (1, h, 0, 0)),
             ],
-            out_specs=pl.BlockSpec((1, 1, rows, width), lambda h, p, j, c: (p, h, 0, 0)),
+            out_specs=pl.BlockSpec((1, rows, width), lambda h, c: (h, 0, 0)),
             scratch_shapes=[
                 pltpu.VMEM((rows, 128), jnp.float32),
                 pltpu.VMEM((rows, 128), jnp.float32),
                 pltpu.VMEM((rows, width), jnp.float32),
             ],
         ),
-        compiler_params=pltpu.CompilerParams(
-            dimension_semantics=("arbitrary", "arbitrary", "arbitrary")
-        ),
+        compiler_params=pltpu.CompilerParams(dimension_semantics=("arbitrary",)),
         cost_estimate=pl.CostEstimate(
             flops=2 * heads * rows * length * width,
             transcendentals=heads * rows * length // 2,
@@ -104,11 +93,10 @@
     gathered = lax.all_gather(stacked, "seq", axis=2, tiled=True)
     rows_first = jnp.swapaxes(queries, 0, 1)
     lent = lax.ppermute(rows_first[:, half:], "seq", swap)
-    both = jnp.stack([rows_first[:, :half], lent], axis=0)
-    info = jnp.stack([me, partner, jnp.int32(0), jnp.int32(half)])
-    out = dense_flash(info, both, gathered)
-    returned = lax.ppermute(out[1], "seq", swap)
-    mine = jnp.concatenate([out[0], returned], axis=1)
+    theirs = dense_flash(jnp.stack([partner, jnp.int32(half)]), lent, gathered)
+    returned = lax.ppermute(theirs, "seq", swap)
+    ours = dense_flash(jnp.stack([me, jnp.int32(0)]), rows_first[:, :half], gathered)
+    mine = jnp.concatenate([ours, returned], axis=1)
     return jnp.swapaxes(mine, 0, 1)
 
 

time: 148 us -> 148 us (level)
  the two profiles are of different devices: /device:TPU:1 before, /device:TPU:225 now
where the time goes in v5:
time: 148 us; the launch traced here: 147 us
  waiting for transfers between devices  32.9 us (22%)
  Pallas kernels  28.2 us (19%)
  starting transfers between devices  26.3 us (18%)
  blocking collectives  25.5 us (17%)
  between operations  14.2 us (10%)
  other arithmetic  9.33 us (6%)
  matrix products  5.92 us (4%)
  local copies, waits for them, and re-layouts  4.91 us (3%)
    pallas_call x2, Pallas kernels, dense_flash(): pl.pallas_call(functools.partial(flash_kernel, scale=scale, block=block),...  28.2 us
    all_gather x1, blocking collectives, sparse_heads(): picked_kv = lax.all_gather(own, 'seq', axis=2, tiled=True)  25.5 us
    all_to_all x1, waiting for transfers between devices, sparse_heads(): arrived = lax.all_to_all(pieces, 'seq', 2, 2, tiled=True)  21.5 us
    ppermute x1, starting transfers between devices, dense_heads(): returned = lax.ppermute(theirs, 'seq', swap)  20 us
    all_gather x1, waiting for transfers between devices, dense_heads(): gathered = lax.all_gather(stacked, 'seq', axis=2, tiled=True)  11.4 us
    all_to_all x1, starting transfers between devices, sparse_heads(): arrived = lax.all_to_all(pieces, 'seq', 2, 2, tiled=True)  6.18 us
    sub x1, other arithmetic, attend_ranked(): weights = jnp.where(visible, jnp.exp(scores - leading), 0.0)  4.65 us
  transfers between devices with their start and end apart: 4, of which 2 were waited for; matrix products, arithmetic and copies ran while one was open for 11% of the time, Pallas kernels for 15%

profile of v5, /device:TPU:225, one launch (start us, length us, event | category | flops | bytes accessed | tf_op | source)
XLA Modules:
  0.0 147.2 jit_solution(13410953277876964017)
XLA Ops:
  7.2 0.0 copy-start
  7.2 0.0 copy-start.3
  7.2 0.0 copy-start.5
  7.2 0.0 all-gather.2.cloned.1.call-start
  7.2 1.2 copy_bitcast_fusion
  8.4 0.9 pad_maximum_fusion.1
  9.3 0.0 all-gather.2.cloned.1.call-update
  9.3 1.7 %fusion.42 = bf16[3,512,128]{2,1,0:T(8,128)(2,1)S(1)} fusion(bf16[512,3,128]{2,0,1:T(8,128)(2,1)} %param.13, s32[512]{0:T(512)S(1)} %iota_add_fusion, s32[3,512]{1,0:T(4,128)} %param.15), kind=kOutput, calls=%fused_computation.34 | convolution fusion | flops 202309632 | bytes 794624 | tf_op jit(solution)/shard_map/ent,ted->end/dot_general | solution.py:127
  11.0 0.0 copy-done.3
  11.0 0.0 copy-done.5
  11.0 0.0 copy-start.2
  11.0 0.6 fusion.39
  11.7 0.0 copy-start.6
  11.7 0.1 pad_maximum_fusion
  11.8 1.0 copy.24
  12.8 6.2 %all-to-all-start = ((bf16[2,3,16,32,128]{4,3,1,0,2:T(8,128)(2,1)}), bf16[2,3,16,32,128]{4,3,1,0,2:T(8,128)(2,1)S(1)}, u32[]{:S(2)}, u32[]{:S(2)}) async-start(bf16[2,3,16,32,128]{4,3,1,0,2:T(8,128)(2,1)} %copy.24), calls=%async_computation | async-start | bytes 1572864 | tf_op jit(solution)/shard_map/all_to_all | solution.py:135
  19.0 0.0 copy-done.2
  19.1 0.7 fusion.64
  19.8 0.1 collective-permute-start
  19.8 0.6 pad_add_fusion.1.info_ref
  20.5 0.6 pad_add_fusion.info_ref
  21.1 0.8 iota_compare_fusion
  21.9 0.0 copy-done.6
  21.9 0.6 fusion.3
  22.5 0.6 fusion.60
  23.2 21.5 %all-to-all-done = bf16[2,3,16,32,128]{4,3,1,0,2:T(8,128)(2,1)S(1)} async-done(((bf16[2,3,16,32,128]{4,3,1,0,2:T(8,128)(2,1)}), bf16[2,3,16,32,128]{4,3,1,0,2:T(8,128)(2,1)S(1)}, u32[]{:S(2)}, u32[]{:S(2)}) %all-to-all-start) | async-done | bytes 786464 | tf_op jit(solution)/shard_map/all_to_all | solution.py:135
  44.7 0.1 reduce_sum.21
  44.8 25.5 %all_gather.7 = bf16[2,3,512,128]{3,2,1,0:T(8,128)(2,1)} all-gather(bf16[2,3,32,128]{3,2,1,0:T(8,128)(2,1)S(1)} %reduce_sum.21), channel_id=1, replica_groups=mesh['dp'=4,'head'=4,'seq'=16] {'seq'}, dimensions={2}, use_global_device_ids=true | all-gather | bytes 835584 | tf_op jit(solution)/shard_map/all_gather | solution.py:137
  70.3 0.0 copy-done
  70.3 2.1 %fusion.52 = f32[3,512,512]{1,2,0:T(8,128)S(1)} fusion(bf16[512,3,128]{2,0,1:T(8,128)(2,1)S(1)} %copy-done, s32[512]{0:T(512)S(1)} %iota_add_fusion, s32[3,512]{1,0:T(4,128)S(1)} %copy-done.3, bf16[2,3,512,128]{3,2,1,0:T(8,128)(2,1)} %all_gather.7), kind=kOutput, calls=%fused_computation.37 | convolution fusion | flops 403636224 | bytes 3940352 | tf_op jit(solution)/shard_map/erd,ekd->erk/dot_general | solution.py:107
  72.3 4.7 %fusion.65 = (f32[3,512]{1,0:T(4,128)}, bf16[3,512,512]{1,2,0:T(8,128)(2,1)}) fusion(f32[3,512,512]{1,2,0:T(8,128)S(1)} %fusion.52, pred[512,512]{0,1:T(8,128)(4,1)} %iota_compare_fusion), kind=kOutput, calls=%fused_computation.60 | output fusion | flops 6291967 | bytes 4986880 | tf_op jit(solution)/shard_map/sub | solution.py:111
  77.0 0.0 copy-start.1
  77.0 0.0 copy-start.4
  77.0 0.0 copy-start.7
  77.0 0.0 collective-permute-done.q_ref
  77.0 11.4 %all-gather.2.cloned.1.call-done.k_ref.v_ref = bf16[2,2,8192,128]{3,2,1,0:T(8,128)(2,1)} async-done(((bf16[2,2,512,128]{3,2,1,0:T(8,128)(2,1)}), bf16[2,2,8192,128]{3,2,1,0:T(8,128)(2,1)}) %all-gather.2.cloned.1.call-update) | async-done | bytes 8388624 | tf_op jit(solution)/shard_map/all_gather | solution.py:93
  88.3 5.5 %shard_map.96 = bf16[2,256,128]{2,1,0:T(8,128)(2,1)} custom-call(s32[2]{0:T(128)} %pad_add_fusion.1.info_ref, bf16[2,256,128]{2,1,0:T(8,128)(2,1)} %collective-permute-done.q_ref, bf16[2,2,8192,128]{3,2,1,0:T(8,128)(2,1)} %all-gather.2.cloned.1.call-done.k_ref.v_ref, bf16[2,2,8192,128]{3,2,1,0:T(8,128)(2,1)} %all-gather.2.cloned.1.call-done.k_ref.v_ref), custom_call_target="tpu_custom_call" | custom-call | flops 1073741824 | bytes 4456448 | tf_op jit(solution)/shard_map/pallas_call | solution.py:58
  93.8 20.0 %collective-permute-start.1 = (bf16[2,256,128]{2,1,0:T(8,128)(2,1)}, bf16[2,256,128]{2,1,0:T(8,128)(2,1)S(1)}, u32[]{:S(2)}, u32[]{:S(2)}) collective-permute-start(bf16[2,256,128]{2,1,0:T(8,128)(2,1)} %shard_map.96), channel_id=1, source_target_pairs={{0,15},{1,14},{2,13},{3,12},{4,11},{5,10},{6,9},{7,8},{8,7},{9,6},... | collective-permute-start | bytes 393224 | tf_op jit(solution)/shard_map/ppermute | solution.py:97
  113.9 0.0 copy-done.1
  113.9 0.0 copy-done.4
  113.9 0.0 copy-done.7
  113.9 0.0 copy-done.8
  113.9 0.9 fusion.48
  114.8 0.9 copy.21
  115.8 22.7 %shard_map.95 = bf16[2,256,128]{2,1,0:T(8,128)(2,1)} custom-call(s32[2]{0:T(128)} %pad_add_fusion.info_ref, bf16[2,256,128]{2,1,0:T(8,128)(2,1)} %get-tuple-element.6.q_ref, bf16[2,2,8192,128]{3,2,1,0:T(8,128)(2,1)} %all-gather.2.cloned.1.call-done.k_ref.v_ref, bf16[2,2,8192,128]{3,2,1,0:T(8,128)(2,1)} %all-gather.2.cloned.1.call-done.k_ref.v_ref), custom_call_target="tpu_custom_call" | custom-call | flops 1073741824 | bytes 4456448 | tf_op jit(solution)/shard_map/pallas_call | solution.py:58
  138.5 0.0 collective-permute-done.1
  138.5 0.9 maximum_bitcast_fusion
  139.4 1.0 copy.20
  (3 shorter events, 0.0 us)
Async XLA Ops:
  7.2 63.1 %copy-start = (bf16[512,3,128]{2,0,1:T(8,128)(2,1)S(1)}, bf16[512,3,128]{2,0,1:T(8,128)(2,1)}, u32[]{:S(2)}) copy-start(bf16[512,3,128]{2,0,1:T(8,128)(2,1)} %param.11) | copy-start | bytes 1179652
  7.2 3.8 %copy-start.3 = (s32[3,512]{1,0:T(4,128)S(1)}, s32[3,512]{1,0:T(4,128)}, u32[]{:S(2)}) copy-start(s32[3,512]{1,0:T(4,128)} %param.15) | copy-start | bytes 18436
  7.2 3.8 %copy-start.5 = (bf16[512,3,128]{2,0,1:T(8,128)(2,1)S(1)}, bf16[512,3,128]{2,0,1:T(8,128)(2,1)}, u32[]{:S(2)}) copy-start(bf16[512,3,128]{2,0,1:T(8,128)(2,1)} %param.12) | copy-start | bytes 1179652
  7.2 81.1 %all-gather.2.cloned.1.call-start = ((), (), s32[]{:S(2)}) async-start(), calls=%async_computation.1 | async-start | bytes 8912896 | tf_op jit(solution)/shard_map/all_gather | solution.py:93
  11.0 8.0 %copy-start.2 = (bf16[512,2,128]{2,1,0:T(2,128)(2,1)S(1)}, bf16[512,2,128]{2,1,0:T(2,128)(2,1)}, u32[]{:S(2)}) copy-start(bf16[512,2,128]{2,1,0:T(2,128)(2,1)} %param.8) | copy-start | bytes 786436
  11.7 10.2 %copy-start.6 = (bf16[3,512]{1,0:T(4,128)(2,1)S(1)}, bf16[3,512]{1,0:T(4,128)(2,1)}, u32[]{:S(2)}) copy-start(bf16[3,512]{1,0:T(4,128)(2,1)} %param.14) | copy-start | bytes 9220
  12.8 31.9 %all-to-all-start = ((bf16[2,3,16,32,128]{4,3,1,0,2:T(8,128)(2,1)}), bf16[2,3,16,32,128]{4,3,1,0,2:T(8,128)(2,1)S(1)}, u32[]{:S(2)}, u32[]{:S(2)}) async-start(bf16[2,3,16,32,128]{4,3,1,0,2:T(8,128)(2,1)} %copy.24), calls=%async_computation | async-start | bytes 1572864 | tf_op jit(solution)/shard_map/all_to_all | solution.py:135
  19.8 57.2 %collective-permute-start = (bf16[2,256,128]{2,1,0:T(8,128)(2,1)}, bf16[2,256,128]{2,1,0:T(8,128)(2,1)}, u32[]{:S(2)}, u32[]{:S(2)}) collective-permute-start(bf16[2,256,128]{2,1,0:T(8,128)(2,1)} %get-tuple-element.7), channel_id=1, source_target_pairs={{0,15},{1,14},{2,13},{3,12},{4,11},{5,10},{6,9},{7,8},{8,7},{9,6},... | collective-permute-start | bytes 393224 | tf_op jit(solution)/shard_map/ppermute | solution.py:95
  77.0 36.9 %copy-start.1 = (bf16[2,3,512,128]{3,2,1,0:T(8,128)(2,1)S(1)}, bf16[2,3,512,128]{3,2,1,0:T(8,128)(2,1)}, u32[]{:S(2)}) copy-start(bf16[2,3,512,128]{3,2,1,0:T(8,128)(2,1)} %all_gather.7) | copy-start | bytes 2359300
  77.0 36.9 %copy-start.4 = (f32[3,512]{1,0:T(4,128)S(1)}, f32[3,512]{1,0:T(4,128)}, u32[]{:S(2)}) copy-start(f32[3,512]{1,0:T(4,128)} %fusion.60) | copy-start | bytes 18436
  77.0 36.9 %copy-start.7 = (bf16[3,512,512]{1,2,0:T(8,128)(2,1)S(1)}, bf16[3,512,512]{1,2,0:T(8,128)(2,1)}, u32[]{:S(2)}) copy-start(bf16[3,512,512]{1,2,0:T(8,128)(2,1)} %get-tuple-element.9) | copy-start | bytes 4718596
  77.0 36.9 %copy-start.8 = (f32[3,512]{1,0:T(4,128)S(1)}, f32[3,512]{1,0:T(4,128)}, u32[]{:S(2)}) copy-start(f32[3,512]{1,0:T(4,128)} %get-tuple-element.8) | copy-start | bytes 18436
  93.8 44.6 %collective-permute-start.1 = (bf16[2,256,128]{2,1,0:T(8,128)(2,1)}, bf16[2,256,128]{2,1,0:T(8,128)(2,1)S(1)}, u32[]{:S(2)}, u32[]{:S(2)}) collective-permute-start(bf16[2,256,128]{2,1,0:T(8,128)(2,1)} %shard_map.96), channel_id=1, source_target_pairs={{0,15},{1,14},{2,13},{3,12},{4,11},{5,10},{6,9},{7,8},{8,7},{9,6},... | collective-permute-start | bytes 393224 | tf_op jit(solution)/shard_map/ppermute | solution.py:97
Sparse Core Ops, SparseCore 0:
  9.9 78.4 all-gather.1

commit v6 on v5

--- a/solution.py
+++ b/solution.py
@@ -12,8 +12,9 @@
 
 
 def flash_kernel(info_ref, q_ref, k_ref, v_ref, o_ref, m_ref, l_ref, acc_ref, *, scale, block):
-    last = info_ref[0]
-    offset = info_ref[1]
+    part = pl.program_id(1)
+    last = info_ref[part]
+    offset = info_ref[2 + part]
     m_ref[...] = jnp.full(m_ref.shape, NEGATIVE, jnp.float32)
     l_ref[...] = jnp.zeros(l_ref.shape, jnp.float32)
     acc_ref[...] = jnp.zeros(acc_ref.shape, jnp.float32)
@@ -21,7 +22,7 @@
     def update(j, masked):
         first = pl.multiple_of(j * block, block)
         scores = lax.dot_general(
-            q_ref[0], k_ref[0, pl.ds(first, block), :], (((1,), (1,)), ((), ())),
+            q_ref[0, 0], k_ref[0, pl.ds(first, block), :], (((1,), (1,)), ((), ())),
             preferred_element_type=jnp.float32,
         ) * scale
         if masked:
@@ -47,36 +48,36 @@
 
     lax.fori_loop(0, last, body, 0)
     update(last, True)
-    o_ref[0] = (acc_ref[...] / l_ref[:, :1]).astype(o_ref.dtype)
+    o_ref[0, 0] = (acc_ref[...] / l_ref[:, :1]).astype(o_ref.dtype)
 
 
 def dense_flash(info, queries, stacked):
-    heads, rows, width = queries.shape
+    parts, heads, rows, width = queries.shape
     length = stacked.shape[2]
     block = 512
     scale = 1.0 / math.sqrt(width)
     return pl.pallas_call(
         functools.partial(flash_kernel, scale=scale, block=block),
-        out_shape=jax.ShapeDtypeStruct((heads, rows, width), jnp.bfloat16),
+        out_shape=jax.ShapeDtypeStruct((parts, heads, rows, width), jnp.bfloat16),
         grid_spec=pltpu.PrefetchScalarGridSpec(
             num_scalar_prefetch=1,
-            grid=(heads,),
+            grid=(heads, parts),
             in_specs=[
-                pl.BlockSpec((1, rows, width), lambda h, c: (h, 0, 0)),
-                pl.BlockSpec((None, 1, length, width), lambda h, c: (0, h, 0, 0)),
-                pl.BlockSpec((None, 1, length, width), lambda h, c: (1, h, 0, 0)),
+                pl.BlockSpec((1, 1, rows, width), lambda h, p, c: (p, h, 0, 0)),
+                pl.BlockSpec((None, 1, length, width), lambda h, p, c: (0, h, 0, 0)),
+                pl.BlockSpec((None, 1, length, width), lambda h, p, c: (1, h, 0, 0)),
             ],
-            out_specs=pl.BlockSpec((1, rows, width), lambda h, c: (h, 0, 0)),
+            out_specs=pl.BlockSpec((1, 1, rows, width), lambda h, p, c: (p, h, 0, 0)),
             scratch_shapes=[
                 pltpu.VMEM((rows, 128), jnp.float32),
                 pltpu.VMEM((rows, 128), jnp.float32),
                 pltpu.VMEM((rows, width), jnp.float32),
             ],
         ),
-        compiler_params=pltpu.CompilerParams(dimension_semantics=("arbitrary",)),
+        compiler_params=pltpu.CompilerParams(dimension_semantics=("arbitrary", "arbitrary")),
         cost_estimate=pl.CostEstimate(
-            flops=2 * heads * rows * length * width,
-            transcendentals=heads * rows * length // 2,
+            flops=2 * parts * heads * rows * length * width,
+            transcendentals=parts * heads * rows * length // 2,
             bytes_accessed=stacked.size + 4 * queries.size,
         ),
     )(info, queries, stacked, stacked)
@@ -93,10 +94,11 @@
     gathered = lax.all_gather(stacked, "seq", axis=2, tiled=True)
     rows_first = jnp.swapaxes(queries, 0, 1)
     lent = lax.ppermute(rows_first[:, half:], "seq", swap)
-    theirs = dense_flash(jnp.stack([partner, jnp.int32(half)]), lent, gathered)
-    returned = lax.ppermute(theirs, "seq", swap)
-    ours = dense_flash(jnp.stack([me, jnp.int32(0)]), rows_first[:, :half], gathered)
-    mine = jnp.concatenate([ours, returned], axis=1)
+    both = jnp.stack([rows_first[:, :half], lent], axis=0)
+    info = jnp.stack([me, partner, jnp.int32(0), jnp.int32(half)])
+    out = dense_flash(info, both, gathered)
+    returned = lax.ppermute(out[1], "seq", swap)
+    mine = jnp.concatenate([out[0], returned], axis=1)
     return jnp.swapaxes(mine, 0, 1)
 
 

time: 148 us -> 138 us (0.932)
  the two profiles are of different devices: /device:TPU:225 before, /device:TPU:1 now
where the time goes in v6:
time: 138 us; the launch traced here: 137 us
  waiting for transfers between devices  40 us (29%)
  Pallas kernels  24.3 us (18%)
  blocking collectives  23.4 us (17%)
  between operations  14.2 us (10%)
  starting transfers between devices  14.1 us (10%)
  other arithmetic  8.61 us (6%)
  matrix products  7.35 us (5%)
  local copies, waits for them, and re-layouts  5.2 us (4%)
    ppermute x1, waiting for transfers between devices, dense_heads(): lent = lax.ppermute(rows_first[:, half:], 'seq', swap)  29.4 us
    pallas_call x1, Pallas kernels, dense_flash(): pl.pallas_call(functools.partial(flash_kernel, scale=scale, block=block),...  24.3 us
    all_gather x1, blocking collectives, sparse_heads(): picked_kv = lax.all_gather(own, 'seq', axis=2, tiled=True)  23.4 us
    all_to_all x1, starting transfers between devices, sparse_heads(): arrived = lax.all_to_all(pieces, 'seq', 2, 2, tiled=True)  9.98 us
    all_gather x1, waiting for transfers between devices, dense_heads(): gathered = lax.all_gather(stacked, 'seq', axis=2, tiled=True)  5.78 us
    ppermute x1, waiting for transfers between devices, dense_heads(): returned = lax.ppermute(out[1], 'seq', swap)  4.87 us
    sub x1, other arithmetic, attend_ranked(): weights = jnp.where(visible, jnp.exp(scores - leading), 0.0)  4.73 us
    ppermute x1, starting transfers between devices, dense_heads(): lent = lax.ppermute(rows_first[:, half:], 'seq', swap)  2.93 us
  transfers between devices with their start and end apart: 4, of which 3 were waited for; matrix products, arithmetic and copies ran while one was open for 12% of the time, Pallas kernels for 0%

profile of v6, /device:TPU:1, one launch (start us, length us, event | category | flops | bytes accessed | tf_op | source)
XLA Modules:
  0.0 137.1 jit_solution(7244579757684365852)
XLA Ops:
  7.2 0.0 copy-start
  7.2 0.0 copy-start.3
  7.2 0.0 copy-start.5
  7.2 0.0 all-gather.2.cloned.1.call-start
  7.2 1.2 copy_bitcast_fusion
  8.4 0.9 pad_maximum_fusion.1
  9.3 0.0 all-gather.2.cloned.1.call-update
  9.3 1.7 %fusion.42 = bf16[3,512,128]{2,1,0:T(8,128)(2,1)S(1)} fusion(bf16[512,3,128]{2,0,1:T(8,128)(2,1)} %param.13, s32[512]{0:T(512)S(1)} %iota_add_fusion, s32[3,512]{1,0:T(4,128)} %param.15), kind=kOutput, calls=%fused_computation.34 | convolution fusion | flops 202309632 | bytes 794624 | tf_op jit(solution)/shard_map/ent,ted->end/dot_general | solution.py:129
  11.0 0.0 copy-done.3
  11.0 0.0 copy-done.5
  11.0 0.0 copy-start.2
  11.0 0.6 fusion.39
  11.7 0.0 copy-start.6
  11.7 0.1 pad_maximum_fusion
  11.8 1.0 copy.24
  12.8 10.0 %all-to-all-start = ((bf16[2,3,16,32,128]{4,3,1,0,2:T(8,128)(2,1)}), bf16[2,3,16,32,128]{4,3,1,0,2:T(8,128)(2,1)S(1)}, u32[]{:S(2)}, u32[]{:S(2)}) async-start(bf16[2,3,16,32,128]{4,3,1,0,2:T(8,128)(2,1)} %copy.24), calls=%async_computation | async-start | bytes 1572864 | tf_op jit(solution)/shard_map/all_to_all | solution.py:137
  22.8 0.0 copy-done.2
  22.9 2.9 %collective-permute-start = (bf16[2,256,128]{2,1,0:T(8,128)(2,1)S(1)}, bf16[2,256,128]{2,1,0:T(8,128)(2,1)S(1)}, u32[]{:S(2)}, u32[]{:S(2)}) collective-permute-start(bf16[2,256,128]{2,1,0:T(8,128)(2,1)S(1)} %get-tuple-element.9), channel_id=1, source_target_pairs={{0,15},{1,14},{2,13},{3,12},{4,11},{5,10},{6,9},{7,8},{8,7},{9,6},... | collective-permute-start | bytes 393224 | tf_op jit(solution)/shard_map/ppermute | solution.py:96
  25.8 0.0 copy-done.6
  25.8 0.6 fusion.3
  26.5 0.6 fusion.60
  27.1 0.7 pad_add_fusion.info_ref
  27.8 0.8 iota_compare_fusion
  28.5 29.4 %collective-permute-done = bf16[2,256,128]{2,1,0:T(8,128)(2,1)S(1)} collective-permute-done((bf16[2,256,128]{2,1,0:T(8,128)(2,1)S(1)}, bf16[2,256,128]{2,1,0:T(8,128)(2,1)S(1)}, u32[]{:S(2)}, u32[]{:S(2)}) %collective-permute-start) | collective-permute-done | bytes 131104 | tf_op jit(solution)/shard_map/ppermute | solution.py:96
  57.9 0.7 pad_maximum_fusion.2.q_ref
  58.6 0.0 all-to-all-done
  58.6 0.1 reduce_sum.21
  58.8 23.4 %all_gather.7 = bf16[2,3,512,128]{3,2,1,0:T(8,128)(2,1)} all-gather(bf16[2,3,32,128]{3,2,1,0:T(8,128)(2,1)S(1)} %reduce_sum.21), channel_id=1, replica_groups=mesh['dp'=4,'head'=4,'seq'=16] {'seq'}, dimensions={2}, use_global_device_ids=true | all-gather | bytes 835584 | tf_op jit(solution)/shard_map/all_gather | solution.py:139
  82.1 0.0 copy-done
  82.1 2.1 %fusion.52 = f32[3,512,512]{1,2,0:T(8,128)S(1)} fusion(bf16[512,3,128]{2,0,1:T(8,128)(2,1)S(1)} %copy-done, s32[512]{0:T(512)S(1)} %iota_add_fusion, s32[3,512]{1,0:T(4,128)S(1)} %copy-done.3, bf16[2,3,512,128]{3,2,1,0:T(8,128)(2,1)} %all_gather.7), kind=kOutput, calls=%fused_computation.37 | convolution fusion | flops 403636224 | bytes 3940352 | tf_op jit(solution)/shard_map/erd,ekd->erk/dot_general | solution.py:109
  84.2 4.7 %fusion.64 = (f32[3,512]{1,0:T(4,128)}, bf16[3,512,512]{1,2,0:T(8,128)(2,1)}) fusion(f32[3,512,512]{1,2,0:T(8,128)S(1)} %fusion.52, pred[512,512]{0,1:T(8,128)(4,1)} %iota_compare_fusion), kind=kOutput, calls=%fused_computation.62 | output fusion | flops 6291967 | bytes 4986880 | tf_op jit(solution)/shard_map/sub | solution.py:113
  88.9 0.0 copy-start.1
  88.9 0.0 copy-start.4
  88.9 0.0 copy-start.7
  88.9 5.8 %all-gather.2.cloned.1.call-done.k_ref.v_ref = bf16[2,2,8192,128]{3,2,1,0:T(8,128)(2,1)} async-done(((bf16[2,2,512,128]{3,2,1,0:T(8,128)(2,1)}), bf16[2,2,8192,128]{3,2,1,0:T(8,128)(2,1)}) %all-gather.2.cloned.1.call-update) | async-done | bytes 8388624 | tf_op jit(solution)/shard_map/all_gather | solution.py:94
  94.7 24.3 %shard_map.95 = bf16[2,2,256,128]{3,2,1,0:T(8,128)(2,1)} custom-call(s32[4]{0:T(128)} %pad_add_fusion.info_ref, bf16[2,2,256,128]{3,2,1,0:T(8,128)(2,1)} %pad_maximum_fusion.2.q_ref, bf16[2,2,8192,128]{3,2,1,0:T(8,128)(2,1)} %all-gather.2.cloned.1.call-done.k_ref.v_ref, bf16[2,2,8192,128]{3,2,1,0:T(8,128)(2,1)} %all-gather.2.cloned.1.call-done.k_ref.v_ref), custom_call_target="tpu_custom_call" | custom-call | flops 2147483648 | bytes 4718592 | tf_op jit(solution)/shard_map/pallas_call | solution.py:59
  119.0 1.0 slice_bitcast_fusion.6
  120.0 1.1 collective-permute-start.1
  121.1 0.0 copy-done.1
  121.1 0.0 copy-done.4
  121.1 0.0 copy-done.7
  121.1 2.3 %fusion.48 = bf16[512,3,128]{0,2,1:T(8,128)(2,1)S(1)} fusion(s32[512]{0:T(512)S(1)} %iota_add_fusion, s32[3,512]{1,0:T(4,128)S(1)} %copy-done.3, bf16[3,512,512]{1,2,0:T(8,128)(2,1)} %get-tuple-element.11, bf16[2,3,512,128]{3,2,1,0:T(8,128)(2,1)S(1)} %copy-done.1, f32[3,512]{1,0:T(4,128)S(1)} %copy-done.4, f32[3,512]{1,0:T(4,128)S(1)} %copy-done.7), kind=kOutput, calls=%fused_computation.36 | convolution fusion | flops 404226048 | bytes 2385920 | tf_op jit(solution)/shard_map/ent,end->ted/dot_general | solution.py:143
  123.5 0.9 copy.21
  124.4 4.9 %collective-permute-done.1 = bf16[2,256,128]{2,1,0:T(8,128)(2,1)S(1)} collective-permute-done((bf16[2,256,128]{2,1,0:T(8,128)(2,1)S(1)}, bf16[2,256,128]{2,1,0:T(8,128)(2,1)S(1)}, u32[]{:S(2)}, u32[]{:S(2)}) %collective-permute-start.1) | collective-permute-done | bytes 131104 | tf_op jit(solution)/shard_map/ppermute | solution.py:100
  129.3 1.0 copy.20
  (4 shorter events, 0.1 us)
Async XLA Ops:
  7.2 75.0 %copy-start = (bf16[512,3,128]{2,0,1:T(8,128)(2,1)S(1)}, bf16[512,3,128]{2,0,1:T(8,128)(2,1)}, u32[]{:S(2)}) copy-start(bf16[512,3,128]{2,0,1:T(8,128)(2,1)} %param.11) | copy-start | bytes 1179652
  7.2 3.8 %copy-start.3 = (s32[3,512]{1,0:T(4,128)S(1)}, s32[3,512]{1,0:T(4,128)}, u32[]{:S(2)}) copy-start(s32[3,512]{1,0:T(4,128)} %param.15) | copy-start | bytes 18436
  7.2 3.8 %copy-start.5 = (bf16[512,3,128]{2,0,1:T(8,128)(2,1)S(1)}, bf16[512,3,128]{2,0,1:T(8,128)(2,1)}, u32[]{:S(2)}) copy-start(bf16[512,3,128]{2,0,1:T(8,128)(2,1)} %param.12) | copy-start | bytes 1179652
  7.2 87.5 %all-gather.2.cloned.1.call-start = ((), (), s32[]{:S(2)}) async-start(), calls=%async_computation.1 | async-start | bytes 8912896 | tf_op jit(solution)/shard_map/all_gather | solution.py:94
  11.0 11.8 %copy-start.2 = (bf16[512,2,128]{2,1,0:T(2,128)(2,1)S(1)}, bf16[512,2,128]{2,1,0:T(2,128)(2,1)}, u32[]{:S(2)}) copy-start(bf16[512,2,128]{2,1,0:T(2,128)(2,1)} %param.8) | copy-start | bytes 786436
  11.7 14.1 %copy-start.6 = (bf16[3,512]{1,0:T(4,128)(2,1)S(1)}, bf16[3,512]{1,0:T(4,128)(2,1)}, u32[]{:S(2)}) copy-start(bf16[3,512]{1,0:T(4,128)(2,1)} %param.14) | copy-start | bytes 9220
  12.8 45.8 %all-to-all-start = ((bf16[2,3,16,32,128]{4,3,1,0,2:T(8,128)(2,1)}), bf16[2,3,16,32,128]{4,3,1,0,2:T(8,128)(2,1)S(1)}, u32[]{:S(2)}, u32[]{:S(2)}) async-start(bf16[2,3,16,32,128]{4,3,1,0,2:T(8,128)(2,1)} %copy.24), calls=%async_computation | async-start | bytes 1572864 | tf_op jit(solution)/shard_map/all_to_all | solution.py:137
  22.9 35.0 %collective-permute-start = (bf16[2,256,128]{2,1,0:T(8,128)(2,1)S(1)}, bf16[2,256,128]{2,1,0:T(8,128)(2,1)S(1)}, u32[]{:S(2)}, u32[]{:S(2)}) collective-permute-start(bf16[2,256,128]{2,1,0:T(8,128)(2,1)S(1)} %get-tuple-element.9), channel_id=1, source_target_pairs={{0,15},{1,14},{2,13},{3,12},{4,11},{5,10},{6,9},{7,8},{8,7},{9,6},... | collective-permute-start | bytes 393224 | tf_op jit(solution)/shard_map/ppermute | solution.py:96
  88.9 32.2 %copy-start.1 = (bf16[2,3,512,128]{3,2,1,0:T(8,128)(2,1)S(1)}, bf16[2,3,512,128]{3,2,1,0:T(8,128)(2,1)}, u32[]{:S(2)}) copy-start(bf16[2,3,512,128]{3,2,1,0:T(8,128)(2,1)} %all_gather.7) | copy-start | bytes 2359300
  88.9 32.2 %copy-start.4 = (f32[3,512]{1,0:T(4,128)S(1)}, f32[3,512]{1,0:T(4,128)}, u32[]{:S(2)}) copy-start(f32[3,512]{1,0:T(4,128)} %fusion.60) | copy-start | bytes 18436
  88.9 32.2 %copy-start.7 = (f32[3,512]{1,0:T(4,128)S(1)}, f32[3,512]{1,0:T(4,128)}, u32[]{:S(2)}) copy-start(f32[3,512]{1,0:T(4,128)} %get-tuple-element.10) | copy-start | bytes 18436
  120.0 9.2 %collective-permute-start.1 = (bf16[2,256,128]{2,1,0:T(8,128)(2,1)S(1)}, bf16[2,256,128]{2,1,0:T(8,128)(2,1)S(1)}, u32[]{:S(2)}, u32[]{:S(2)}) collective-permute-start(bf16[2,256,128]{2,1,0:T(8,128)(2,1)S(1)} %get-tuple-element.7), channel_id=1, source_target_pairs={{0,15},{1,14},{2,13},{3,12},{4,11},{5,10},{6,9},{7,8},{8,7},{9,6},... | collective-permute-start | bytes 393224 | tf_op jit(solution)/shard_map/ppermute | solution.py:100
Sparse Core Ops, SparseCore 0:
  9.9 84.7 all-gather.1

commit v7 on v6

--- a/solution.py
+++ b/solution.py
@@ -9,17 +9,17 @@
 from jax.sharding import PartitionSpec as P
 
 NEGATIVE = -1e30
+KEY_BLOCK = 256
 
 
-def flash_kernel(info_ref, q_ref, k_ref, v_ref, o_ref, m_ref, l_ref, acc_ref, *, scale, block):
+def flash_kernel(info_ref, q_ref, k_ref, v_ref, own_ref, lent_ref, *, scale, block):
     part = pl.program_id(1)
     last = info_ref[part]
     offset = info_ref[2 + part]
-    m_ref[...] = jnp.full(m_ref.shape, NEGATIVE, jnp.float32)
-    l_ref[...] = jnp.zeros(l_ref.shape, jnp.float32)
-    acc_ref[...] = jnp.zeros(acc_ref.shape, jnp.float32)
+    rows_n = q_ref.shape[2]
 
-    def update(j, masked):
+    def update(j, carry, masked):
+        m_prev, l_prev, acc = carry
         first = pl.multiple_of(j * block, block)
         scores = lax.dot_general(
             q_ref[0, 0], k_ref[0, pl.ds(first, block), :], (((1,), (1,)), ((), ())),
@@ -29,36 +29,42 @@
             rows = lax.broadcasted_iota(jnp.int32, scores.shape, 0) + offset
             cols = lax.broadcasted_iota(jnp.int32, scores.shape, 1)
             scores = jnp.where(cols <= rows, scores, NEGATIVE)
-        m_prev = m_ref[:, :1]
         m_new = jnp.maximum(m_prev, jnp.max(scores, axis=1, keepdims=True))
         shrink = jnp.exp(m_prev - m_new)
         weights = jnp.exp(scores - m_new)
-        l_new = l_ref[:, :1] * shrink + jnp.sum(weights, axis=1, keepdims=True)
+        l_new = l_prev * shrink + jnp.sum(weights, axis=1, keepdims=True)
         moved = jnp.dot(
             weights.astype(jnp.bfloat16), v_ref[0, pl.ds(first, block), :],
             preferred_element_type=jnp.float32,
         )
-        acc_ref[...] = acc_ref[...] * shrink + moved
-        m_ref[...] = jnp.broadcast_to(m_new, m_ref.shape)
-        l_ref[...] = jnp.broadcast_to(l_new, l_ref.shape)
+        return m_new, l_new, acc * shrink + moved
 
-    def body(j, carry):
-        update(j, False)
-        return carry
+    init = (
+        jnp.full((rows_n, 1), NEGATIVE, jnp.float32),
+        jnp.zeros((rows_n, 1), jnp.float32),
+        jnp.zeros((rows_n, q_ref.shape[3]), jnp.float32),
+    )
+    carry = lax.fori_loop(0, last, lambda j, c: update(j, c, False), init)
+    m_f, l_f, acc_f = update(last, carry, True)
+    result = (acc_f / l_f).astype(own_ref.dtype)
 
-    lax.fori_loop(0, last, body, 0)
-    update(last, True)
-    o_ref[0, 0] = (acc_ref[...] / l_ref[:, :1]).astype(o_ref.dtype)
+    @pl.when(part == 0)
+    def _():
+        own_ref[0] = result
+
+    @pl.when(part == 1)
+    def _():
+        lent_ref[0] = result
 
 
 def dense_flash(info, queries, stacked):
     parts, heads, rows, width = queries.shape
     length = stacked.shape[2]
-    block = 512
+    block = KEY_BLOCK
     scale = 1.0 / math.sqrt(width)
     return pl.pallas_call(
         functools.partial(flash_kernel, scale=scale, block=block),
-        out_shape=jax.ShapeDtypeStruct((parts, heads, rows, width), jnp.bfloat16),
+        out_shape=[jax.ShapeDtypeStruct((heads, rows, width), jnp.bfloat16)] * 2,
         grid_spec=pltpu.PrefetchScalarGridSpec(
             num_scalar_prefetch=1,
             grid=(heads, parts),
@@ -67,12 +73,7 @@
                 pl.BlockSpec((None, 1, length, width), lambda h, p, c: (0, h, 0, 0)),
                 pl.BlockSpec((None, 1, length, width), lambda h, p, c: (1, h, 0, 0)),
             ],
-            out_specs=pl.BlockSpec((1, 1, rows, width), lambda h, p, c: (p, h, 0, 0)),
-            scratch_shapes=[
-                pltpu.VMEM((rows, 128), jnp.float32),
-                pltpu.VMEM((rows, 128), jnp.float32),
-                pltpu.VMEM((rows, width), jnp.float32),
-            ],
+            out_specs=[pl.BlockSpec((1, rows, width), lambda h, p, c: (h, 0, 0))] * 2,
         ),
         compiler_params=pltpu.CompilerParams(dimension_semantics=("arbitrary", "arbitrary")),
         cost_estimate=pl.CostEstimate(
@@ -95,10 +96,12 @@
     rows_first = jnp.swapaxes(queries, 0, 1)
     lent = lax.ppermute(rows_first[:, half:], "seq", swap)
     both = jnp.stack([rows_first[:, :half], lent], axis=0)
-    info = jnp.stack([me, partner, jnp.int32(0), jnp.int32(half)])
-    out = dense_flash(info, both, gathered)
-    returned = lax.ppermute(out[1], "seq", swap)
-    mine = jnp.concatenate([out[0], returned], axis=1)
+    ends = jnp.stack([me * tok_rows, partner * tok_rows + half])
+    lasts = ends // KEY_BLOCK
+    info = jnp.concatenate([lasts, ends - lasts * KEY_BLOCK]).astype(jnp.int32)
+    ours, theirs = dense_flash(info, both, gathered)
+    returned = lax.ppermute(theirs, "seq", swap)
+    mine = jnp.concatenate([ours, returned], axis=1)
     return jnp.swapaxes(mine, 0, 1)
 
 

time: 138 us -> 145 us (1.051)
  Pallas kernels: 24.3 us -> 32.8 us
  waiting for transfers between devices: 40 us -> 42.3 us
    pallas_call x1, Pallas kernels: 24.3 us -> 32.8 us  [dense_flash(): pl.pallas_call(functools.partial(flash_kernel, scale=scale, block=block),...]
    ppermute x1, waiting for transfers between devices: 4.87 us -> 6.97 us  [dense_heads(): returned = lax.ppermute(theirs, 'seq', swap)]
  transfers between devices with their start and end apart: 4 -> 4, of which waited for: 3 -> 3; matrix products, arithmetic and copies ran while one was open for 12% -> 11% of each run, Pallas kernels for 0% -> 0%
where the time goes in v7:
time: 145 us
  waiting for transfers between devices  42.3 us (29%)
  Pallas kernels  32.8 us (23%)
  blocking collectives  23.2 us (16%)
  between operations  14.2 us (10%)
  starting transfers between devices  13.5 us (9%)
  other arithmetic  8.56 us (6%)
  matrix products  5.96 us (4%)
  local copies, waits for them, and re-layouts  4.24 us (3%)
    pallas_call x1, Pallas kernels, dense_flash(): pl.pallas_call(functools.partial(flash_kernel, scale=scale, block=block),...  32.8 us
    ppermute x1, waiting for transfers between devices, dense_heads(): lent = lax.ppermute(rows_first[:, half:], 'seq', swap)  29.3 us
    all_gather x1, blocking collectives, sparse_heads(): picked_kv = lax.all_gather(own, 'seq', axis=2, tiled=True)  23.2 us
    all_to_all x1, starting transfers between devices, sparse_heads(): arrived = lax.all_to_all(pieces, 'seq', 2, 2, tiled=True)  9.98 us
    ppermute x1, waiting for transfers between devices, dense_heads(): returned = lax.ppermute(theirs, 'seq', swap)  6.97 us
    all_gather x1, waiting for transfers between devices, dense_heads(): gathered = lax.all_gather(stacked, 'seq', axis=2, tiled=True)  6 us
    sub x1, other arithmetic, attend_ranked(): weights = jnp.where(visible, jnp.exp(scores - leading), 0.0)  4.66 us
    ppermute x1, starting transfers between devices, dense_heads(): lent = lax.ppermute(rows_first[:, half:], 'seq', swap)  2.93 us
  transfers between devices with their start and end apart: 4, of which 3 were waited for; matrix products, arithmetic and copies ran while one was open for 11% of the time, Pallas kernels for 0%

profile of v7, /device:TPU:1, one launch (start us, length us, event | category | flops | bytes accessed | tf_op | source)
XLA Modules:
  0.0 144.8 jit_solution(9006153153440207752)
XLA Ops:
  7.2 0.0 copy-start
  7.2 0.0 copy-start.4
  7.2 0.0 copy-start.6
  7.2 0.0 all-gather.2.cloned.1.call-start
  7.2 1.2 copy_bitcast_fusion
  8.4 0.9 pad_maximum_fusion.1
  9.3 0.0 all-gather.2.cloned.1.call-update
  9.3 1.7 %fusion.42 = bf16[3,512,128]{2,1,0:T(8,128)(2,1)S(1)} fusion(bf16[512,3,128]{2,0,1:T(8,128)(2,1)} %param.13, s32[512]{0:T(512)S(1)} %iota_add_fusion, s32[3,512]{1,0:T(4,128)} %param.15), kind=kOutput, calls=%fused_computation.34 | convolution fusion | flops 202309632 | bytes 794624 | tf_op jit(solution)/shard_map/ent,ted->end/dot_general | solution.py:132
  11.0 0.0 copy-done.4
  11.0 0.0 copy-done.6
  11.0 0.0 copy-start.2
  11.0 0.6 fusion.39
  11.7 0.0 copy-start.7
  11.7 0.1 pad_maximum_fusion
  11.8 1.1 copy.24
  12.8 10.0 %all-to-all-start = ((bf16[2,3,16,32,128]{4,3,1,0,2:T(8,128)(2,1)}), bf16[2,3,16,32,128]{4,3,1,0,2:T(8,128)(2,1)S(1)}, u32[]{:S(2)}, u32[]{:S(2)}) async-start(bf16[2,3,16,32,128]{4,3,1,0,2:T(8,128)(2,1)} %copy.24), calls=%async_computation | async-start | bytes 1572864 | tf_op jit(solution)/shard_map/all_to_all | solution.py:140
  22.8 0.0 copy-done.2
  22.9 2.9 %collective-permute-start = (bf16[2,256,128]{2,1,0:T(8,128)(2,1)S(1)}, bf16[2,256,128]{2,1,0:T(8,128)(2,1)S(1)}, u32[]{:S(2)}, u32[]{:S(2)}) collective-permute-start(bf16[2,256,128]{2,1,0:T(8,128)(2,1)S(1)} %get-tuple-element.13), channel_id=1, source_target_pairs={{0,15},{1,14},{2,13},{3,12},{4,11},{5,10},{6,9},{7,8},{8,7},{9,6},... | collective-permute-start | bytes 393224 | tf_op jit(solution)/shard_map/ppermute | solution.py:97
  25.8 0.1 multiply_subtract_fusion
  25.9 0.0 copy-done.7
  25.9 0.6 fusion.3
  26.6 0.6 fusion.60
  27.2 0.6 pad_add_fusion.1.info_ref
  27.8 0.8 iota_compare_fusion
  28.6 29.3 %collective-permute-done = bf16[2,256,128]{2,1,0:T(8,128)(2,1)S(1)} collective-permute-done((bf16[2,256,128]{2,1,0:T(8,128)(2,1)S(1)}, bf16[2,256,128]{2,1,0:T(8,128)(2,1)S(1)}, u32[]{:S(2)}, u32[]{:S(2)}) %collective-permute-start) | collective-permute-done | bytes 131104 | tf_op jit(solution)/shard_map/ppermute | solution.py:97
  57.9 0.7 pad_maximum_fusion.2.q_ref
  58.6 0.0 all-to-all-done
  58.6 0.1 reduce_sum.21
  58.8 23.2 %all_gather.7 = bf16[2,3,512,128]{3,2,1,0:T(8,128)(2,1)} all-gather(bf16[2,3,32,128]{3,2,1,0:T(8,128)(2,1)S(1)} %reduce_sum.21), channel_id=1, replica_groups=mesh['dp'=4,'head'=4,'seq'=16] {'seq'}, dimensions={2}, use_global_device_ids=true | all-gather | bytes 835584 | tf_op jit(solution)/shard_map/all_gather | solution.py:142
  82.0 0.0 copy-done
  82.0 2.1 %fusion.52 = f32[3,512,512]{1,2,0:T(8,128)S(1)} fusion(bf16[512,3,128]{2,0,1:T(8,128)(2,1)S(1)} %copy-done, s32[512]{0:T(512)S(1)} %iota_add_fusion, s32[3,512]{1,0:T(4,128)S(1)} %copy-done.4, bf16[2,3,512,128]{3,2,1,0:T(8,128)(2,1)} %all_gather.7), kind=kOutput, calls=%fused_computation.37 | convolution fusion | flops 403636224 | bytes 3940352 | tf_op jit(solution)/shard_map/erd,ekd->erk/dot_general | solution.py:112
  84.1 4.7 %fusion.64 = (f32[3,512]{1,0:T(4,128)}, bf16[3,512,512]{1,2,0:T(8,128)(2,1)}) fusion(f32[3,512,512]{1,2,0:T(8,128)S(1)} %fusion.52, pred[512,512]{0,1:T(8,128)(4,1)} %iota_compare_fusion), kind=kOutput, calls=%fused_computation.66 | output fusion | flops 6291967 | bytes 4986880 | tf_op jit(solution)/shard_map/sub | solution.py:116
  88.7 0.0 copy-start.1
  88.7 0.0 copy-start.5
  88.7 0.0 copy-start.8
  88.7 6.0 %all-gather.2.cloned.1.call-done.k_ref.v_ref = bf16[2,2,8192,128]{3,2,1,0:T(8,128)(2,1)} async-done(((bf16[2,2,512,128]{3,2,1,0:T(8,128)(2,1)}), bf16[2,2,8192,128]{3,2,1,0:T(8,128)(2,1)}) %all-gather.2.cloned.1.call-update) | async-done | bytes 8388624 | tf_op jit(solution)/shard_map/all_gather | solution.py:95
  94.7 32.8 %shard_map.95 = (bf16[2,256,128]{2,1,0:T(8,128)(2,1)}, bf16[2,256,128]{2,1,0:T(8,128)(2,1)}) custom-call(s32[4]{0:T(128)} %pad_add_fusion.1.info_ref, bf16[2,2,256,128]{3,2,1,0:T(8,128)(2,1)} %pad_maximum_fusion.2.q_ref, bf16[2,2,8192,128]{3,2,1,0:T(8,128)(2,1)} %all-gather.2.cloned.1.call-done.k_ref.v_ref, ...), custom_call_target="tpu_custom_call" | custom-call | flops 2147483648 | bytes 4718592 | tf_op jit(solution)/shard_map/pallas_call | solution.py:65
  127.6 0.5 collective-permute-start.1
  128.1 0.0 copy-done.1
  128.1 0.0 copy-done.5
  128.1 0.0 copy-done.8
  128.1 0.0 copy-done.9
  128.1 0.0 copy-start.3
  128.1 0.9 fusion.48
  129.0 0.9 copy.21
  130.0 7.0 %collective-permute-done.1 = bf16[2,256,128]{2,1,0:T(8,128)(2,1)S(1)} collective-permute-done((bf16[2,256,128]{2,1,0:T(8,128)(2,1)}, bf16[2,256,128]{2,1,0:T(8,128)(2,1)S(1)}, u32[]{:S(2)}, u32[]{:S(2)}) %collective-permute-start.1) | collective-permute-done | bytes 131104 | tf_op jit(solution)/shard_map/ppermute | solution.py:103
  136.9 0.0 copy-done.3
  136.9 1.0 copy.20
  (5 shorter events, 0.1 us)
Async XLA Ops:
  7.2 74.8 %copy-start = (bf16[512,3,128]{2,0,1:T(8,128)(2,1)S(1)}, bf16[512,3,128]{2,0,1:T(8,128)(2,1)}, u32[]{:S(2)}) copy-start(bf16[512,3,128]{2,0,1:T(8,128)(2,1)} %param.11) | copy-start | bytes 1179652
  7.2 3.8 %copy-start.4 = (s32[3,512]{1,0:T(4,128)S(1)}, s32[3,512]{1,0:T(4,128)}, u32[]{:S(2)}) copy-start(s32[3,512]{1,0:T(4,128)} %param.15) | copy-start | bytes 18436
  7.2 3.8 %copy-start.6 = (bf16[512,3,128]{2,0,1:T(8,128)(2,1)S(1)}, bf16[512,3,128]{2,0,1:T(8,128)(2,1)}, u32[]{:S(2)}) copy-start(bf16[512,3,128]{2,0,1:T(8,128)(2,1)} %param.12) | copy-start | bytes 1179652
  7.2 87.5 %all-gather.2.cloned.1.call-start = ((), (), s32[]{:S(2)}) async-start(), calls=%async_computation.1 | async-start | bytes 8912896 | tf_op jit(solution)/shard_map/all_gather | solution.py:95
  11.0 11.8 %copy-start.2 = (bf16[512,2,128]{2,1,0:T(2,128)(2,1)S(1)}, bf16[512,2,128]{2,1,0:T(2,128)(2,1)}, u32[]{:S(2)}) copy-start(bf16[512,2,128]{2,1,0:T(2,128)(2,1)} %param.8) | copy-start | bytes 786436
  11.7 14.2 %copy-start.7 = (bf16[3,512]{1,0:T(4,128)(2,1)S(1)}, bf16[3,512]{1,0:T(4,128)(2,1)}, u32[]{:S(2)}) copy-start(bf16[3,512]{1,0:T(4,128)(2,1)} %param.14) | copy-start | bytes 9220
  12.8 45.8 %all-to-all-start = ((bf16[2,3,16,32,128]{4,3,1,0,2:T(8,128)(2,1)}), bf16[2,3,16,32,128]{4,3,1,0,2:T(8,128)(2,1)S(1)}, u32[]{:S(2)}, u32[]{:S(2)}) async-start(bf16[2,3,16,32,128]{4,3,1,0,2:T(8,128)(2,1)} %copy.24), calls=%async_computation | async-start | bytes 1572864 | tf_op jit(solution)/shard_map/all_to_all | solution.py:140
  22.9 35.0 %collective-permute-start = (bf16[2,256,128]{2,1,0:T(8,128)(2,1)S(1)}, bf16[2,256,128]{2,1,0:T(8,128)(2,1)S(1)}, u32[]{:S(2)}, u32[]{:S(2)}) collective-permute-start(bf16[2,256,128]{2,1,0:T(8,128)(2,1)S(1)} %get-tuple-element.13), channel_id=1, source_target_pairs={{0,15},{1,14},{2,13},{3,12},{4,11},{5,10},{6,9},{7,8},{8,7},{9,6},... | collective-permute-start | bytes 393224 | tf_op jit(solution)/shard_map/ppermute | solution.py:97
  88.7 39.4 %copy-start.1 = (bf16[2,3,512,128]{3,2,1,0:T(8,128)(2,1)S(1)}, bf16[2,3,512,128]{3,2,1,0:T(8,128)(2,1)}, u32[]{:S(2)}) copy-start(bf16[2,3,512,128]{3,2,1,0:T(8,128)(2,1)} %all_gather.7) | copy-start | bytes 2359300
  88.7 39.4 %copy-start.5 = (f32[3,512]{1,0:T(4,128)S(1)}, f32[3,512]{1,0:T(4,128)}, u32[]{:S(2)}) copy-start(f32[3,512]{1,0:T(4,128)} %fusion.60) | copy-start | bytes 18436
  88.7 39.4 %copy-start.8 = (bf16[3,512,512]{1,2,0:T(8,128)(2,1)S(1)}, bf16[3,512,512]{1,2,0:T(8,128)(2,1)}, u32[]{:S(2)}) copy-start(bf16[3,512,512]{1,2,0:T(8,128)(2,1)} %get-tuple-element.15) | copy-start | bytes 4718596
  88.7 39.4 %copy-start.9 = (f32[3,512]{1,0:T(4,128)S(1)}, f32[3,512]{1,0:T(4,128)}, u32[]{:S(2)}) copy-start(f32[3,512]{1,0:T(4,128)} %get-tuple-element.14) | copy-start | bytes 18436
  127.6 9.4 %collective-permute-start.1 = (bf16[2,256,128]{2,1,0:T(8,128)(2,1)}, bf16[2,256,128]{2,1,0:T(8,128)(2,1)S(1)}, u32[]{:S(2)}, u32[]{:S(2)}) collective-permute-start(bf16[2,256,128]{2,1,0:T(8,128)(2,1)} %get-tuple-element.5), channel_id=1, source_target_pairs={{0,15},{1,14},{2,13},{3,12},{4,11},{5,10},{6,9},{7,8},{8,7},{9,6},... | collective-permute-start | bytes 393224 | tf_op jit(solution)/shard_map/ppermute | solution.py:103
  128.1 8.8 %copy-start.3 = (bf16[2,256,128]{2,1,0:T(8,128)(2,1)S(1)}, bf16[2,256,128]{2,1,0:T(8,128)(2,1)}, u32[]{:S(2)}) copy-start(bf16[2,256,128]{2,1,0:T(8,128)(2,1)} %get-tuple-element.4) | copy-start | bytes 393220
Sparse Core Ops, SparseCore 0:
  9.9 84.7 all-gather.1

commit v8 on v7

--- a/solution.py
+++ b/solution.py
@@ -9,7 +9,7 @@
 from jax.sharding import PartitionSpec as P
 
 NEGATIVE = -1e30
-KEY_BLOCK = 256
+KEY_BLOCK = 512
 
 
 def flash_kernel(info_ref, q_ref, k_ref, v_ref, own_ref, lent_ref, *, scale, block):

time: 145 us -> 133 us (0.917)
  Pallas kernels: 32.8 us -> 20.4 us
    pallas_call x1, Pallas kernels: 32.8 us -> 20.4 us  [dense_flash(): pl.pallas_call(functools.partial(flash_kernel, scale=scale, block=block),...]
  transfers between devices with their start and end apart: 4 -> 4, of which waited for: 3 -> 3; matrix products, arithmetic and copies ran while one was open for 11% -> 12% of each run, Pallas kernels for 0% -> 0%
where the time goes in v8:
time: 133 us; the launch traced here: 132 us
  waiting for transfers between devices  41.5 us (31%)
  blocking collectives  23.2 us (17%)
  Pallas kernels  20.4 us (15%)
  starting transfers between devices  14.3 us (11%)
  between operations  14.2 us (11%)
  other arithmetic  8.56 us (6%)
  matrix products  5.96 us (4%)
  local copies, waits for them, and re-layouts  4.24 us (3%)
    ppermute x1, waiting for transfers between devices, dense_heads(): lent = lax.ppermute(rows_first[:, half:], 'seq', swap)  29.3 us
    all_gather x1, blocking collectives, sparse_heads(): picked_kv = lax.all_gather(own, 'seq', axis=2, tiled=True)  23.2 us
    pallas_call x1, Pallas kernels, dense_flash(): pl.pallas_call(functools.partial(flash_kernel, scale=scale, block=block),...  20.4 us
    all_to_all x1, starting transfers between devices, sparse_heads(): arrived = lax.all_to_all(pieces, 'seq', 2, 2, tiled=True)  9.98 us
    ppermute x1, waiting for transfers between devices, dense_heads(): returned = lax.ppermute(theirs, 'seq', swap)  6.15 us
    all_gather x1, waiting for transfers between devices, dense_heads(): gathered = lax.all_gather(stacked, 'seq', axis=2, tiled=True)  6 us
    sub x1, other arithmetic, attend_ranked(): weights = jnp.where(visible, jnp.exp(scores - leading), 0.0)  4.66 us
    ppermute x1, starting transfers between devices, dense_heads(): lent = lax.ppermute(rows_first[:, half:], 'seq', swap)  2.93 us
  transfers between devices with their start and end apart: 4, of which 3 were waited for; matrix products, arithmetic and copies ran while one was open for 12% of the time, Pallas kernels for 0%

profile of v8, /device:TPU:1, one launch (start us, length us, event | category | flops | bytes accessed | tf_op | source)
XLA Modules:
  0.0 132.4 jit_solution(4339240947713081302)
XLA Ops:
  7.2 0.0 copy-start
  7.2 0.0 copy-start.4
  7.2 0.0 copy-start.6
  7.2 0.0 all-gather.2.cloned.1.call-start
  7.2 1.2 copy_bitcast_fusion
  8.4 0.9 pad_maximum_fusion.1
  9.3 0.0 all-gather.2.cloned.1.call-update
  9.3 1.7 %fusion.42 = bf16[3,512,128]{2,1,0:T(8,128)(2,1)S(1)} fusion(bf16[512,3,128]{2,0,1:T(8,128)(2,1)} %param.13, s32[512]{0:T(512)S(1)} %iota_add_fusion, s32[3,512]{1,0:T(4,128)} %param.15), kind=kOutput, calls=%fused_computation.34 | convolution fusion | flops 202309632 | bytes 794624 | tf_op jit(solution)/shard_map/ent,ted->end/dot_general | solution.py:132
  11.0 0.0 copy-done.4
  11.0 0.0 copy-done.6
  11.0 0.0 copy-start.2
  11.0 0.6 fusion.39
  11.7 0.0 copy-start.7
  11.7 0.1 pad_maximum_fusion
  11.8 1.1 copy.24
  12.8 10.0 %all-to-all-start = ((bf16[2,3,16,32,128]{4,3,1,0,2:T(8,128)(2,1)}), bf16[2,3,16,32,128]{4,3,1,0,2:T(8,128)(2,1)S(1)}, u32[]{:S(2)}, u32[]{:S(2)}) async-start(bf16[2,3,16,32,128]{4,3,1,0,2:T(8,128)(2,1)} %copy.24), calls=%async_computation | async-start | bytes 1572864 | tf_op jit(solution)/shard_map/all_to_all | solution.py:140
  22.8 0.0 copy-done.2
  22.9 2.9 %collective-permute-start = (bf16[2,256,128]{2,1,0:T(8,128)(2,1)S(1)}, bf16[2,256,128]{2,1,0:T(8,128)(2,1)S(1)}, u32[]{:S(2)}, u32[]{:S(2)}) collective-permute-start(bf16[2,256,128]{2,1,0:T(8,128)(2,1)S(1)} %get-tuple-element.13), channel_id=1, source_target_pairs={{0,15},{1,14},{2,13},{3,12},{4,11},{5,10},{6,9},{7,8},{8,7},{9,6},... | collective-permute-start | bytes 393224 | tf_op jit(solution)/shard_map/ppermute | solution.py:97
  25.8 0.1 multiply_subtract_fusion
  25.9 0.0 copy-done.7
  25.9 0.6 fusion.3
  26.6 0.6 fusion.60
  27.2 0.6 pad_add_fusion.1.info_ref
  27.8 0.8 iota_compare_fusion
  28.6 29.3 %collective-permute-done = bf16[2,256,128]{2,1,0:T(8,128)(2,1)S(1)} collective-permute-done((bf16[2,256,128]{2,1,0:T(8,128)(2,1)S(1)}, bf16[2,256,128]{2,1,0:T(8,128)(2,1)S(1)}, u32[]{:S(2)}, u32[]{:S(2)}) %collective-permute-start) | collective-permute-done | bytes 131104 | tf_op jit(solution)/shard_map/ppermute | solution.py:97
  57.9 0.7 pad_maximum_fusion.2.q_ref
  58.6 0.0 all-to-all-done
  58.6 0.1 reduce_sum.21
  58.8 23.2 %all_gather.7 = bf16[2,3,512,128]{3,2,1,0:T(8,128)(2,1)} all-gather(bf16[2,3,32,128]{3,2,1,0:T(8,128)(2,1)S(1)} %reduce_sum.21), channel_id=1, replica_groups=mesh['dp'=4,'head'=4,'seq'=16] {'seq'}, dimensions={2}, use_global_device_ids=true | all-gather | bytes 835584 | tf_op jit(solution)/shard_map/all_gather | solution.py:142
  82.0 0.0 copy-done
  82.0 2.1 %fusion.52 = f32[3,512,512]{1,2,0:T(8,128)S(1)} fusion(bf16[512,3,128]{2,0,1:T(8,128)(2,1)S(1)} %copy-done, s32[512]{0:T(512)S(1)} %iota_add_fusion, s32[3,512]{1,0:T(4,128)S(1)} %copy-done.4, bf16[2,3,512,128]{3,2,1,0:T(8,128)(2,1)} %all_gather.7), kind=kOutput, calls=%fused_computation.37 | convolution fusion | flops 403636224 | bytes 3940352 | tf_op jit(solution)/shard_map/erd,ekd->erk/dot_general | solution.py:112
  84.1 4.7 %fusion.64 = (f32[3,512]{1,0:T(4,128)}, bf16[3,512,512]{1,2,0:T(8,128)(2,1)}) fusion(f32[3,512,512]{1,2,0:T(8,128)S(1)} %fusion.52, pred[512,512]{0,1:T(8,128)(4,1)} %iota_compare_fusion), kind=kOutput, calls=%fused_computation.66 | output fusion | flops 6291967 | bytes 4986880 | tf_op jit(solution)/shard_map/sub | solution.py:116
  88.7 0.0 copy-start.1
  88.7 0.0 copy-start.5
  88.7 0.0 copy-start.8
  88.7 6.0 %all-gather.2.cloned.1.call-done.k_ref.v_ref = bf16[2,2,8192,128]{3,2,1,0:T(8,128)(2,1)} async-done(((bf16[2,2,512,128]{3,2,1,0:T(8,128)(2,1)}), bf16[2,2,8192,128]{3,2,1,0:T(8,128)(2,1)}) %all-gather.2.cloned.1.call-update) | async-done | bytes 8388624 | tf_op jit(solution)/shard_map/all_gather | solution.py:95
  94.7 20.4 %shard_map.95 = (bf16[2,256,128]{2,1,0:T(8,128)(2,1)}, bf16[2,256,128]{2,1,0:T(8,128)(2,1)}) custom-call(s32[4]{0:T(128)} %pad_add_fusion.1.info_ref, bf16[2,2,256,128]{3,2,1,0:T(8,128)(2,1)} %pad_maximum_fusion.2.q_ref, bf16[2,2,8192,128]{3,2,1,0:T(8,128)(2,1)} %all-gather.2.cloned.1.call-done.k_ref.v_ref, ...), custom_call_target="tpu_custom_call" | custom-call | flops 2147483648 | bytes 4718592 | tf_op jit(solution)/shard_map/pallas_call | solution.py:65
  115.1 1.3 %collective-permute-start.1 = (bf16[2,256,128]{2,1,0:T(8,128)(2,1)}, bf16[2,256,128]{2,1,0:T(8,128)(2,1)S(1)}, u32[]{:S(2)}, u32[]{:S(2)}) collective-permute-start(bf16[2,256,128]{2,1,0:T(8,128)(2,1)} %get-tuple-element.5), channel_id=1, source_target_pairs={{0,15},{1,14},{2,13},{3,12},{4,11},{5,10},{6,9},{7,8},{8,7},{9,6},... | collective-permute-start | bytes 393224 | tf_op jit(solution)/shard_map/ppermute | solution.py:103
  116.5 0.0 copy-done.1
  116.5 0.0 copy-done.5
  116.5 0.0 copy-done.8
  116.5 0.0 copy-done.9
  116.5 0.0 copy-start.3
  116.5 0.9 fusion.48
  117.4 0.9 copy.21
  118.4 6.2 %collective-permute-done.1 = bf16[2,256,128]{2,1,0:T(8,128)(2,1)S(1)} collective-permute-done((bf16[2,256,128]{2,1,0:T(8,128)(2,1)}, bf16[2,256,128]{2,1,0:T(8,128)(2,1)S(1)}, u32[]{:S(2)}, u32[]{:S(2)}) %collective-permute-start.1) | collective-permute-done | bytes 131104 | tf_op jit(solution)/shard_map/ppermute | solution.py:103
  124.5 0.0 copy-done.3
  124.5 1.0 copy.20
  (5 shorter events, 0.1 us)
Async XLA Ops:
  7.2 74.8 %copy-start = (bf16[512,3,128]{2,0,1:T(8,128)(2,1)S(1)}, bf16[512,3,128]{2,0,1:T(8,128)(2,1)}, u32[]{:S(2)}) copy-start(bf16[512,3,128]{2,0,1:T(8,128)(2,1)} %param.11) | copy-start | bytes 1179652
  7.2 3.8 %copy-start.4 = (s32[3,512]{1,0:T(4,128)S(1)}, s32[3,512]{1,0:T(4,128)}, u32[]{:S(2)}) copy-start(s32[3,512]{1,0:T(4,128)} %param.15) | copy-start | bytes 18436
  7.2 3.8 %copy-start.6 = (bf16[512,3,128]{2,0,1:T(8,128)(2,1)S(1)}, bf16[512,3,128]{2,0,1:T(8,128)(2,1)}, u32[]{:S(2)}) copy-start(bf16[512,3,128]{2,0,1:T(8,128)(2,1)} %param.12) | copy-start | bytes 1179652
  7.2 87.5 %all-gather.2.cloned.1.call-start = ((), (), s32[]{:S(2)}) async-start(), calls=%async_computation.1 | async-start | bytes 8912896 | tf_op jit(solution)/shard_map/all_gather | solution.py:95
  11.0 11.8 %copy-start.2 = (bf16[512,2,128]{2,1,0:T(2,128)(2,1)S(1)}, bf16[512,2,128]{2,1,0:T(2,128)(2,1)}, u32[]{:S(2)}) copy-start(bf16[512,2,128]{2,1,0:T(2,128)(2,1)} %param.8) | copy-start | bytes 786436
  11.7 14.2 %copy-start.7 = (bf16[3,512]{1,0:T(4,128)(2,1)S(1)}, bf16[3,512]{1,0:T(4,128)(2,1)}, u32[]{:S(2)}) copy-start(bf16[3,512]{1,0:T(4,128)(2,1)} %param.14) | copy-start | bytes 9220
  12.8 45.8 %all-to-all-start = ((bf16[2,3,16,32,128]{4,3,1,0,2:T(8,128)(2,1)}), bf16[2,3,16,32,128]{4,3,1,0,2:T(8,128)(2,1)S(1)}, u32[]{:S(2)}, u32[]{:S(2)}) async-start(bf16[2,3,16,32,128]{4,3,1,0,2:T(8,128)(2,1)} %copy.24), calls=%async_computation | async-start | bytes 1572864 | tf_op jit(solution)/shard_map/all_to_all | solution.py:140
  22.9 35.0 %collective-permute-start = (bf16[2,256,128]{2,1,0:T(8,128)(2,1)S(1)}, bf16[2,256,128]{2,1,0:T(8,128)(2,1)S(1)}, u32[]{:S(2)}, u32[]{:S(2)}) collective-permute-start(bf16[2,256,128]{2,1,0:T(8,128)(2,1)S(1)} %get-tuple-element.13), channel_id=1, source_target_pairs={{0,15},{1,14},{2,13},{3,12},{4,11},{5,10},{6,9},{7,8},{8,7},{9,6},... | collective-permute-start | bytes 393224 | tf_op jit(solution)/shard_map/ppermute | solution.py:97
  88.7 27.8 %copy-start.1 = (bf16[2,3,512,128]{3,2,1,0:T(8,128)(2,1)S(1)}, bf16[2,3,512,128]{3,2,1,0:T(8,128)(2,1)}, u32[]{:S(2)}) copy-start(bf16[2,3,512,128]{3,2,1,0:T(8,128)(2,1)} %all_gather.7) | copy-start | bytes 2359300
  88.7 27.8 %copy-start.5 = (f32[3,512]{1,0:T(4,128)S(1)}, f32[3,512]{1,0:T(4,128)}, u32[]{:S(2)}) copy-start(f32[3,512]{1,0:T(4,128)} %fusion.60) | copy-start | bytes 18436
  88.7 27.8 %copy-start.8 = (bf16[3,512,512]{1,2,0:T(8,128)(2,1)S(1)}, bf16[3,512,512]{1,2,0:T(8,128)(2,1)}, u32[]{:S(2)}) copy-start(bf16[3,512,512]{1,2,0:T(8,128)(2,1)} %get-tuple-element.15) | copy-start | bytes 4718596
  88.7 27.8 %copy-start.9 = (f32[3,512]{1,0:T(4,128)S(1)}, f32[3,512]{1,0:T(4,128)}, u32[]{:S(2)}) copy-start(f32[3,512]{1,0:T(4,128)} %get-tuple-element.14) | copy-start | bytes 18436
  115.1 9.4 %collective-permute-start.1 = (bf16[2,256,128]{2,1,0:T(8,128)(2,1)}, bf16[2,256,128]{2,1,0:T(8,128)(2,1)S(1)}, u32[]{:S(2)}, u32[]{:S(2)}) collective-permute-start(bf16[2,256,128]{2,1,0:T(8,128)(2,1)} %get-tuple-element.5), channel_id=1, source_target_pairs={{0,15},{1,14},{2,13},{3,12},{4,11},{5,10},{6,9},{7,8},{8,7},{9,6},... | collective-permute-start | bytes 393224 | tf_op jit(solution)/shard_map/ppermute | solution.py:103
  116.5 8.0 %copy-start.3 = (bf16[2,256,128]{2,1,0:T(8,128)(2,1)S(1)}, bf16[2,256,128]{2,1,0:T(8,128)(2,1)}, u32[]{:S(2)}) copy-start(bf16[2,256,128]{2,1,0:T(8,128)(2,1)} %get-tuple-element.4) | copy-start | bytes 393220
Sparse Core Ops, SparseCore 0:
  9.9 84.7 all-gather.1

commit v9 on v8

--- a/solution.py
+++ b/solution.py
@@ -139,7 +139,8 @@
     pieces = local_kv.reshape(kinds, heads_, count, chosen // count, width_)
     arrived = lax.all_to_all(pieces, "seq", 2, 2, tiled=True)
     own = jnp.sum(arrived.astype(jnp.float32), axis=2).astype(jnp.bfloat16)
-    picked_kv = lax.all_gather(own, "seq", axis=2, tiled=True)
+    spread = jnp.broadcast_to(own[:, :, None], (kinds, heads_, count) + own.shape[2:])
+    picked_kv = lax.all_to_all(spread, "seq", 2, 2, tiled=True).reshape(kinds, heads_, chosen, width_)
     picked_q = pick(queries)
     gate_rows = jnp.einsum("ent,et->en", one_hot, gate_logit, preferred_element_type=jnp.float32)
     results = attend_ranked(picked_q, picked_kv[0], picked_kv[1], gate_rows)

time: 133 us -> 144 us (1.083)
  blocking collectives: 23.2 us -> 39.5 us
  starting transfers between devices: 14.3 us -> 7.86 us
  local copies, waits for them, and re-layouts: 4.24 us -> 6.05 us
    all_to_all x0 -> x1, blocking collectives: none -> 39.5 us  [sparse_heads(): arrived = lax.all_to_all(pieces, 'seq', 2, 2, tiled=True)]
    all_gather x1 -> x0, blocking collectives: 23.2 us -> none  [sparse_heads(): picked_kv = lax.all_gather(own, 'seq', axis=2, tiled=True)]
    all_to_all x1, starting transfers between devices: 9.98 us -> 3.51 us  [sparse_heads(): lax.all_to_all(spread, 'seq', 2, 2, tiled=True)]
  transfers between devices with their start and end apart: 4 -> 4, of which waited for: 3 -> 3; matrix products, arithmetic and copies ran while one was open for 12% -> 13% of each run, Pallas kernels for 0% -> 0%
where the time goes in v9:
time: 144 us
  waiting for transfers between devices  40.6 us (28%)
  blocking collectives  39.5 us (27%)
  Pallas kernels  20.4 us (14%)
  between operations  14.2 us (10%)
  other arithmetic  8.61 us (6%)
  starting transfers between devices  7.86 us (5%)
  matrix products  6.62 us (5%)
  local copies, waits for them, and re-layouts  6.05 us (4%)
    all_to_all x1, blocking collectives, sparse_heads(): arrived = lax.all_to_all(pieces, 'seq', 2, 2, tiled=True)  39.5 us
    ppermute x1, waiting for transfers between devices, dense_heads(): lent = lax.ppermute(rows_first[:, half:], 'seq', swap)  30.2 us
    pallas_call x1, Pallas kernels, dense_flash(): pl.pallas_call(functools.partial(flash_kernel, scale=scale, block=block),...  20.4 us
    ppermute x1, waiting for transfers between devices, dense_heads(): returned = lax.ppermute(theirs, 'seq', swap)  5.39 us
    all_gather x1, waiting for transfers between devices, dense_heads(): gathered = lax.all_gather(stacked, 'seq', axis=2, tiled=True)  4.97 us
    sub x1, other arithmetic, attend_ranked(): weights = jnp.where(visible, jnp.exp(scores - leading), 0.0)  4.72 us
    all_to_all x1, starting transfers between devices, sparse_heads(): lax.all_to_all(spread, 'seq', 2, 2, tiled=True)  3.51 us
    ppermute x1, starting transfers between devices, dense_heads(): lent = lax.ppermute(rows_first[:, half:], 'seq', swap)  2.89 us
  transfers between devices with their start and end apart: 4, of which 3 were waited for; matrix products, arithmetic and copies ran while one was open for 13% of the time, Pallas kernels for 0%

profile of v9, /device:TPU:1, one launch (start us, length us, event | category | flops | bytes accessed | tf_op | source)
XLA Modules:
  0.0 143.8 jit_solution(13885046216151926975)
XLA Ops:
  7.2 0.0 copy-start
  7.2 0.0 copy-start.4
  7.2 0.0 copy-start.6
  7.2 0.0 all-gather.2.cloned.1.call-start
  7.2 1.2 copy_bitcast_fusion
  8.4 0.8 pad_maximum_fusion.1
  9.3 0.0 all-gather.2.cloned.1.call-update
  9.3 1.7 %fusion.42 = bf16[3,512,128]{2,1,0:T(8,128)(2,1)S(1)} fusion(bf16[512,3,128]{2,0,1:T(8,128)(2,1)} %param.13, s32[512]{0:T(512)S(1)} %iota_add_fusion, s32[3,512]{1,0:T(4,128)} %param.15), kind=kOutput, calls=%fused_computation.34 | convolution fusion | flops 202309632 | bytes 794624 | tf_op jit(solution)/shard_map/ent,ted->end/dot_general | solution.py:132
  11.0 0.0 copy-done.4
  11.0 0.0 copy-done.6
  11.0 0.6 fusion.39
  11.7 0.1 pad_maximum_fusion
  11.7 0.0 copy-start.2
  11.7 0.1 copy.38
  11.8 0.0 copy-start.7
  11.9 39.5 %all_to_all.10 = bf16[2,3,16,32,128]{4,3,1,0,2:T(8,128)(2,1)S(1)} all-to-all(bf16[2,3,16,32,128]{4,3,1,0,2:T(8,128)(2,1)S(1)} %copy.38), channel_id=1, replica_groups=mesh['dp'=4,'head'=4,'seq'=16] {'seq'}, dimensions={2} | all-to-all | bytes 1572864 | tf_op jit(solution)/shard_map/all_to_all | solution.py:140
  51.3 0.1 reduce_sum.21
  51.5 1.1 broadcast_in_dim.34
  52.6 3.5 %all-to-all-start.1 = ((bf16[2,3,16,32,128]{4,3,1,0,2:T(8,128)(2,1)}), bf16[2,3,16,32,128]{4,3,1,0,2:T(8,128)(2,1)S(1)}, u32[]{:S(2)}, u32[]{:S(2)}) async-start(bf16[2,3,16,32,128]{4,3,1,0,2:T(8,128)(2,1)} %broadcast_in_dim.34), calls=%async_computation.1 | async-start | bytes 1572864 | tf_op jit(solution)/shard_map/all_to_all | solution.py:143
  56.1 0.0 copy-done.2
  56.2 2.9 %collective-permute-start = (bf16[2,256,128]{2,1,0:T(8,128)(2,1)S(1)}, bf16[2,256,128]{2,1,0:T(8,128)(2,1)S(1)}, u32[]{:S(2)}, u32[]{:S(2)}) collective-permute-start(bf16[2,256,128]{2,1,0:T(8,128)(2,1)S(1)} %get-tuple-element.17), channel_id=1, source_target_pairs={{0,15},{1,14},{2,13},{3,12},{4,11},{5,10},{6,9},{7,8},{8,7},{9,6},... | collective-permute-start | bytes 393224 | tf_op jit(solution)/shard_map/ppermute | solution.py:97
  59.1 0.1 multiply_subtract_fusion
  59.2 0.0 copy-done.7
  59.2 0.6 fusion.3
  59.8 0.6 fusion.60
  60.5 0.6 pad_add_fusion.1.info_ref
  61.1 0.8 iota_compare_fusion
  61.9 30.2 %collective-permute-done = bf16[2,256,128]{2,1,0:T(8,128)(2,1)S(1)} collective-permute-done((bf16[2,256,128]{2,1,0:T(8,128)(2,1)S(1)}, bf16[2,256,128]{2,1,0:T(8,128)(2,1)S(1)}, u32[]{:S(2)}, u32[]{:S(2)}) %collective-permute-start) | collective-permute-done | bytes 131104 | tf_op jit(solution)/shard_map/ppermute | solution.py:97
  92.0 0.7 pad_maximum_fusion.2.q_ref
  92.8 0.0 all-to-all-done.1
  92.8 0.1 fusion.64
  92.8 0.8 copy.39
  93.6 0.8 copy.28
  94.4 0.0 copy-done
  94.4 2.0 %fusion.52 = f32[3,512,512]{1,2,0:T(8,128)S(1)} fusion(bf16[3,512,128]{2,1,0:T(8,128)(2,1)} %bitcast.39, bf16[512,3,128]{2,0,1:T(8,128)(2,1)S(1)} %copy-done, s32[512]{0:T(512)S(1)} %iota_add_fusion, s32[3,512]{1,0:T(4,128)S(1)} %copy-done.4), kind=kOutput, calls=%fused_computation.37 | convolution fusion | flops 403636224 | bytes 3940352 | tf_op jit(solution)/shard_map/erd,ekd->erk/dot_general | solution.py:112
  96.5 4.7 %fusion.65 = (f32[3,512]{1,0:T(4,128)}, bf16[3,512,512]{1,2,0:T(8,128)(2,1)}) fusion(f32[3,512,512]{1,2,0:T(8,128)S(1)} %fusion.52, pred[512,512]{0,1:T(8,128)(4,1)} %iota_compare_fusion), kind=kOutput, calls=%fused_computation.65 | output fusion | flops 6291967 | bytes 4986880 | tf_op jit(solution)/shard_map/sub | solution.py:116
  101.2 5.0 %all-gather.2.cloned.1.call-done.k_ref.v_ref = bf16[2,2,8192,128]{3,2,1,0:T(8,128)(2,1)} async-done(((bf16[2,2,512,128]{3,2,1,0:T(8,128)(2,1)}), bf16[2,2,8192,128]{3,2,1,0:T(8,128)(2,1)}) %all-gather.2.cloned.1.call-update) | async-done | bytes 8388624 | tf_op jit(solution)/shard_map/all_gather | solution.py:95
  106.2 20.4 %shard_map.95 = (bf16[2,256,128]{2,1,0:T(8,128)(2,1)}, bf16[2,256,128]{2,1,0:T(8,128)(2,1)}) custom-call(s32[4]{0:T(128)} %pad_add_fusion.1.info_ref, bf16[2,2,256,128]{3,2,1,0:T(8,128)(2,1)} %pad_maximum_fusion.2.q_ref, bf16[2,2,8192,128]{3,2,1,0:T(8,128)(2,1)} %all-gather.2.cloned.1.call-done.k_ref.v_ref, ...), custom_call_target="tpu_custom_call" | custom-call | flops 2147483648 | bytes 4718592 | tf_op jit(solution)/shard_map/pallas_call | solution.py:65
  126.6 1.4 collective-permute-start.1
  128.0 0.0 copy-done.1
  128.0 0.0 copy-done.5
  128.0 0.0 copy-done.9
  128.0 0.0 copy-start.3
  128.1 1.6 %fusion.48 = bf16[512,3,128]{0,2,1:T(8,128)(2,1)S(1)} fusion(s32[512]{0:T(512)S(1)} %iota_add_fusion, s32[3,512]{1,0:T(4,128)S(1)} %copy-done.4, bf16[3,512,128]{2,1,0:T(8,128)(2,1)S(1)} %bitcast.41, bf16[3,512,512]{1,2,0:T(8,128)(2,1)S(1)} %copy-done.8, f32[3,512]{1,0:T(4,128)S(1)} %copy-done.5, f32[3,512]{1,0:T(4,128)S(1)} %copy-done.9), kind=kOutput, calls=%fused_computation.36 | convolution fusion | flops 404226048 | bytes 2379776 | tf_op jit(solution)/shard_map/ent,end->ted/dot_general | solution.py:147
  129.7 0.9 copy.33
  130.6 5.4 %collective-permute-done.1 = bf16[2,256,128]{2,1,0:T(8,128)(2,1)S(1)} collective-permute-done((bf16[2,256,128]{2,1,0:T(8,128)(2,1)}, bf16[2,256,128]{2,1,0:T(8,128)(2,1)S(1)}, u32[]{:S(2)}, u32[]{:S(2)}) %collective-permute-start.1) | collective-permute-done | bytes 131104 | tf_op jit(solution)/shard_map/ppermute | solution.py:103
  136.0 0.0 copy-done.3
  136.0 1.0 copy.32
  (9 shorter events, 0.1 us)
Async XLA Ops:
  7.2 87.3 %copy-start = (bf16[512,3,128]{2,0,1:T(8,128)(2,1)S(1)}, bf16[512,3,128]{2,0,1:T(8,128)(2,1)}, u32[]{:S(2)}) copy-start(bf16[512,3,128]{2,0,1:T(8,128)(2,1)} %param.11) | copy-start | bytes 1179652
  7.2 3.8 %copy-start.4 = (s32[3,512]{1,0:T(4,128)S(1)}, s32[3,512]{1,0:T(4,128)}, u32[]{:S(2)}) copy-start(s32[3,512]{1,0:T(4,128)} %param.15) | copy-start | bytes 18436
  7.2 3.8 %copy-start.6 = (bf16[512,3,128]{2,0,1:T(8,128)(2,1)S(1)}, bf16[512,3,128]{2,0,1:T(8,128)(2,1)}, u32[]{:S(2)}) copy-start(bf16[512,3,128]{2,0,1:T(8,128)(2,1)} %param.12) | copy-start | bytes 1179652
  7.2 99.0 %all-gather.2.cloned.1.call-start = ((), (), s32[]{:S(2)}) async-start(), calls=%async_computation.2 | async-start | bytes 8912896 | tf_op jit(solution)/shard_map/all_gather | solution.py:95
  11.7 44.4 %copy-start.2 = (bf16[512,2,128]{2,1,0:T(2,128)(2,1)S(1)}, bf16[512,2,128]{2,1,0:T(2,128)(2,1)}, u32[]{:S(2)}) copy-start(bf16[512,2,128]{2,1,0:T(2,128)(2,1)} %param.8) | copy-start | bytes 786436
  11.8 47.3 %copy-start.7 = (bf16[3,512]{1,0:T(4,128)(2,1)S(1)}, bf16[3,512]{1,0:T(4,128)(2,1)}, u32[]{:S(2)}) copy-start(bf16[3,512]{1,0:T(4,128)(2,1)} %param.14) | copy-start | bytes 9220
  52.6 40.2 %all-to-all-start.1 = ((bf16[2,3,16,32,128]{4,3,1,0,2:T(8,128)(2,1)}), bf16[2,3,16,32,128]{4,3,1,0,2:T(8,128)(2,1)S(1)}, u32[]{:S(2)}, u32[]{:S(2)}) async-start(bf16[2,3,16,32,128]{4,3,1,0,2:T(8,128)(2,1)} %broadcast_in_dim.34), calls=%async_computation.1 | async-start | bytes 1572864 | tf_op jit(solution)/shard_map/all_to_all | solution.py:143
  56.2 35.8 %collective-permute-start = (bf16[2,256,128]{2,1,0:T(8,128)(2,1)S(1)}, bf16[2,256,128]{2,1,0:T(8,128)(2,1)S(1)}, u32[]{:S(2)}, u32[]{:S(2)}) collective-permute-start(bf16[2,256,128]{2,1,0:T(8,128)(2,1)S(1)} %get-tuple-element.17), channel_id=1, source_target_pairs={{0,15},{1,14},{2,13},{3,12},{4,11},{5,10},{6,9},{7,8},{8,7},{9,6},... | collective-permute-start | bytes 393224 | tf_op jit(solution)/shard_map/ppermute | solution.py:97
  101.2 26.8 %copy-start.1 = (bf16[1,3,16,32,128]{4,3,2,1,0:T(8,128)(2,1)S(1)}, bf16[1,3,16,32,128]{4,3,2,1,0:T(8,128)(2,1)}, u32[]{:S(2)}) copy-start(bf16[1,3,16,32,128]{4,3,2,1,0:T(8,128)(2,1)} %copy.39) | copy-start | bytes 1179652
  101.2 26.8 %copy-start.5 = (f32[3,512]{1,0:T(4,128)S(1)}, f32[3,512]{1,0:T(4,128)}, u32[]{:S(2)}) copy-start(f32[3,512]{1,0:T(4,128)} %fusion.60) | copy-start | bytes 18436
  101.2 26.8 %copy-start.8 = (bf16[3,512,512]{1,2,0:T(8,128)(2,1)S(1)}, bf16[3,512,512]{1,2,0:T(8,128)(2,1)}, u32[]{:S(2)}) copy-start(bf16[3,512,512]{1,2,0:T(8,128)(2,1)} %get-tuple-element.19) | copy-start | bytes 4718596
  101.2 26.8 %copy-start.9 = (f32[3,512]{1,0:T(4,128)S(1)}, f32[3,512]{1,0:T(4,128)}, u32[]{:S(2)}) copy-start(f32[3,512]{1,0:T(4,128)} %get-tuple-element.18) | copy-start | bytes 18436
  126.6 9.4 %collective-permute-start.1 = (bf16[2,256,128]{2,1,0:T(8,128)(2,1)}, bf16[2,256,128]{2,1,0:T(8,128)(2,1)S(1)}, u32[]{:S(2)}, u32[]{:S(2)}) collective-permute-start(bf16[2,256,128]{2,1,0:T(8,128)(2,1)} %get-tuple-element.5), channel_id=1, source_target_pairs={{0,15},{1,14},{2,13},{3,12},{4,11},{5,10},{6,9},{7,8},{8,7},{9,6},... | collective-permute-start | bytes 393224 | tf_op jit(solution)/shard_map/ppermute | solution.py:103
  128.0 7.9 %copy-start.3 = (bf16[2,256,128]{2,1,0:T(8,128)(2,1)S(1)}, bf16[2,256,128]{2,1,0:T(8,128)(2,1)}, u32[]{:S(2)}) copy-start(bf16[2,256,128]{2,1,0:T(8,128)(2,1)} %get-tuple-element.4) | copy-start | bytes 393220
Sparse Core Ops, SparseCore 0:
  9.9 96.2 all-gather.1

commit v10 on v8

--- a/solution.py
+++ b/solution.py
@@ -9,7 +9,7 @@
 from jax.sharding import PartitionSpec as P
 
 NEGATIVE = -1e30
-KEY_BLOCK = 512
+KEY_BLOCK = 2048
 
 
 def flash_kernel(info_ref, q_ref, k_ref, v_ref, own_ref, lent_ref, *, scale, block):
@@ -97,7 +97,7 @@
     lent = lax.ppermute(rows_first[:, half:], "seq", swap)
     both = jnp.stack([rows_first[:, :half], lent], axis=0)
     ends = jnp.stack([me * tok_rows, partner * tok_rows + half])
-    lasts = ends // KEY_BLOCK
+    lasts = (ends + half - 1) // KEY_BLOCK
     info = jnp.concatenate([lasts, ends - lasts * KEY_BLOCK]).astype(jnp.int32)
     ours, theirs = dense_flash(info, both, gathered)
     returned = lax.ppermute(theirs, "seq", swap)

time: 133 us -> 128 us (0.962)
  Pallas kernels: 20.4 us -> 15.9 us
    pallas_call x1, Pallas kernels: 20.4 us -> 15.9 us  [dense_flash(): pl.pallas_call(functools.partial(flash_kernel, scale=scale, block=block),...]
where the time goes in v10:
time: 128 us
  waiting for transfers between devices  41.7 us (33%)
  blocking collectives  23.2 us (18%)
  Pallas kernels  15.9 us (12%)
  between operations  14.2 us (11%)
  starting transfers between devices  14.1 us (11%)
  other arithmetic  8.56 us (7%)
  matrix products  5.96 us (5%)
  local copies, waits for them, and re-layouts  4.24 us (3%)
    ppermute x1, waiting for transfers between devices, dense_heads(): lent = lax.ppermute(rows_first[:, half:], 'seq', swap)  29.3 us
    all_gather x1, blocking collectives, sparse_heads(): picked_kv = lax.all_gather(own, 'seq', axis=2, tiled=True)  23.2 us
    pallas_call x1, Pallas kernels, dense_flash(): pl.pallas_call(functools.partial(flash_kernel, scale=scale, block=block),...  15.9 us
    all_to_all x1, starting transfers between devices, sparse_heads(): arrived = lax.all_to_all(pieces, 'seq', 2, 2, tiled=True)  9.98 us
    ppermute x1, waiting for transfers between devices, dense_heads(): returned = lax.ppermute(theirs, 'seq', swap)  6.38 us
    all_gather x1, waiting for transfers between devices, dense_heads(): gathered = lax.all_gather(stacked, 'seq', axis=2, tiled=True)  6 us
    sub x1, other arithmetic, attend_ranked(): weights = jnp.where(visible, jnp.exp(scores - leading), 0.0)  4.66 us
    ppermute x1, starting transfers between devices, dense_heads(): lent = lax.ppermute(rows_first[:, half:], 'seq', swap)  2.93 us
  transfers between devices with their start and end apart: 4, of which 3 were waited for; matrix products, arithmetic and copies ran while one was open for 12% of the time, Pallas kernels for 0%

profile of v10, /device:TPU:1, one launch (start us, length us, event | category | flops | bytes accessed | tf_op | source)
XLA Modules:
  0.0 127.8 jit_solution(9467124693282934831)
XLA Ops:
  7.2 0.0 copy-start
  7.2 0.0 copy-start.4
  7.2 0.0 copy-start.6
  7.2 0.0 all-gather.2.cloned.1.call-start
  7.2 1.2 copy_bitcast_fusion
  8.4 0.9 pad_maximum_fusion.1
  9.3 0.0 all-gather.2.cloned.1.call-update
  9.3 1.7 %fusion.42 = bf16[3,512,128]{2,1,0:T(8,128)(2,1)S(1)} fusion(bf16[512,3,128]{2,0,1:T(8,128)(2,1)} %param.13, s32[512]{0:T(512)S(1)} %iota_add_fusion, s32[3,512]{1,0:T(4,128)} %param.15), kind=kOutput, calls=%fused_computation.34 | convolution fusion | flops 202309632 | bytes 794624 | tf_op jit(solution)/shard_map/ent,ted->end/dot_general | solution.py:132
  11.0 0.0 copy-done.4
  11.0 0.0 copy-done.6
  11.0 0.0 copy-start.2
  11.0 0.6 fusion.39
  11.7 0.0 copy-start.7
  11.7 0.1 pad_maximum_fusion
  11.8 1.1 copy.24
  12.8 10.0 %all-to-all-start = ((bf16[2,3,16,32,128]{4,3,1,0,2:T(8,128)(2,1)}), bf16[2,3,16,32,128]{4,3,1,0,2:T(8,128)(2,1)S(1)}, u32[]{:S(2)}, u32[]{:S(2)}) async-start(bf16[2,3,16,32,128]{4,3,1,0,2:T(8,128)(2,1)} %copy.24), calls=%async_computation | async-start | bytes 1572864 | tf_op jit(solution)/shard_map/all_to_all | solution.py:140
  22.8 0.0 copy-done.2
  22.9 2.9 %collective-permute-start = (bf16[2,256,128]{2,1,0:T(8,128)(2,1)S(1)}, bf16[2,256,128]{2,1,0:T(8,128)(2,1)S(1)}, u32[]{:S(2)}, u32[]{:S(2)}) collective-permute-start(bf16[2,256,128]{2,1,0:T(8,128)(2,1)S(1)} %get-tuple-element.13), channel_id=1, source_target_pairs={{0,15},{1,14},{2,13},{3,12},{4,11},{5,10},{6,9},{7,8},{8,7},{9,6},... | collective-permute-start | bytes 393224 | tf_op jit(solution)/shard_map/ppermute | solution.py:97
  25.8 0.1 multiply_subtract_fusion
  25.9 0.0 copy-done.7
  25.9 0.6 fusion.3
  26.6 0.6 fusion.60
  27.2 0.6 pad_add_fusion.1.info_ref
  27.8 0.8 iota_compare_fusion
  28.6 29.3 %collective-permute-done = bf16[2,256,128]{2,1,0:T(8,128)(2,1)S(1)} collective-permute-done((bf16[2,256,128]{2,1,0:T(8,128)(2,1)S(1)}, bf16[2,256,128]{2,1,0:T(8,128)(2,1)S(1)}, u32[]{:S(2)}, u32[]{:S(2)}) %collective-permute-start) | collective-permute-done | bytes 131104 | tf_op jit(solution)/shard_map/ppermute | solution.py:97
  57.9 0.7 pad_maximum_fusion.2.q_ref
  58.6 0.0 all-to-all-done
  58.6 0.1 reduce_sum.21
  58.8 23.2 %all_gather.7 = bf16[2,3,512,128]{3,2,1,0:T(8,128)(2,1)} all-gather(bf16[2,3,32,128]{3,2,1,0:T(8,128)(2,1)S(1)} %reduce_sum.21), channel_id=1, replica_groups=mesh['dp'=4,'head'=4,'seq'=16] {'seq'}, dimensions={2}, use_global_device_ids=true | all-gather | bytes 835584 | tf_op jit(solution)/shard_map/all_gather | solution.py:142
  82.0 0.0 copy-done
  82.0 2.1 %fusion.52 = f32[3,512,512]{1,2,0:T(8,128)S(1)} fusion(bf16[512,3,128]{2,0,1:T(8,128)(2,1)S(1)} %copy-done, s32[512]{0:T(512)S(1)} %iota_add_fusion, s32[3,512]{1,0:T(4,128)S(1)} %copy-done.4, bf16[2,3,512,128]{3,2,1,0:T(8,128)(2,1)} %all_gather.7), kind=kOutput, calls=%fused_computation.37 | convolution fusion | flops 403636224 | bytes 3940352 | tf_op jit(solution)/shard_map/erd,ekd->erk/dot_general | solution.py:112
  84.1 4.7 %fusion.64 = (f32[3,512]{1,0:T(4,128)}, bf16[3,512,512]{1,2,0:T(8,128)(2,1)}) fusion(f32[3,512,512]{1,2,0:T(8,128)S(1)} %fusion.52, pred[512,512]{0,1:T(8,128)(4,1)} %iota_compare_fusion), kind=kOutput, calls=%fused_computation.66 | output fusion | flops 6291967 | bytes 4986880 | tf_op jit(solution)/shard_map/sub | solution.py:116
  88.7 0.0 copy-start.1
  88.7 0.0 copy-start.5
  88.7 0.0 copy-start.8
  88.7 6.0 %all-gather.2.cloned.1.call-done.k_ref.v_ref = bf16[2,2,8192,128]{3,2,1,0:T(8,128)(2,1)} async-done(((bf16[2,2,512,128]{3,2,1,0:T(8,128)(2,1)}), bf16[2,2,8192,128]{3,2,1,0:T(8,128)(2,1)}) %all-gather.2.cloned.1.call-update) | async-done | bytes 8388624 | tf_op jit(solution)/shard_map/all_gather | solution.py:95
  94.7 15.9 %shard_map.95 = (bf16[2,256,128]{2,1,0:T(8,128)(2,1)}, bf16[2,256,128]{2,1,0:T(8,128)(2,1)}) custom-call(s32[4]{0:T(128)} %pad_add_fusion.1.info_ref, bf16[2,2,256,128]{3,2,1,0:T(8,128)(2,1)} %pad_maximum_fusion.2.q_ref, bf16[2,2,8192,128]{3,2,1,0:T(8,128)(2,1)} %all-gather.2.cloned.1.call-done.k_ref.v_ref, ...), custom_call_target="tpu_custom_call" | custom-call | flops 2147483648 | bytes 4718592 | tf_op jit(solution)/shard_map/pallas_call | solution.py:65
  110.6 1.1 collective-permute-start.1
  111.7 0.0 copy-done.1
  111.7 0.0 copy-done.5
  111.7 0.0 copy-done.8
  111.7 0.0 copy-done.9
  111.7 0.0 copy-start.3
  111.7 0.9 fusion.48
  112.7 0.9 copy.21
  113.6 6.4 %collective-permute-done.1 = bf16[2,256,128]{2,1,0:T(8,128)(2,1)S(1)} collective-permute-done((bf16[2,256,128]{2,1,0:T(8,128)(2,1)}, bf16[2,256,128]{2,1,0:T(8,128)(2,1)S(1)}, u32[]{:S(2)}, u32[]{:S(2)}) %collective-permute-start.1) | collective-permute-done | bytes 131104 | tf_op jit(solution)/shard_map/ppermute | solution.py:103
  120.0 0.0 copy-done.3
  120.0 1.0 copy.20
  (5 shorter events, 0.1 us)
Async XLA Ops:
  7.2 74.8 %copy-start = (bf16[512,3,128]{2,0,1:T(8,128)(2,1)S(1)}, bf16[512,3,128]{2,0,1:T(8,128)(2,1)}, u32[]{:S(2)}) copy-start(bf16[512,3,128]{2,0,1:T(8,128)(2,1)} %param.11) | copy-start | bytes 1179652
  7.2 3.8 %copy-start.4 = (s32[3,512]{1,0:T(4,128)S(1)}, s32[3,512]{1,0:T(4,128)}, u32[]{:S(2)}) copy-start(s32[3,512]{1,0:T(4,128)} %param.15) | copy-start | bytes 18436
  7.2 3.8 %copy-start.6 = (bf16[512,3,128]{2,0,1:T(8,128)(2,1)S(1)}, bf16[512,3,128]{2,0,1:T(8,128)(2,1)}, u32[]{:S(2)}) copy-start(bf16[512,3,128]{2,0,1:T(8,128)(2,1)} %param.12) | copy-start | bytes 1179652
  7.2 87.5 %all-gather.2.cloned.1.call-start = ((), (), s32[]{:S(2)}) async-start(), calls=%async_computation.1 | async-start | bytes 8912896 | tf_op jit(solution)/shard_map/all_gather | solution.py:95
  11.0 11.8 %copy-start.2 = (bf16[512,2,128]{2,1,0:T(2,128)(2,1)S(1)}, bf16[512,2,128]{2,1,0:T(2,128)(2,1)}, u32[]{:S(2)}) copy-start(bf16[512,2,128]{2,1,0:T(2,128)(2,1)} %param.8) | copy-start | bytes 786436
  11.7 14.2 %copy-start.7 = (bf16[3,512]{1,0:T(4,128)(2,1)S(1)}, bf16[3,512]{1,0:T(4,128)(2,1)}, u32[]{:S(2)}) copy-start(bf16[3,512]{1,0:T(4,128)(2,1)} %param.14) | copy-start | bytes 9220
  12.8 45.8 %all-to-all-start = ((bf16[2,3,16,32,128]{4,3,1,0,2:T(8,128)(2,1)}), bf16[2,3,16,32,128]{4,3,1,0,2:T(8,128)(2,1)S(1)}, u32[]{:S(2)}, u32[]{:S(2)}) async-start(bf16[2,3,16,32,128]{4,3,1,0,2:T(8,128)(2,1)} %copy.24), calls=%async_computation | async-start | bytes 1572864 | tf_op jit(solution)/shard_map/all_to_all | solution.py:140
  22.9 35.0 %collective-permute-start = (bf16[2,256,128]{2,1,0:T(8,128)(2,1)S(1)}, bf16[2,256,128]{2,1,0:T(8,128)(2,1)S(1)}, u32[]{:S(2)}, u32[]{:S(2)}) collective-permute-start(bf16[2,256,128]{2,1,0:T(8,128)(2,1)S(1)} %get-tuple-element.13), channel_id=1, source_target_pairs={{0,15},{1,14},{2,13},{3,12},{4,11},{5,10},{6,9},{7,8},{8,7},{9,6},... | collective-permute-start | bytes 393224 | tf_op jit(solution)/shard_map/ppermute | solution.py:97
  88.7 23.0 %copy-start.1 = (bf16[2,3,512,128]{3,2,1,0:T(8,128)(2,1)S(1)}, bf16[2,3,512,128]{3,2,1,0:T(8,128)(2,1)}, u32[]{:S(2)}) copy-start(bf16[2,3,512,128]{3,2,1,0:T(8,128)(2,1)} %all_gather.7) | copy-start | bytes 2359300
  88.7 23.0 %copy-start.5 = (f32[3,512]{1,0:T(4,128)S(1)}, f32[3,512]{1,0:T(4,128)}, u32[]{:S(2)}) copy-start(f32[3,512]{1,0:T(4,128)} %fusion.60) | copy-start | bytes 18436
  88.7 23.0 %copy-start.8 = (bf16[3,512,512]{1,2,0:T(8,128)(2,1)S(1)}, bf16[3,512,512]{1,2,0:T(8,128)(2,1)}, u32[]{:S(2)}) copy-start(bf16[3,512,512]{1,2,0:T(8,128)(2,1)} %get-tuple-element.15) | copy-start | bytes 4718596
  88.7 23.0 %copy-start.9 = (f32[3,512]{1,0:T(4,128)S(1)}, f32[3,512]{1,0:T(4,128)}, u32[]{:S(2)}) copy-start(f32[3,512]{1,0:T(4,128)} %get-tuple-element.14) | copy-start | bytes 18436
  110.6 9.3 %collective-permute-start.1 = (bf16[2,256,128]{2,1,0:T(8,128)(2,1)}, bf16[2,256,128]{2,1,0:T(8,128)(2,1)S(1)}, u32[]{:S(2)}, u32[]{:S(2)}) collective-permute-start(bf16[2,256,128]{2,1,0:T(8,128)(2,1)} %get-tuple-element.5), channel_id=1, source_target_pairs={{0,15},{1,14},{2,13},{3,12},{4,11},{5,10},{6,9},{7,8},{8,7},{9,6},... | collective-permute-start | bytes 393224 | tf_op jit(solution)/shard_map/ppermute | solution.py:103
  111.7 8.2 %copy-start.3 = (bf16[2,256,128]{2,1,0:T(8,128)(2,1)S(1)}, bf16[2,256,128]{2,1,0:T(8,128)(2,1)}, u32[]{:S(2)}) copy-start(bf16[2,256,128]{2,1,0:T(8,128)(2,1)} %get-tuple-element.4) | copy-start | bytes 393220
Sparse Core Ops, SparseCore 0:
  9.9 84.7 all-gather.1

commit v11 on v10

--- a/solution.py
+++ b/solution.py
@@ -57,7 +57,7 @@
         lent_ref[0] = result
 
 
-def dense_flash(info, queries, stacked):
+def dense_flash(info, queries, stacked, head=0):
     parts, heads, rows, width = queries.shape
     length = stacked.shape[2]
     block = KEY_BLOCK
@@ -70,8 +70,8 @@
             grid=(heads, parts),
             in_specs=[
                 pl.BlockSpec((1, 1, rows, width), lambda h, p, c: (p, h, 0, 0)),
-                pl.BlockSpec((None, 1, length, width), lambda h, p, c: (0, h, 0, 0)),
-                pl.BlockSpec((None, 1, length, width), lambda h, p, c: (1, h, 0, 0)),
+                pl.BlockSpec((None, 1, length, width), lambda h, p, c: (0, h + head, 0, 0)),
+                pl.BlockSpec((None, 1, length, width), lambda h, p, c: (1, h + head, 0, 0)),
             ],
             out_specs=[pl.BlockSpec((1, rows, width), lambda h, p, c: (h, 0, 0))] * 2,
         ),
@@ -99,9 +99,11 @@
     ends = jnp.stack([me * tok_rows, partner * tok_rows + half])
     lasts = (ends + half - 1) // KEY_BLOCK
     info = jnp.concatenate([lasts, ends - lasts * KEY_BLOCK]).astype(jnp.int32)
-    ours, theirs = dense_flash(info, both, gathered)
-    returned = lax.ppermute(theirs, "seq", swap)
-    mine = jnp.concatenate([ours, returned], axis=1)
+    pieces = []
+    for h in range(heads):
+        ours, theirs = dense_flash(info, both[:, h : h + 1], gathered, h)
+        pieces.append(jnp.concatenate([ours, lax.ppermute(theirs, "seq", swap)], axis=1))
+    mine = jnp.concatenate(pieces, axis=0)
     return jnp.swapaxes(mine, 0, 1)
 
 

time: 128 us -> 129 us (level)
  waiting for transfers between devices: 41.7 us -> 37.3 us
  Pallas kernels: 15.9 us -> 19.5 us
  starting transfers between devices: 14.1 us -> 15.9 us
    ppermute x1 -> x2, waiting for transfers between devices: 6.38 us -> 2.11 us  [dense_heads(): lax.ppermute(theirs, 'seq', swap)]
    pallas_call x1 -> x2, Pallas kernels: 15.9 us -> 19.5 us  [dense_flash(): pl.pallas_call(functools.partial(flash_kernel, scale=scale, block=block),...]
    ppermute x1 -> x2, starting transfers between devices: 1.1 us -> 2.94 us  [dense_heads(): lax.ppermute(theirs, 'seq', swap)]
  transfers between devices with their start and end apart: 4 -> 5, of which waited for: 3 -> 3; matrix products, arithmetic and copies ran while one was open for 12% -> 12% of each run, Pallas kernels for 0% -> 8%
where the time goes in v11:
time: 129 us
  waiting for transfers between devices  37.3 us (29%)
  blocking collectives  23.3 us (18%)
  Pallas kernels  19.5 us (15%)
  starting transfers between devices  15.9 us (12%)
  between operations  14.2 us (11%)
  other arithmetic  8.59 us (7%)
  matrix products  5.95 us (5%)
  local copies, waits for them, and re-layouts  4.25 us (3%)
    ppermute x1, waiting for transfers between devices, dense_heads(): lent = lax.ppermute(rows_first[:, half:], 'seq', swap)  29.3 us
    all_gather x1, blocking collectives, sparse_heads(): picked_kv = lax.all_gather(own, 'seq', axis=2, tiled=True)  23.3 us
    pallas_call x2, Pallas kernels, dense_flash(): pl.pallas_call(functools.partial(flash_kernel, scale=scale, block=block),...  19.5 us
    all_to_all x1, starting transfers between devices, sparse_heads(): arrived = lax.all_to_all(pieces, 'seq', 2, 2, tiled=True)  9.98 us
    all_gather x1, waiting for transfers between devices, dense_heads(): gathered = lax.all_gather(stacked, 'seq', axis=2, tiled=True)  5.89 us
    sub x1, other arithmetic, attend_ranked(): weights = jnp.where(visible, jnp.exp(scores - leading), 0.0)  4.67 us
    ppermute x2, starting transfers between devices, dense_heads(): lax.ppermute(theirs, 'seq', swap)  2.94 us
    ppermute x1, starting transfers between devices, dense_heads(): lent = lax.ppermute(rows_first[:, half:], 'seq', swap)  2.93 us
  transfers between devices with their start and end apart: 5, of which 3 were waited for; matrix products, arithmetic and copies ran while one was open for 12% of the time, Pallas kernels for 8%

profile of v11, /device:TPU:1, one launch (start us, length us, event | category | flops | bytes accessed | tf_op | source)
XLA Modules:
  0.0 129.0 jit_solution(14669429120478015916)
XLA Ops:
  7.2 0.0 copy-start
  7.2 0.0 copy-start.5
  7.2 0.0 copy-start.7
  7.2 0.0 all-gather.2.cloned.1.call-start
  7.2 1.2 copy_bitcast_fusion
  8.4 0.8 pad_maximum_fusion.1
  9.3 0.0 all-gather.2.cloned.1.call-update
  9.3 1.7 %fusion.42 = bf16[3,512,128]{2,1,0:T(8,128)(2,1)S(1)} fusion(bf16[512,3,128]{2,0,1:T(8,128)(2,1)} %param.13, s32[512]{0:T(512)S(1)} %iota_add_fusion, s32[3,512]{1,0:T(4,128)} %param.15), kind=kOutput, calls=%fused_computation.34 | convolution fusion | flops 202309632 | bytes 794624 | tf_op jit(solution)/shard_map/ent,ted->end/dot_general | solution.py:134
  11.0 0.0 copy-done.5
  11.0 0.0 copy-done.7
  11.0 0.0 copy-start.2
  11.0 0.6 fusion.39
  11.7 0.0 copy-start.8
  11.7 0.1 pad_maximum_fusion
  11.8 1.1 copy.24
  12.8 10.0 %all-to-all-start = ((bf16[2,3,16,32,128]{4,3,1,0,2:T(8,128)(2,1)}), bf16[2,3,16,32,128]{4,3,1,0,2:T(8,128)(2,1)S(1)}, u32[]{:S(2)}, u32[]{:S(2)}) async-start(bf16[2,3,16,32,128]{4,3,1,0,2:T(8,128)(2,1)} %copy.24), calls=%async_computation | async-start | bytes 1572864 | tf_op jit(solution)/shard_map/all_to_all | solution.py:142
  22.8 0.0 copy-done.2
  22.9 2.9 %collective-permute-start = (bf16[2,256,128]{2,1,0:T(8,128)(2,1)S(1)}, bf16[2,256,128]{2,1,0:T(8,128)(2,1)S(1)}, u32[]{:S(2)}, u32[]{:S(2)}) collective-permute-start(bf16[2,256,128]{2,1,0:T(8,128)(2,1)S(1)} %get-tuple-element.19), channel_id=1, source_target_pairs={{0,15},{1,14},{2,13},{3,12},{4,11},{5,10},{6,9},{7,8},{8,7},{9,6},... | collective-permute-start | bytes 393224 | tf_op jit(solution)/shard_map/ppermute | solution.py:97
  25.8 0.1 multiply_subtract_fusion
  25.9 0.0 copy-done.8
  25.9 0.6 fusion.3
  26.6 0.6 fusion.61
  27.2 0.7 pad_add_fusion.1.info_ref
  27.8 0.8 iota_compare_fusion
  28.6 29.3 %collective-permute-done = bf16[2,256,128]{2,1,0:T(8,128)(2,1)S(1)} collective-permute-done((bf16[2,256,128]{2,1,0:T(8,128)(2,1)S(1)}, bf16[2,256,128]{2,1,0:T(8,128)(2,1)S(1)}, u32[]{:S(2)}, u32[]{:S(2)}) %collective-permute-start) | collective-permute-done | bytes 131104 | tf_op jit(solution)/shard_map/ppermute | solution.py:97
  57.9 0.7 fusion.58
  58.6 0.0 all-to-all-done
  58.6 0.1 reduce_sum.21
  58.7 23.3 %all_gather.7 = bf16[2,3,512,128]{3,2,1,0:T(8,128)(2,1)} all-gather(bf16[2,3,32,128]{3,2,1,0:T(8,128)(2,1)S(1)} %reduce_sum.21), channel_id=1, replica_groups=mesh['dp'=4,'head'=4,'seq'=16] {'seq'}, dimensions={2}, use_global_device_ids=true | all-gather | bytes 835584 | tf_op jit(solution)/shard_map/all_gather | solution.py:144
  82.1 0.0 copy-done
  82.1 2.1 %fusion.52 = f32[3,512,512]{1,2,0:T(8,128)S(1)} fusion(bf16[512,3,128]{2,0,1:T(8,128)(2,1)S(1)} %copy-done, s32[512]{0:T(512)S(1)} %iota_add_fusion, s32[3,512]{1,0:T(4,128)S(1)} %copy-done.5, bf16[2,3,512,128]{3,2,1,0:T(8,128)(2,1)} %all_gather.7), kind=kOutput, calls=%fused_computation.37 | convolution fusion | flops 403636224 | bytes 3940352 | tf_op jit(solution)/shard_map/erd,ekd->erk/dot_general | solution.py:114
  84.2 4.7 %fusion.65 = (f32[3,512]{1,0:T(4,128)}, bf16[3,512,512]{1,2,0:T(8,128)(2,1)}) fusion(f32[3,512,512]{1,2,0:T(8,128)S(1)} %fusion.52, pred[512,512]{0,1:T(8,128)(4,1)} %iota_compare_fusion), kind=kOutput, calls=%fused_computation.69 | output fusion | flops 6291967 | bytes 4986880 | tf_op jit(solution)/shard_map/sub | solution.py:118
  88.8 5.9 %all-gather.2.cloned.1.call-done.k_ref.v_ref = bf16[2,2,8192,128]{3,2,1,0:T(8,128)(2,1)} async-done(((bf16[2,2,512,128]{3,2,1,0:T(8,128)(2,1)}), bf16[2,2,8192,128]{3,2,1,0:T(8,128)(2,1)}) %all-gather.2.cloned.1.call-update) | async-done | bytes 8388624 | tf_op jit(solution)/shard_map/all_gather | solution.py:95
  94.7 9.7 %shard_map.96 = (bf16[1,256,128]{2,1,0:T(8,128)(2,1)}, bf16[1,256,128]{2,1,0:T(8,128)(2,1)}) custom-call(s32[4]{0:T(128)} %pad_add_fusion.1.info_ref, bf16[2,1,256,128]{3,2,1,0:T(8,128)(2,1)} %get-tuple-element.17.q_ref, bf16[2,2,8192,128]{3,2,1,0:T(8,128)(2,1)} %all-gather.2.cloned.1.call-done.k_ref.v_ref, ...), custom_call_target="tpu_custom_call" | custom-call | flops 1073741824 | bytes 4456448 | tf_op jit(solution)/shard_map/pallas_call | solution.py:65
  104.4 0.2 collective-permute-start.2
  104.6 9.8 %shard_map.95 = (bf16[1,256,128]{2,1,0:T(8,128)(2,1)}, bf16[1,256,128]{2,1,0:T(8,128)(2,1)}) custom-call(s32[4]{0:T(128)} %pad_add_fusion.1.info_ref, bf16[2,1,256,128]{3,2,1,0:T(8,128)(2,1)} %get-tuple-element.16.q_ref, bf16[2,2,8192,128]{3,2,1,0:T(8,128)(2,1)} %all-gather.2.cloned.1.call-done.k_ref.v_ref, ...), custom_call_target="tpu_custom_call" | custom-call | flops 1073741824 | bytes 4456448 | tf_op jit(solution)/shard_map/pallas_call | solution.py:65
  114.5 2.7 %collective-permute-start.1 = (bf16[1,256,128]{2,1,0:T(8,128)(2,1)}, bf16[1,256,128]{2,1,0:T(8,128)(2,1)S(1)}, u32[]{:S(2)}, u32[]{:S(2)}) collective-permute-start(bf16[1,256,128]{2,1,0:T(8,128)(2,1)} %get-tuple-element.7), channel_id=1, source_target_pairs={{0,15},{1,14},{2,13},{3,12},{4,11},{5,10},{6,9},{7,8},{8,7},{9,6},... | collective-permute-start | bytes 196616 | tf_op jit(solution)/shard_map/ppermute | solution.py:105
  117.2 0.0 copy-done.1
  117.2 0.0 copy-done.6
  117.2 0.0 copy-done.9
  117.2 0.0 copy-done.10
  117.2 0.0 copy-start.3
  117.2 0.0 copy-start.4
  117.2 0.9 fusion.48
  118.2 0.9 copy.21
  119.1 0.0 collective-permute-done.2
  119.1 2.1 %collective-permute-done.1 = bf16[1,256,128]{2,1,0:T(8,128)(2,1)S(1)} collective-permute-done((bf16[1,256,128]{2,1,0:T(8,128)(2,1)}, bf16[1,256,128]{2,1,0:T(8,128)(2,1)S(1)}, u32[]{:S(2)}, u32[]{:S(2)}) %collective-permute-start.1) | collective-permute-done | bytes 65568 | tf_op jit(solution)/shard_map/ppermute | solution.py:105
  121.2 1.0 copy.20
  (10 shorter events, 0.1 us)
Async XLA Ops:
  7.2 74.9 %copy-start = (bf16[512,3,128]{2,0,1:T(8,128)(2,1)S(1)}, bf16[512,3,128]{2,0,1:T(8,128)(2,1)}, u32[]{:S(2)}) copy-start(bf16[512,3,128]{2,0,1:T(8,128)(2,1)} %param.11) | copy-start | bytes 1179652
  7.2 3.8 %copy-start.5 = (s32[3,512]{1,0:T(4,128)S(1)}, s32[3,512]{1,0:T(4,128)}, u32[]{:S(2)}) copy-start(s32[3,512]{1,0:T(4,128)} %param.15) | copy-start | bytes 18436
  7.2 3.8 %copy-start.7 = (bf16[512,3,128]{2,0,1:T(8,128)(2,1)S(1)}, bf16[512,3,128]{2,0,1:T(8,128)(2,1)}, u32[]{:S(2)}) copy-start(bf16[512,3,128]{2,0,1:T(8,128)(2,1)} %param.12) | copy-start | bytes 1179652
  7.2 87.5 %all-gather.2.cloned.1.call-start = ((), (), s32[]{:S(2)}) async-start(), calls=%async_computation.1 | async-start | bytes 8912896 | tf_op jit(solution)/shard_map/all_gather | solution.py:95
  11.0 11.8 %copy-start.2 = (bf16[512,2,128]{2,1,0:T(2,128)(2,1)S(1)}, bf16[512,2,128]{2,1,0:T(2,128)(2,1)}, u32[]{:S(2)}) copy-start(bf16[512,2,128]{2,1,0:T(2,128)(2,1)} %param.8) | copy-start | bytes 786436
  11.7 14.2 %copy-start.8 = (bf16[3,512]{1,0:T(4,128)(2,1)S(1)}, bf16[3,512]{1,0:T(4,128)(2,1)}, u32[]{:S(2)}) copy-start(bf16[3,512]{1,0:T(4,128)(2,1)} %param.14) | copy-start | bytes 9220
  12.8 45.8 %all-to-all-start = ((bf16[2,3,16,32,128]{4,3,1,0,2:T(8,128)(2,1)}), bf16[2,3,16,32,128]{4,3,1,0,2:T(8,128)(2,1)S(1)}, u32[]{:S(2)}, u32[]{:S(2)}) async-start(bf16[2,3,16,32,128]{4,3,1,0,2:T(8,128)(2,1)} %copy.24), calls=%async_computation | async-start | bytes 1572864 | tf_op jit(solution)/shard_map/all_to_all | solution.py:142
  22.9 35.0 %collective-permute-start = (bf16[2,256,128]{2,1,0:T(8,128)(2,1)S(1)}, bf16[2,256,128]{2,1,0:T(8,128)(2,1)S(1)}, u32[]{:S(2)}, u32[]{:S(2)}) collective-permute-start(bf16[2,256,128]{2,1,0:T(8,128)(2,1)S(1)} %get-tuple-element.19), channel_id=1, source_target_pairs={{0,15},{1,14},{2,13},{3,12},{4,11},{5,10},{6,9},{7,8},{8,7},{9,6},... | collective-permute-start | bytes 393224 | tf_op jit(solution)/shard_map/ppermute | solution.py:97
  104.4 14.7 %collective-permute-start.2 = (bf16[1,256,128]{2,1,0:T(8,128)(2,1)}, bf16[1,256,128]{2,1,0:T(8,128)(2,1)S(1)}, u32[]{:S(2)}, u32[]{:S(2)}) collective-permute-start(bf16[1,256,128]{2,1,0:T(8,128)(2,1)} %get-tuple-element.9), channel_id=1, source_target_pairs={{0,15},{1,14},{2,13},{3,12},{4,11},{5,10},{6,9},{7,8},{8,7},{9,6},... | collective-permute-start | bytes 196616 | tf_op jit(solution)/shard_map/ppermute | solution.py:105
  104.6 12.6 %copy-start.1 = (bf16[2,3,512,128]{3,2,1,0:T(8,128)(2,1)S(1)}, bf16[2,3,512,128]{3,2,1,0:T(8,128)(2,1)}, u32[]{:S(2)}) copy-start(bf16[2,3,512,128]{3,2,1,0:T(8,128)(2,1)} %all_gather.7) | copy-start | bytes 2359300
  104.6 12.6 %copy-start.6 = (f32[3,512]{1,0:T(4,128)S(1)}, f32[3,512]{1,0:T(4,128)}, u32[]{:S(2)}) copy-start(f32[3,512]{1,0:T(4,128)} %fusion.61) | copy-start | bytes 18436
  104.6 12.6 %copy-start.9 = (bf16[3,512,512]{1,2,0:T(8,128)(2,1)S(1)}, bf16[3,512,512]{1,2,0:T(8,128)(2,1)}, u32[]{:S(2)}) copy-start(bf16[3,512,512]{1,2,0:T(8,128)(2,1)} %get-tuple-element.21) | copy-start | bytes 4718596
  104.6 12.6 %copy-start.10 = (f32[3,512]{1,0:T(4,128)S(1)}, f32[3,512]{1,0:T(4,128)}, u32[]{:S(2)}) copy-start(f32[3,512]{1,0:T(4,128)} %get-tuple-element.20) | copy-start | bytes 18436
  114.5 6.7 %collective-permute-start.1 = (bf16[1,256,128]{2,1,0:T(8,128)(2,1)}, bf16[1,256,128]{2,1,0:T(8,128)(2,1)S(1)}, u32[]{:S(2)}, u32[]{:S(2)}) collective-permute-start(bf16[1,256,128]{2,1,0:T(8,128)(2,1)} %get-tuple-element.7), channel_id=1, source_target_pairs={{0,15},{1,14},{2,13},{3,12},{4,11},{5,10},{6,9},{7,8},{8,7},{9,6},... | collective-permute-start | bytes 196616 | tf_op jit(solution)/shard_map/ppermute | solution.py:105
  117.2 4.0 %copy-start.3 = (bf16[1,256,128]{2,1,0:T(8,128)(2,1)S(1)}, bf16[1,256,128]{2,1,0:T(8,128)(2,1)}, u32[]{:S(2)}) copy-start(bf16[1,256,128]{2,1,0:T(8,128)(2,1)} %get-tuple-element.8) | copy-start | bytes 196612
  117.2 4.0 %copy-start.4 = (bf16[1,256,128]{2,1,0:T(8,128)(2,1)S(1)}, bf16[1,256,128]{2,1,0:T(8,128)(2,1)}, u32[]{:S(2)}) copy-start(bf16[1,256,128]{2,1,0:T(8,128)(2,1)} %get-tuple-element.6) | copy-start | bytes 196612
Sparse Core Ops, SparseCore 0:
  9.9 84.7 all-gather.1

commit v12 on v10

--- a/solution.py
+++ b/solution.py
@@ -20,9 +20,11 @@
 
     def update(j, carry, masked):
         m_prev, l_prev, acc = carry
-        first = pl.multiple_of(j * block, block)
+        per = block // k_ref.shape[1]
+        first = pl.multiple_of(j * per, per)
+        keys = k_ref[pl.ds(first, per)].reshape(block, k_ref.shape[2])
         scores = lax.dot_general(
-            q_ref[0, 0], k_ref[0, pl.ds(first, block), :], (((1,), (1,)), ((), ())),
+            q_ref[0, 0], keys, (((1,), (1,)), ((), ())),
             preferred_element_type=jnp.float32,
         ) * scale
         if masked:
@@ -34,7 +36,7 @@
         weights = jnp.exp(scores - m_new)
         l_new = l_prev * shrink + jnp.sum(weights, axis=1, keepdims=True)
         moved = jnp.dot(
-            weights.astype(jnp.bfloat16), v_ref[0, pl.ds(first, block), :],
+            weights.astype(jnp.bfloat16), v_ref[pl.ds(first, per)].reshape(block, v_ref.shape[2]),
             preferred_element_type=jnp.float32,
         )
         return m_new, l_new, acc * shrink + moved
@@ -59,7 +61,8 @@
 
 def dense_flash(info, queries, stacked):
     parts, heads, rows, width = queries.shape
-    length = stacked.shape[2]
+    pieces, kinds, heads_kv, sub, width_kv = stacked.shape
+    length = pieces * sub
     block = KEY_BLOCK
     scale = 1.0 / math.sqrt(width)
     return pl.pallas_call(
@@ -70,8 +73,8 @@
             grid=(heads, parts),
             in_specs=[
                 pl.BlockSpec((1, 1, rows, width), lambda h, p, c: (p, h, 0, 0)),
-                pl.BlockSpec((None, 1, length, width), lambda h, p, c: (0, h, 0, 0)),
-                pl.BlockSpec((None, 1, length, width), lambda h, p, c: (1, h, 0, 0)),
+                pl.BlockSpec((pieces, None, None, sub, width), lambda h, p, c: (0, 0, h, 0, 0)),
+                pl.BlockSpec((pieces, None, None, sub, width), lambda h, p, c: (0, 1, h, 0, 0)),
             ],
             out_specs=[pl.BlockSpec((1, rows, width), lambda h, p, c: (h, 0, 0))] * 2,
         ),
@@ -92,7 +95,7 @@
     half = tok_rows // 2
     swap = [(i, count - 1 - i) for i in range(count)]
     stacked = jnp.stack([jnp.swapaxes(keys, 0, 1), jnp.swapaxes(values, 0, 1)], axis=0)
-    gathered = lax.all_gather(stacked, "seq", axis=2, tiled=True)
+    gathered = lax.all_gather(stacked, "seq", axis=0)
     rows_first = jnp.swapaxes(queries, 0, 1)
     lent = lax.ppermute(rows_first[:, half:], "seq", swap)
     both = jnp.stack([rows_first[:, :half], lent], axis=0)

time: 128 us -> 128 us (level)
  no operation moved by 1% of the time
where the time goes in v12:
time: 128 us
  waiting for transfers between devices  41.7 us (33%)
  blocking collectives  23.2 us (18%)
  Pallas kernels  16 us (12%)
  between operations  14.2 us (11%)
  starting transfers between devices  14.1 us (11%)
  other arithmetic  8.56 us (7%)
  matrix products  5.97 us (5%)
  local copies, waits for them, and re-layouts  4.24 us (3%)
    ppermute x1, waiting for transfers between devices, dense_heads(): lent = lax.ppermute(rows_first[:, half:], 'seq', swap)  29.3 us
    all_gather x1, blocking collectives, sparse_heads(): picked_kv = lax.all_gather(own, 'seq', axis=2, tiled=True)  23.2 us
    pallas_call x1, Pallas kernels, dense_flash(): pl.pallas_call(functools.partial(flash_kernel, scale=scale, block=block),...  16 us
    all_to_all x1, starting transfers between devices, sparse_heads(): arrived = lax.all_to_all(pieces, 'seq', 2, 2, tiled=True)  9.98 us
    ppermute x1, waiting for transfers between devices, dense_heads(): returned = lax.ppermute(theirs, 'seq', swap)  6.32 us
    all_gather x1, waiting for transfers between devices, dense_heads(): gathered = lax.all_gather(stacked, 'seq', axis=0)  5.98 us
    sub x1, other arithmetic, attend_ranked(): weights = jnp.where(visible, jnp.exp(scores - leading), 0.0)  4.66 us
    ppermute x1, starting transfers between devices, dense_heads(): lent = lax.ppermute(rows_first[:, half:], 'seq', swap)  2.93 us
  transfers between devices with their start and end apart: 4, of which 3 were waited for; matrix products, arithmetic and copies ran while one was open for 12% of the time, Pallas kernels for 0%

profile of v12, /device:TPU:1, one launch (start us, length us, event | category | flops | bytes accessed | tf_op | source)
XLA Modules:
  0.0 127.9 jit_solution(7724559457918429138)
XLA Ops:
  7.2 0.0 copy-start
  7.2 0.0 copy-start.4
  7.2 0.0 copy-start.6
  7.2 0.0 all-gather.3.cloned.1.call-start
  7.2 1.2 copy_bitcast_fusion
  8.4 0.9 pad_maximum_fusion.1
  9.3 0.0 all-gather.3.cloned.1.call-update
  9.3 1.7 %fusion.42 = bf16[3,512,128]{2,1,0:T(8,128)(2,1)S(1)} fusion(bf16[512,3,128]{2,0,1:T(8,128)(2,1)} %param.13, s32[512]{0:T(512)S(1)} %iota_add_fusion, s32[3,512]{1,0:T(4,128)} %param.15), kind=kOutput, calls=%fused_computation.34 | convolution fusion | flops 202309632 | bytes 794624 | tf_op jit(solution)/shard_map/ent,ted->end/dot_general | solution.py:135
  11.0 0.0 copy-done.4
  11.0 0.0 copy-done.6
  11.0 0.0 copy-start.2
  11.0 0.6 fusion.39
  11.7 0.0 copy-start.7
  11.7 0.1 pad_maximum_fusion
  11.8 1.1 copy.23
  12.8 10.0 %all-to-all-start = ((bf16[2,3,16,32,128]{4,3,1,0,2:T(8,128)(2,1)}), bf16[2,3,16,32,128]{4,3,1,0,2:T(8,128)(2,1)S(1)}, u32[]{:S(2)}, u32[]{:S(2)}) async-start(bf16[2,3,16,32,128]{4,3,1,0,2:T(8,128)(2,1)} %copy.23), calls=%async_computation | async-start | bytes 1572864 | tf_op jit(solution)/shard_map/all_to_all | solution.py:143
  22.8 0.0 copy-done.2
  22.9 2.9 %collective-permute-start = (bf16[2,256,128]{2,1,0:T(8,128)(2,1)S(1)}, bf16[2,256,128]{2,1,0:T(8,128)(2,1)S(1)}, u32[]{:S(2)}, u32[]{:S(2)}) collective-permute-start(bf16[2,256,128]{2,1,0:T(8,128)(2,1)S(1)} %get-tuple-element.13), channel_id=1, source_target_pairs={{0,15},{1,14},{2,13},{3,12},{4,11},{5,10},{6,9},{7,8},{8,7},{9,6},... | collective-permute-start | bytes 393224 | tf_op jit(solution)/shard_map/ppermute | solution.py:100
  25.8 0.1 multiply_subtract_fusion
  25.9 0.0 copy-done.7
  25.9 0.6 fusion.3
  26.6 0.6 fusion.60
  27.2 0.6 pad_add_fusion.1.info_ref
  27.8 0.8 iota_compare_fusion
  28.6 29.3 %collective-permute-done = bf16[2,256,128]{2,1,0:T(8,128)(2,1)S(1)} collective-permute-done((bf16[2,256,128]{2,1,0:T(8,128)(2,1)S(1)}, bf16[2,256,128]{2,1,0:T(8,128)(2,1)S(1)}, u32[]{:S(2)}, u32[]{:S(2)}) %collective-permute-start) | collective-permute-done | bytes 131104 | tf_op jit(solution)/shard_map/ppermute | solution.py:100
  57.9 0.7 pad_maximum_fusion.2.q_ref
  58.7 0.0 all-to-all-done
  58.7 0.1 reduce_sum.21
  58.8 23.2 %all_gather.11 = bf16[2,3,512,128]{3,2,1,0:T(8,128)(2,1)} all-gather(bf16[2,3,32,128]{3,2,1,0:T(8,128)(2,1)S(1)} %reduce_sum.21), channel_id=1, replica_groups=mesh['dp'=4,'head'=4,'seq'=16] {'seq'}, dimensions={2}, use_global_device_ids=true | all-gather | bytes 835584 | tf_op jit(solution)/shard_map/all_gather | solution.py:145
  82.0 0.0 copy-done
  82.0 2.1 %fusion.52 = f32[3,512,512]{1,2,0:T(8,128)S(1)} fusion(bf16[512,3,128]{2,0,1:T(8,128)(2,1)S(1)} %copy-done, s32[512]{0:T(512)S(1)} %iota_add_fusion, s32[3,512]{1,0:T(4,128)S(1)} %copy-done.4, bf16[2,3,512,128]{3,2,1,0:T(8,128)(2,1)} %all_gather.11), kind=kOutput, calls=%fused_computation.37 | convolution fusion | flops 403636224 | bytes 3940352 | tf_op jit(solution)/shard_map/erd,ekd->erk/dot_general | solution.py:115
  84.1 4.7 %fusion.64 = (f32[3,512]{1,0:T(4,128)}, bf16[3,512,512]{1,2,0:T(8,128)(2,1)}) fusion(f32[3,512,512]{1,2,0:T(8,128)S(1)} %fusion.52, pred[512,512]{0,1:T(8,128)(4,1)} %iota_compare_fusion), kind=kOutput, calls=%fused_computation.66 | output fusion | flops 6291967 | bytes 4986880 | tf_op jit(solution)/shard_map/sub | solution.py:119
  88.8 6.0 %all-gather.3.cloned.1.call-done = bf16[32,2,512,128]{3,2,1,0:T(8,128)(2,1)} async-done(((bf16[2,2,512,128]{3,2,1,0:T(8,128)(2,1)}), bf16[32,2,512,128]{3,2,1,0:T(8,128)(2,1)}) %all-gather.3.cloned.1.call-update) | async-done | bytes 8388624 | tf_op jit(solution)/shard_map/all_gather | solution.py:98
  94.7 0.0 copy-start.1
  94.7 0.0 copy-start.8
  94.7 0.0 copy-start.9
  94.7 16.0 %shard_map.95 = (bf16[2,256,128]{2,1,0:T(8,128)(2,1)}, bf16[2,256,128]{2,1,0:T(8,128)(2,1)}) custom-call(s32[4]{0:T(128)} %pad_add_fusion.1.info_ref, bf16[2,2,256,128]{3,2,1,0:T(8,128)(2,1)} %pad_maximum_fusion.2.q_ref, bf16[16,2,2,512,128]{4,3,2,1,0:T(8,128)(2,1)} %bitcast.43, bf16[16,2,2,512,128]{4,3,2,1,0:T(8,128)(2,1)} %bitcast.44), custom_call_target="tpu_custom_call" | custom-call | flops 2147483648 | bytes 4718592 | tf_op jit(solution)/shard_map/pallas_call | solution.py:68
  110.8 1.1 collective-permute-start.1
  111.9 0.0 copy-done.1
  111.9 0.0 copy-done.5
  111.9 0.0 copy-done.8
  111.9 0.0 copy-done.9
  111.9 0.0 copy-start.3
  111.9 0.9 fusion.48
  112.8 0.9 copy.20
  113.8 6.3 %collective-permute-done.1 = bf16[2,256,128]{2,1,0:T(8,128)(2,1)S(1)} collective-permute-done((bf16[2,256,128]{2,1,0:T(8,128)(2,1)}, bf16[2,256,128]{2,1,0:T(8,128)(2,1)S(1)}, u32[]{:S(2)}, u32[]{:S(2)}) %collective-permute-start.1) | collective-permute-done | bytes 131104 | tf_op jit(solution)/shard_map/ppermute | solution.py:106
  120.1 0.0 copy-done.3
  120.1 1.0 copy.19
  (5 shorter events, 0.1 us)
Async XLA Ops:
  7.2 74.8 %copy-start = (bf16[512,3,128]{2,0,1:T(8,128)(2,1)S(1)}, bf16[512,3,128]{2,0,1:T(8,128)(2,1)}, u32[]{:S(2)}) copy-start(bf16[512,3,128]{2,0,1:T(8,128)(2,1)} %param.11) | copy-start | bytes 1179652
  7.2 3.8 %copy-start.4 = (s32[3,512]{1,0:T(4,128)S(1)}, s32[3,512]{1,0:T(4,128)}, u32[]{:S(2)}) copy-start(s32[3,512]{1,0:T(4,128)} %param.15) | copy-start | bytes 18436
  7.2 3.8 %copy-start.6 = (bf16[512,3,128]{2,0,1:T(8,128)(2,1)S(1)}, bf16[512,3,128]{2,0,1:T(8,128)(2,1)}, u32[]{:S(2)}) copy-start(bf16[512,3,128]{2,0,1:T(8,128)(2,1)} %param.12) | copy-start | bytes 1179652
  7.2 87.5 %all-gather.3.cloned.1.call-start = ((), (), s32[]{:S(2)}) async-start(), calls=%async_computation.1 | async-start | bytes 8912896 | tf_op jit(solution)/shard_map/all_gather | solution.py:98
  11.0 11.8 %copy-start.2 = (bf16[512,2,128]{2,1,0:T(2,128)(2,1)S(1)}, bf16[512,2,128]{2,1,0:T(2,128)(2,1)}, u32[]{:S(2)}) copy-start(bf16[512,2,128]{2,1,0:T(2,128)(2,1)} %param.8) | copy-start | bytes 786436
  11.7 14.2 %copy-start.7 = (bf16[3,512]{1,0:T(4,128)(2,1)S(1)}, bf16[3,512]{1,0:T(4,128)(2,1)}, u32[]{:S(2)}) copy-start(bf16[3,512]{1,0:T(4,128)(2,1)} %param.14) | copy-start | bytes 9220
  12.8 45.8 %all-to-all-start = ((bf16[2,3,16,32,128]{4,3,1,0,2:T(8,128)(2,1)}), bf16[2,3,16,32,128]{4,3,1,0,2:T(8,128)(2,1)S(1)}, u32[]{:S(2)}, u32[]{:S(2)}) async-start(bf16[2,3,16,32,128]{4,3,1,0,2:T(8,128)(2,1)} %copy.23), calls=%async_computation | async-start | bytes 1572864 | tf_op jit(solution)/shard_map/all_to_all | solution.py:143
  22.9 35.0 %collective-permute-start = (bf16[2,256,128]{2,1,0:T(8,128)(2,1)S(1)}, bf16[2,256,128]{2,1,0:T(8,128)(2,1)S(1)}, u32[]{:S(2)}, u32[]{:S(2)}) collective-permute-start(bf16[2,256,128]{2,1,0:T(8,128)(2,1)S(1)} %get-tuple-element.13), channel_id=1, source_target_pairs={{0,15},{1,14},{2,13},{3,12},{4,11},{5,10},{6,9},{7,8},{8,7},{9,6},... | collective-permute-start | bytes 393224 | tf_op jit(solution)/shard_map/ppermute | solution.py:100
  94.7 17.2 %copy-start.1 = (bf16[2,3,512,128]{3,2,1,0:T(8,128)(2,1)S(1)}, bf16[2,3,512,128]{3,2,1,0:T(8,128)(2,1)}, u32[]{:S(2)}) copy-start(bf16[2,3,512,128]{3,2,1,0:T(8,128)(2,1)} %all_gather.11) | copy-start | bytes 2359300
  94.7 17.2 %copy-start.5 = (f32[3,512]{1,0:T(4,128)S(1)}, f32[3,512]{1,0:T(4,128)}, u32[]{:S(2)}) copy-start(f32[3,512]{1,0:T(4,128)} %fusion.60) | copy-start | bytes 18436
  94.7 17.2 %copy-start.8 = (bf16[3,512,512]{1,2,0:T(8,128)(2,1)S(1)}, bf16[3,512,512]{1,2,0:T(8,128)(2,1)}, u32[]{:S(2)}) copy-start(bf16[3,512,512]{1,2,0:T(8,128)(2,1)} %get-tuple-element.15) | copy-start | bytes 4718596
  94.7 17.2 %copy-start.9 = (f32[3,512]{1,0:T(4,128)S(1)}, f32[3,512]{1,0:T(4,128)}, u32[]{:S(2)}) copy-start(f32[3,512]{1,0:T(4,128)} %get-tuple-element.14) | copy-start | bytes 18436
  110.8 9.3 %collective-permute-start.1 = (bf16[2,256,128]{2,1,0:T(8,128)(2,1)}, bf16[2,256,128]{2,1,0:T(8,128)(2,1)S(1)}, u32[]{:S(2)}, u32[]{:S(2)}) collective-permute-start(bf16[2,256,128]{2,1,0:T(8,128)(2,1)} %get-tuple-element.5), channel_id=1, source_target_pairs={{0,15},{1,14},{2,13},{3,12},{4,11},{5,10},{6,9},{7,8},{8,7},{9,6},... | collective-permute-start | bytes 393224 | tf_op jit(solution)/shard_map/ppermute | solution.py:106
  111.9 8.2 %copy-start.3 = (bf16[2,256,128]{2,1,0:T(8,128)(2,1)S(1)}, bf16[2,256,128]{2,1,0:T(8,128)(2,1)}, u32[]{:S(2)}) copy-start(bf16[2,256,128]{2,1,0:T(8,128)(2,1)} %get-tuple-element.4) | copy-start | bytes 393220
Sparse Core Ops, SparseCore 0:
  9.9 84.8 all-gather.2

commit v13 on v12

--- a/solution.py
+++ b/solution.py
@@ -142,7 +142,18 @@
     pieces = local_kv.reshape(kinds, heads_, count, chosen // count, width_)
     arrived = lax.all_to_all(pieces, "seq", 2, 2, tiled=True)
     own = jnp.sum(arrived.astype(jnp.float32), axis=2).astype(jnp.bfloat16)
-    picked_kv = lax.all_gather(own, "seq", axis=2, tiled=True)
+    me = lax.axis_index("seq")
+    picked_kv = own
+    step = 1
+    while step < count:
+        arrived_part = lax.ppermute(picked_kv, "seq", [(i, i ^ step) for i in range(count)])
+        low = (me & step) == 0
+        picked_kv = jnp.where(
+            low,
+            jnp.concatenate([picked_kv, arrived_part], axis=2),
+            jnp.concatenate([arrived_part, picked_kv], axis=2),
+        )
+        step *= 2
     picked_q = pick(queries)
     gate_rows = jnp.einsum("ent,et->en", one_hot, gate_logit, preferred_element_type=jnp.float32)
     results = attend_ranked(picked_q, picked_kv[0], picked_kv[1], gate_rows)

time: 128 us -> 153 us (1.20)
  waiting for transfers between devices: 41.7 us -> 85.3 us
  blocking collectives: 23.2 us -> 0 us
  starting transfers between devices: 14.1 us -> 16.9 us
    ppermute x0 -> x4, waiting for transfers between devices: none -> 49.6 us  [sparse_heads(): lax.ppermute(picked_kv, 'seq', [(i, i ^ step) for i in range(count)])]
    all_to_all x1, waiting for transfers between devices: 0.01 us -> 29.6 us  [sparse_heads(): arrived = lax.all_to_all(pieces, 'seq', 2, 2, tiled=True)]
    ppermute x1, waiting for transfers between devices: 29.3 us -> 0.01 us  [dense_heads(): lent = lax.ppermute(rows_first[:, half:], 'seq', swap)]
    all_gather x1 -> x0, blocking collectives: 23.2 us -> none  [sparse_heads(): picked_kv = lax.all_gather(own, 'seq', axis=2, tiled=True)]
    all_gather x1, waiting for transfers between devices: 5.98 us -> 0.01 us  [dense_heads(): gathered = lax.all_gather(stacked, 'seq', axis=0)]
    ppermute x0 -> x4, starting transfers between devices: none -> 4.15 us  [sparse_heads(): lax.ppermute(picked_kv, 'seq', [(i, i ^ step) for i in range(count)])]
    ppermute x1, starting transfers between devices: 2.93 us -> 0.57 us  [dense_heads(): lent = lax.ppermute(rows_first[:, half:], 'seq', swap)]
  transfers between devices with their start and end apart: 4 -> 8, of which waited for: 3 -> 6; matrix products, arithmetic and copies ran while one was open for 12% -> 11% of each run, Pallas kernels for 0% -> 0%
where the time goes in v13:
time: 153 us; the launch traced here: 152 us
  waiting for transfers between devices  85.3 us (56%)
  starting transfers between devices  16.9 us (11%)
  Pallas kernels  16 us (10%)
  between operations  14.2 us (9%)
  other arithmetic  9.83 us (6%)
  matrix products  5.92 us (4%)
  local copies, waits for them, and re-layouts  4.24 us (3%)
    ppermute x4, waiting for transfers between devices, sparse_heads(): lax.ppermute(picked_kv, 'seq', [(i, i ^ step) for i in range(count)])  49.6 us
    all_to_all x1, waiting for transfers between devices, sparse_heads(): arrived = lax.all_to_all(pieces, 'seq', 2, 2, tiled=True)  29.6 us
    pallas_call x1, Pallas kernels, dense_flash(): pl.pallas_call(functools.partial(flash_kernel, scale=scale, block=block),...  16 us
    all_to_all x1, starting transfers between devices, sparse_heads(): arrived = lax.all_to_all(pieces, 'seq', 2, 2, tiled=True)  9.98 us
    ppermute x1, waiting for transfers between devices, dense_heads(): returned = lax.ppermute(theirs, 'seq', swap)  6.03 us
    sub x1, other arithmetic, attend_ranked(): weights = jnp.where(visible, jnp.exp(scores - leading), 0.0)  4.67 us
    ppermute x4, starting transfers between devices, sparse_heads(): lax.ppermute(picked_kv, 'seq', [(i, i ^ step) for i in range(count)])  4.15 us
  transfers between devices with their start and end apart: 8, of which 6 were waited for; matrix products, arithmetic and copies ran while one was open for 11% of the time, Pallas kernels for 0%

profile of v13, /device:TPU:1, one launch (start us, length us, event | category | flops | bytes accessed | tf_op | source)
XLA Modules:
  0.0 152.5 jit_solution(9380938136853845697)
XLA Ops:
  7.2 0.0 copy-start
  7.2 0.0 copy-start.4
  7.2 0.0 copy-start.6
  7.2 0.0 all-gather.3.cloned.1.call-start
  7.2 1.2 copy_bitcast_fusion
  8.4 0.8 pad_maximum_fusion.1
  9.3 0.0 all-gather.3.cloned.1.call-update
  9.3 1.7 %fusion.42 = bf16[3,512,128]{2,1,0:T(8,128)(2,1)S(1)} fusion(bf16[512,3,128]{2,0,1:T(8,128)(2,1)} %param.13, s32[512]{0:T(512)S(1)} %iota_add_fusion, s32[3,512]{1,0:T(4,128)} %param.15), kind=kOutput, calls=%fused_computation.34 | convolution fusion | flops 202309632 | bytes 794624 | tf_op jit(solution)/shard_map/ent,ted->end/dot_general | solution.py:135
  11.0 0.0 copy-done.4
  11.0 0.0 copy-done.6
  11.0 0.0 copy-start.2
  11.0 0.6 fusion.39
  11.7 0.0 copy-start.7
  11.7 0.1 pad_maximum_fusion
  11.8 1.1 copy.23
  12.8 10.0 %all-to-all-start = ((bf16[2,3,16,32,128]{4,3,1,0,2:T(8,128)(2,1)}), bf16[2,3,16,32,128]{4,3,1,0,2:T(8,128)(2,1)S(1)}, u32[]{:S(2)}, u32[]{:S(2)}) async-start(bf16[2,3,16,32,128]{4,3,1,0,2:T(8,128)(2,1)} %copy.23), calls=%async_computation | async-start | bytes 1572864 | tf_op jit(solution)/shard_map/all_to_all | solution.py:143
  22.8 0.0 copy-done.2
  22.9 29.6 %all-to-all-done = bf16[2,3,16,32,128]{4,3,1,0,2:T(8,128)(2,1)S(1)} async-done(((bf16[2,3,16,32,128]{4,3,1,0,2:T(8,128)(2,1)}), bf16[2,3,16,32,128]{4,3,1,0,2:T(8,128)(2,1)S(1)}, u32[]{:S(2)}, u32[]{:S(2)}) %all-to-all-start) | async-done | bytes 786464 | tf_op jit(solution)/shard_map/all_to_all | solution.py:143
  52.5 0.1 reduce_sum.21
  52.6 0.1 collective-permute-start.2
  52.7 0.6 collective-permute-start
  53.3 0.6 collective-permute-done.2
  54.0 1.2 collective-permute-start.3
  55.2 0.0 copy-done.7
  55.2 0.6 fusion.3
  55.8 10.3 %collective-permute-done.3 = bf16[2,3,64,128]{3,2,1,0:T(8,128)(2,1)S(1)} collective-permute-done((bf16[2,3,64,128]{3,2,1,0:T(8,128)(2,1)S(1)}, bf16[2,3,64,128]{3,2,1,0:T(8,128)(2,1)S(1)}, u32[]{:S(2)}, u32[]{:S(2)}) %collective-permute-start.3) | collective-permute-done | bytes 98336 | tf_op jit(solution)/shard_map/ppermute | solution.py:149
  66.1 0.1 maximum_select_fusion.2
  66.1 0.6 collective-permute-start.4
  66.8 0.6 fusion.60
  67.4 14.5 %collective-permute-done.4 = bf16[2,3,128,128]{3,2,1,0:T(8,128)(2,1)S(1)} collective-permute-done((bf16[2,3,128,128]{3,2,1,0:T(8,128)(2,1)S(1)}, bf16[2,3,128,128]{3,2,1,0:T(8,128)(2,1)S(1)}, u32[]{:S(2)}, u32[]{:S(2)}) %collective-permute-start.4) | collective-permute-done | bytes 196640 | tf_op jit(solution)/shard_map/ppermute | solution.py:149
  81.9 0.1 maximum_select_fusion.1
  82.0 2.2 %collective-permute-start.5 = (bf16[2,3,256,128]{3,2,1,0:T(8,128)(2,1)S(1)}, bf16[2,3,256,128]{3,2,1,0:T(8,128)(2,1)S(1)}, u32[]{:S(2)}, u32[]{:S(2)}) collective-permute-start(bf16[2,3,256,128]{3,2,1,0:T(8,128)(2,1)S(1)} %maximum_select_fusion.1), channel_id=1, source_target_pairs={{0,8},{1,9},{2,10},{3,11},{4,12},{5,13},{6,14},{7,15},{8,0},{9,1},... | collective-permute-start | bytes 1179656 | tf_op jit(solution)/shard_map/ppermute | solution.py:149
  84.2 0.1 multiply_subtract_fusion
  84.3 0.6 pad_add_fusion.1.info_ref
  84.9 0.8 iota_compare_fusion
  85.7 0.0 collective-permute-done
  85.7 0.7 pad_maximum_fusion.2.q_ref
  86.4 24.2 %collective-permute-done.5 = bf16[2,3,256,128]{3,2,1,0:T(8,128)(2,1)S(1)} collective-permute-done((bf16[2,3,256,128]{3,2,1,0:T(8,128)(2,1)S(1)}, bf16[2,3,256,128]{3,2,1,0:T(8,128)(2,1)S(1)}, u32[]{:S(2)}, u32[]{:S(2)}) %collective-permute-start.5) | collective-permute-done | bytes 393248 | tf_op jit(solution)/shard_map/ppermute | solution.py:149
  110.7 1.1 maximum_select_fusion
  111.8 2.0 %fusion.52 = f32[3,512,512]{1,2,0:T(8,128)S(1)} fusion(bf16[512,3,128]{2,0,1:T(8,128)(2,1)S(1)} %copy-done, s32[512]{0:T(512)S(1)} %iota_add_fusion, s32[3,512]{1,0:T(4,128)S(1)} %copy-done.4, bf16[2,3,512,128]{3,2,1,0:T(8,128)(2,1)} %maximum_select_fusion), kind=kOutput, calls=%fused_computation.37 | convolution fusion | flops 403636224 | bytes 3940352 | tf_op jit(solution)/shard_map/erd,ekd->erk/dot_general | solution.py:115
  113.8 4.7 %fusion.64 = (f32[3,512]{1,0:T(4,128)}, bf16[3,512,512]{1,2,0:T(8,128)(2,1)}) fusion(f32[3,512,512]{1,2,0:T(8,128)S(1)} %fusion.52, pred[512,512]{0,1:T(8,128)(4,1)} %iota_compare_fusion), kind=kOutput, calls=%fused_computation.70 | output fusion | flops 6291967 | bytes 4986880 | tf_op jit(solution)/shard_map/sub | solution.py:119
  118.5 16.0 %shard_map.95 = (bf16[2,256,128]{2,1,0:T(8,128)(2,1)}, bf16[2,256,128]{2,1,0:T(8,128)(2,1)}) custom-call(s32[4]{0:T(128)} %pad_add_fusion.1.info_ref, bf16[2,2,256,128]{3,2,1,0:T(8,128)(2,1)} %pad_maximum_fusion.2.q_ref, bf16[16,2,2,512,128]{4,3,2,1,0:T(8,128)(2,1)} %bitcast.43, bf16[16,2,2,512,128]{4,3,2,1,0:T(8,128)(2,1)} %bitcast.44), custom_call_target="tpu_custom_call" | custom-call | flops 2147483648 | bytes 4718592 | tf_op jit(solution)/shard_map/pallas_call | solution.py:68
  134.5 2.2 %collective-permute-start.1 = (bf16[2,256,128]{2,1,0:T(8,128)(2,1)}, bf16[2,256,128]{2,1,0:T(8,128)(2,1)S(1)}, u32[]{:S(2)}, u32[]{:S(2)}) collective-permute-start(bf16[2,256,128]{2,1,0:T(8,128)(2,1)} %get-tuple-element.5), channel_id=1, source_target_pairs={{0,15},{1,14},{2,13},{3,12},{4,11},{5,10},{6,9},{7,8},{8,7},{9,6},... | collective-permute-start | bytes 393224 | tf_op jit(solution)/shard_map/ppermute | solution.py:106
  136.7 0.0 copy-done.5
  136.8 0.9 fusion.48
  137.7 0.9 copy.20
  138.6 6.0 %collective-permute-done.1 = bf16[2,256,128]{2,1,0:T(8,128)(2,1)S(1)} collective-permute-done((bf16[2,256,128]{2,1,0:T(8,128)(2,1)}, bf16[2,256,128]{2,1,0:T(8,128)(2,1)S(1)}, u32[]{:S(2)}, u32[]{:S(2)}) %collective-permute-start.1) | collective-permute-done | bytes 131104 | tf_op jit(solution)/shard_map/ppermute | solution.py:106
  144.7 1.0 copy.19
  (16 shorter events, 0.1 us)
Async XLA Ops:
  7.2 104.6 %copy-start = (bf16[512,3,128]{2,0,1:T(8,128)(2,1)S(1)}, bf16[512,3,128]{2,0,1:T(8,128)(2,1)}, u32[]{:S(2)}) copy-start(bf16[512,3,128]{2,0,1:T(8,128)(2,1)} %param.11) | copy-start | bytes 1179652
  7.2 3.8 %copy-start.4 = (s32[3,512]{1,0:T(4,128)S(1)}, s32[3,512]{1,0:T(4,128)}, u32[]{:S(2)}) copy-start(s32[3,512]{1,0:T(4,128)} %param.15) | copy-start | bytes 18436
  7.2 3.8 %copy-start.6 = (bf16[512,3,128]{2,0,1:T(8,128)(2,1)S(1)}, bf16[512,3,128]{2,0,1:T(8,128)(2,1)}, u32[]{:S(2)}) copy-start(bf16[512,3,128]{2,0,1:T(8,128)(2,1)} %param.12) | copy-start | bytes 1179652
  7.2 111.3 %all-gather.3.cloned.1.call-start = ((), (), s32[]{:S(2)}) async-start(), calls=%async_computation.1 | async-start | bytes 8912896 | tf_op jit(solution)/shard_map/all_gather | solution.py:98
  11.0 11.8 %copy-start.2 = (bf16[512,2,128]{2,1,0:T(2,128)(2,1)S(1)}, bf16[512,2,128]{2,1,0:T(2,128)(2,1)}, u32[]{:S(2)}) copy-start(bf16[512,2,128]{2,1,0:T(2,128)(2,1)} %param.8) | copy-start | bytes 786436
  11.7 43.5 %copy-start.7 = (bf16[3,512]{1,0:T(4,128)(2,1)S(1)}, bf16[3,512]{1,0:T(4,128)(2,1)}, u32[]{:S(2)}) copy-start(bf16[3,512]{1,0:T(4,128)(2,1)} %param.14) | copy-start | bytes 9220
  12.8 39.7 %all-to-all-start = ((bf16[2,3,16,32,128]{4,3,1,0,2:T(8,128)(2,1)}), bf16[2,3,16,32,128]{4,3,1,0,2:T(8,128)(2,1)S(1)}, u32[]{:S(2)}, u32[]{:S(2)}) async-start(bf16[2,3,16,32,128]{4,3,1,0,2:T(8,128)(2,1)} %copy.23), calls=%async_computation | async-start | bytes 1572864 | tf_op jit(solution)/shard_map/all_to_all | solution.py:143
  52.6 1.3 collective-permute-start.2
  52.7 33.0 %collective-permute-start = (bf16[2,256,128]{2,1,0:T(8,128)(2,1)S(1)}, bf16[2,256,128]{2,1,0:T(8,128)(2,1)S(1)}, u32[]{:S(2)}, u32[]{:S(2)}) collective-permute-start(bf16[2,256,128]{2,1,0:T(8,128)(2,1)S(1)} %get-tuple-element.13), channel_id=1, source_target_pairs={{0,15},{1,14},{2,13},{3,12},{4,11},{5,10},{6,9},{7,8},{8,7},{9,6},... | collective-permute-start | bytes 393224 | tf_op jit(solution)/shard_map/ppermute | solution.py:100
  54.0 12.1 %collective-permute-start.3 = (bf16[2,3,64,128]{3,2,1,0:T(8,128)(2,1)S(1)}, bf16[2,3,64,128]{3,2,1,0:T(8,128)(2,1)S(1)}, u32[]{:S(2)}, u32[]{:S(2)}) collective-permute-start(bf16[2,3,64,128]{3,2,1,0:T(8,128)(2,1)S(1)} %maximum_select_fusion.3), channel_id=1, source_target_pairs={{0,2},{1,3},{2,0},{3,1},{4,6},{5,7},{6,4},{7,5},{8,10},{9,11},{10,... | collective-permute-start | bytes 294920 | tf_op jit(solution)/shard_map/ppermute | solution.py:149
  66.1 15.8 %collective-permute-start.4 = (bf16[2,3,128,128]{3,2,1,0:T(8,128)(2,1)S(1)}, bf16[2,3,128,128]{3,2,1,0:T(8,128)(2,1)S(1)}, u32[]{:S(2)}, u32[]{:S(2)}) collective-permute-start(bf16[2,3,128,128]{3,2,1,0:T(8,128)(2,1)S(1)} %maximum_select_fusion.2), channel_id=1, source_target_pairs={{0,4},{1,5},{2,6},{3,7},{4,0},{5,1},{6,2},{7,3},{8,12},{9,13},{10,... | collective-permute-start | bytes 589832 | tf_op jit(solution)/shard_map/ppermute | solution.py:149
  82.0 28.6 %collective-permute-start.5 = (bf16[2,3,256,128]{3,2,1,0:T(8,128)(2,1)S(1)}, bf16[2,3,256,128]{3,2,1,0:T(8,128)(2,1)S(1)}, u32[]{:S(2)}, u32[]{:S(2)}) collective-permute-start(bf16[2,3,256,128]{3,2,1,0:T(8,128)(2,1)S(1)} %maximum_select_fusion.1), channel_id=1, source_target_pairs={{0,8},{1,9},{2,10},{3,11},{4,12},{5,13},{6,14},{7,15},{8,0},{9,1},... | collective-permute-start | bytes 1179656 | tf_op jit(solution)/shard_map/ppermute | solution.py:149
  118.5 18.2 %copy-start.1 = (bf16[2,3,512,128]{3,2,1,0:T(8,128)(2,1)S(1)}, bf16[2,3,512,128]{3,2,1,0:T(8,128)(2,1)}, u32[]{:S(2)}) copy-start(bf16[2,3,512,128]{3,2,1,0:T(8,128)(2,1)} %maximum_select_fusion) | copy-start | bytes 2359300
  118.5 18.2 %copy-start.5 = (f32[3,512]{1,0:T(4,128)S(1)}, f32[3,512]{1,0:T(4,128)}, u32[]{:S(2)}) copy-start(f32[3,512]{1,0:T(4,128)} %fusion.60) | copy-start | bytes 18436
  118.5 18.2 %copy-start.8 = (bf16[3,512,512]{1,2,0:T(8,128)(2,1)S(1)}, bf16[3,512,512]{1,2,0:T(8,128)(2,1)}, u32[]{:S(2)}) copy-start(bf16[3,512,512]{1,2,0:T(8,128)(2,1)} %get-tuple-element.15) | copy-start | bytes 4718596
  118.5 18.2 %copy-start.9 = (f32[3,512]{1,0:T(4,128)S(1)}, f32[3,512]{1,0:T(4,128)}, u32[]{:S(2)}) copy-start(f32[3,512]{1,0:T(4,128)} %get-tuple-element.14) | copy-start | bytes 18436
  134.5 10.1 %collective-permute-start.1 = (bf16[2,256,128]{2,1,0:T(8,128)(2,1)}, bf16[2,256,128]{2,1,0:T(8,128)(2,1)S(1)}, u32[]{:S(2)}, u32[]{:S(2)}) collective-permute-start(bf16[2,256,128]{2,1,0:T(8,128)(2,1)} %get-tuple-element.5), channel_id=1, source_target_pairs={{0,15},{1,14},{2,13},{3,12},{4,11},{5,10},{6,9},{7,8},{8,7},{9,6},... | collective-permute-start | bytes 393224 | tf_op jit(solution)/shard_map/ppermute | solution.py:106
  136.8 7.9 %copy-start.3 = (bf16[2,256,128]{2,1,0:T(8,128)(2,1)S(1)}, bf16[2,256,128]{2,1,0:T(8,128)(2,1)}, u32[]{:S(2)}) copy-start(bf16[2,256,128]{2,1,0:T(8,128)(2,1)} %get-tuple-element.4) | copy-start | bytes 393220
Sparse Core Ops, SparseCore 0:
  9.9 98.9 all-gather.2

commit v14 on v10

--- a/solution.py
+++ b/solution.py
@@ -10,6 +10,7 @@
 
 NEGATIVE = -1e30
 KEY_BLOCK = 2048
+TAIL_BLOCK = 512
 
 
 def flash_kernel(info_ref, q_ref, k_ref, v_ref, own_ref, lent_ref, *, scale, block):
@@ -18,11 +19,11 @@
     offset = info_ref[2 + part]
     rows_n = q_ref.shape[2]
 
-    def update(j, carry, masked):
+    def update(j, carry, masked, wide=block):
         m_prev, l_prev, acc = carry
         first = pl.multiple_of(j * block, block)
         scores = lax.dot_general(
-            q_ref[0, 0], k_ref[0, pl.ds(first, block), :], (((1,), (1,)), ((), ())),
+            q_ref[0, 0], k_ref[0, pl.ds(first, wide), :], (((1,), (1,)), ((), ())),
             preferred_element_type=jnp.float32,
         ) * scale
         if masked:
@@ -34,7 +35,7 @@
         weights = jnp.exp(scores - m_new)
         l_new = l_prev * shrink + jnp.sum(weights, axis=1, keepdims=True)
         moved = jnp.dot(
-            weights.astype(jnp.bfloat16), v_ref[0, pl.ds(first, block), :],
+            weights.astype(jnp.bfloat16), v_ref[0, pl.ds(first, wide), :],
             preferred_element_type=jnp.float32,
         )
         return m_new, l_new, acc * shrink + moved
@@ -45,7 +46,11 @@
         jnp.zeros((rows_n, q_ref.shape[3]), jnp.float32),
     )
     carry = lax.fori_loop(0, last, lambda j, c: update(j, c, False), init)
-    m_f, l_f, acc_f = update(last, carry, True)
+    widths = list(range(TAIL_BLOCK, block + 1, TAIL_BLOCK))
+    which = (offset + rows_n - 1) // TAIL_BLOCK
+    m_f, l_f, acc_f = lax.switch(
+        which, [lambda c, w=w: update(last, c, True, w) for w in widths], carry
+    )
     result = (acc_f / l_f).astype(own_ref.dtype)
 
     @pl.when(part == 0)

time: 128 us -> 127 us (level)
  no operation moved by 1% of the time
where the time goes in v14:
time: 127 us
  waiting for transfers between devices  41.2 us (32%)
  blocking collectives  23.2 us (18%)
  Pallas kernels  14.7 us (12%)
  starting transfers between devices  14.5 us (11%)
  between operations  14.2 us (11%)
  other arithmetic  8.56 us (7%)
  matrix products  5.96 us (5%)
  local copies, waits for them, and re-layouts  4.24 us (3%)
    ppermute x1, waiting for transfers between devices, dense_heads(): lent = lax.ppermute(rows_first[:, half:], 'seq', swap)  29.3 us
    all_gather x1, blocking collectives, sparse_heads(): picked_kv = lax.all_gather(own, 'seq', axis=2, tiled=True)  23.2 us
    pallas_call x1, Pallas kernels, dense_flash(): pl.pallas_call(functools.partial(flash_kernel, scale=scale, block=block),...  14.7 us
    all_to_all x1, starting transfers between devices, sparse_heads(): arrived = lax.all_to_all(pieces, 'seq', 2, 2, tiled=True)  9.98 us
    all_gather x1, waiting for transfers between devices, dense_heads(): gathered = lax.all_gather(stacked, 'seq', axis=2, tiled=True)  6 us
    ppermute x1, waiting for transfers between devices, dense_heads(): returned = lax.ppermute(theirs, 'seq', swap)  5.9 us
    sub x1, other arithmetic, attend_ranked(): weights = jnp.where(visible, jnp.exp(scores - leading), 0.0)  4.66 us
    ppermute x1, starting transfers between devices, dense_heads(): lent = lax.ppermute(rows_first[:, half:], 'seq', swap)  2.93 us
  transfers between devices with their start and end apart: 4, of which 3 were waited for; matrix products, arithmetic and copies ran while one was open for 12% of the time, Pallas kernels for 0%

profile of v14, /device:TPU:1, one launch (start us, length us, event | category | flops | bytes accessed | tf_op | source)
XLA Modules:
  0.0 126.6 jit_solution(14214227861280333995)
XLA Ops:
  7.2 0.0 copy-start
  7.2 0.0 copy-start.4
  7.2 0.0 copy-start.6
  7.2 0.0 all-gather.2.cloned.1.call-start
  7.2 1.2 copy_bitcast_fusion
  8.4 0.9 pad_maximum_fusion.1
  9.3 0.0 all-gather.2.cloned.1.call-update
  9.3 1.7 %fusion.42 = bf16[3,512,128]{2,1,0:T(8,128)(2,1)S(1)} fusion(bf16[512,3,128]{2,0,1:T(8,128)(2,1)} %param.13, s32[512]{0:T(512)S(1)} %iota_add_fusion, s32[3,512]{1,0:T(4,128)} %param.15), kind=kOutput, calls=%fused_computation.34 | convolution fusion | flops 202309632 | bytes 794624 | tf_op jit(solution)/shard_map/ent,ted->end/dot_general | solution.py:137
  11.0 0.0 copy-done.4
  11.0 0.0 copy-done.6
  11.0 0.0 copy-start.2
  11.0 0.6 fusion.39
  11.7 0.0 copy-start.7
  11.7 0.1 pad_maximum_fusion
  11.8 1.1 copy.24
  12.8 10.0 %all-to-all-start = ((bf16[2,3,16,32,128]{4,3,1,0,2:T(8,128)(2,1)}), bf16[2,3,16,32,128]{4,3,1,0,2:T(8,128)(2,1)S(1)}, u32[]{:S(2)}, u32[]{:S(2)}) async-start(bf16[2,3,16,32,128]{4,3,1,0,2:T(8,128)(2,1)} %copy.24), calls=%async_computation | async-start | bytes 1572864 | tf_op jit(solution)/shard_map/all_to_all | solution.py:145
  22.8 0.0 copy-done.2
  22.9 2.9 %collective-permute-start = (bf16[2,256,128]{2,1,0:T(8,128)(2,1)S(1)}, bf16[2,256,128]{2,1,0:T(8,128)(2,1)S(1)}, u32[]{:S(2)}, u32[]{:S(2)}) collective-permute-start(bf16[2,256,128]{2,1,0:T(8,128)(2,1)S(1)} %get-tuple-element.13), channel_id=1, source_target_pairs={{0,15},{1,14},{2,13},{3,12},{4,11},{5,10},{6,9},{7,8},{8,7},{9,6},... | collective-permute-start | bytes 393224 | tf_op jit(solution)/shard_map/ppermute | solution.py:102
  25.8 0.1 multiply_subtract_fusion
  25.9 0.0 copy-done.7
  25.9 0.6 fusion.3
  26.6 0.6 fusion.60
  27.2 0.6 pad_add_fusion.1.info_ref
  27.8 0.8 iota_compare_fusion
  28.6 29.3 %collective-permute-done = bf16[2,256,128]{2,1,0:T(8,128)(2,1)S(1)} collective-permute-done((bf16[2,256,128]{2,1,0:T(8,128)(2,1)S(1)}, bf16[2,256,128]{2,1,0:T(8,128)(2,1)S(1)}, u32[]{:S(2)}, u32[]{:S(2)}) %collective-permute-start) | collective-permute-done | bytes 131104 | tf_op jit(solution)/shard_map/ppermute | solution.py:102
  57.9 0.7 pad_maximum_fusion.2.q_ref
  58.6 0.0 all-to-all-done
  58.6 0.1 reduce_sum.21
  58.8 23.2 %all_gather.7 = bf16[2,3,512,128]{3,2,1,0:T(8,128)(2,1)} all-gather(bf16[2,3,32,128]{3,2,1,0:T(8,128)(2,1)S(1)} %reduce_sum.21), channel_id=1, replica_groups=mesh['dp'=4,'head'=4,'seq'=16] {'seq'}, dimensions={2}, use_global_device_ids=true | all-gather | bytes 835584 | tf_op jit(solution)/shard_map/all_gather | solution.py:147
  82.0 0.0 copy-done
  82.0 2.1 %fusion.52 = f32[3,512,512]{1,2,0:T(8,128)S(1)} fusion(bf16[512,3,128]{2,0,1:T(8,128)(2,1)S(1)} %copy-done, s32[512]{0:T(512)S(1)} %iota_add_fusion, s32[3,512]{1,0:T(4,128)S(1)} %copy-done.4, bf16[2,3,512,128]{3,2,1,0:T(8,128)(2,1)} %all_gather.7), kind=kOutput, calls=%fused_computation.37 | convolution fusion | flops 403636224 | bytes 3940352 | tf_op jit(solution)/shard_map/erd,ekd->erk/dot_general | solution.py:117
  84.1 4.7 %fusion.64 = (f32[3,512]{1,0:T(4,128)}, bf16[3,512,512]{1,2,0:T(8,128)(2,1)}) fusion(f32[3,512,512]{1,2,0:T(8,128)S(1)} %fusion.52, pred[512,512]{0,1:T(8,128)(4,1)} %iota_compare_fusion), kind=kOutput, calls=%fused_computation.66 | output fusion | flops 6291967 | bytes 4986880 | tf_op jit(solution)/shard_map/sub | solution.py:121
  88.7 0.0 copy-start.1
  88.7 0.0 copy-start.5
  88.7 0.0 copy-start.8
  88.7 6.0 %all-gather.2.cloned.1.call-done.k_ref.v_ref = bf16[2,2,8192,128]{3,2,1,0:T(8,128)(2,1)} async-done(((bf16[2,2,512,128]{3,2,1,0:T(8,128)(2,1)}), bf16[2,2,8192,128]{3,2,1,0:T(8,128)(2,1)}) %all-gather.2.cloned.1.call-update) | async-done | bytes 8388624 | tf_op jit(solution)/shard_map/all_gather | solution.py:100
  94.7 14.7 %shard_map.95 = (bf16[2,256,128]{2,1,0:T(8,128)(2,1)}, bf16[2,256,128]{2,1,0:T(8,128)(2,1)}) custom-call(s32[4]{0:T(128)} %pad_add_fusion.1.info_ref, bf16[2,2,256,128]{3,2,1,0:T(8,128)(2,1)} %pad_maximum_fusion.2.q_ref, bf16[2,2,8192,128]{3,2,1,0:T(8,128)(2,1)} %all-gather.2.cloned.1.call-done.k_ref.v_ref, ...), custom_call_target="tpu_custom_call" | custom-call | flops 2147483648 | bytes 4718592 | tf_op jit(solution)/shard_map/pallas_call | solution.py:70
  109.4 1.6 %collective-permute-start.1 = (bf16[2,256,128]{2,1,0:T(8,128)(2,1)}, bf16[2,256,128]{2,1,0:T(8,128)(2,1)S(1)}, u32[]{:S(2)}, u32[]{:S(2)}) collective-permute-start(bf16[2,256,128]{2,1,0:T(8,128)(2,1)} %get-tuple-element.5), channel_id=1, source_target_pairs={{0,15},{1,14},{2,13},{3,12},{4,11},{5,10},{6,9},{7,8},{8,7},{9,6},... | collective-permute-start | bytes 393224 | tf_op jit(solution)/shard_map/ppermute | solution.py:108
  111.0 0.0 copy-done.1
  111.0 0.0 copy-done.5
  111.0 0.0 copy-done.8
  111.0 0.0 copy-done.9
  111.0 0.0 copy-start.3
  111.0 0.9 fusion.48
  111.9 0.9 copy.21
  112.8 5.9 %collective-permute-done.1 = bf16[2,256,128]{2,1,0:T(8,128)(2,1)S(1)} collective-permute-done((bf16[2,256,128]{2,1,0:T(8,128)(2,1)}, bf16[2,256,128]{2,1,0:T(8,128)(2,1)S(1)}, u32[]{:S(2)}, u32[]{:S(2)}) %collective-permute-start.1) | collective-permute-done | bytes 131104 | tf_op jit(solution)/shard_map/ppermute | solution.py:108
  118.7 0.0 copy-done.3
  118.8 1.0 copy.20
  (5 shorter events, 0.1 us)
Async XLA Ops:
  7.2 74.8 %copy-start = (bf16[512,3,128]{2,0,1:T(8,128)(2,1)S(1)}, bf16[512,3,128]{2,0,1:T(8,128)(2,1)}, u32[]{:S(2)}) copy-start(bf16[512,3,128]{2,0,1:T(8,128)(2,1)} %param.11) | copy-start | bytes 1179652
  7.2 3.8 %copy-start.4 = (s32[3,512]{1,0:T(4,128)S(1)}, s32[3,512]{1,0:T(4,128)}, u32[]{:S(2)}) copy-start(s32[3,512]{1,0:T(4,128)} %param.15) | copy-start | bytes 18436
  7.2 3.8 %copy-start.6 = (bf16[512,3,128]{2,0,1:T(8,128)(2,1)S(1)}, bf16[512,3,128]{2,0,1:T(8,128)(2,1)}, u32[]{:S(2)}) copy-start(bf16[512,3,128]{2,0,1:T(8,128)(2,1)} %param.12) | copy-start | bytes 1179652
  7.2 87.5 %all-gather.2.cloned.1.call-start = ((), (), s32[]{:S(2)}) async-start(), calls=%async_computation.1 | async-start | bytes 8912896 | tf_op jit(solution)/shard_map/all_gather | solution.py:100
  11.0 11.8 %copy-start.2 = (bf16[512,2,128]{2,1,0:T(2,128)(2,1)S(1)}, bf16[512,2,128]{2,1,0:T(2,128)(2,1)}, u32[]{:S(2)}) copy-start(bf16[512,2,128]{2,1,0:T(2,128)(2,1)} %param.8) | copy-start | bytes 786436
  11.7 14.2 %copy-start.7 = (bf16[3,512]{1,0:T(4,128)(2,1)S(1)}, bf16[3,512]{1,0:T(4,128)(2,1)}, u32[]{:S(2)}) copy-start(bf16[3,512]{1,0:T(4,128)(2,1)} %param.14) | copy-start | bytes 9220
  12.8 45.8 %all-to-all-start = ((bf16[2,3,16,32,128]{4,3,1,0,2:T(8,128)(2,1)}), bf16[2,3,16,32,128]{4,3,1,0,2:T(8,128)(2,1)S(1)}, u32[]{:S(2)}, u32[]{:S(2)}) async-start(bf16[2,3,16,32,128]{4,3,1,0,2:T(8,128)(2,1)} %copy.24), calls=%async_computation | async-start | bytes 1572864 | tf_op jit(solution)/shard_map/all_to_all | solution.py:145
  22.9 35.0 %collective-permute-start = (bf16[2,256,128]{2,1,0:T(8,128)(2,1)S(1)}, bf16[2,256,128]{2,1,0:T(8,128)(2,1)S(1)}, u32[]{:S(2)}, u32[]{:S(2)}) collective-permute-start(bf16[2,256,128]{2,1,0:T(8,128)(2,1)S(1)} %get-tuple-element.13), channel_id=1, source_target_pairs={{0,15},{1,14},{2,13},{3,12},{4,11},{5,10},{6,9},{7,8},{8,7},{9,6},... | collective-permute-start | bytes 393224 | tf_op jit(solution)/shard_map/ppermute | solution.py:102
  88.7 22.3 %copy-start.1 = (bf16[2,3,512,128]{3,2,1,0:T(8,128)(2,1)S(1)}, bf16[2,3,512,128]{3,2,1,0:T(8,128)(2,1)}, u32[]{:S(2)}) copy-start(bf16[2,3,512,128]{3,2,1,0:T(8,128)(2,1)} %all_gather.7) | copy-start | bytes 2359300
  88.7 22.3 %copy-start.5 = (f32[3,512]{1,0:T(4,128)S(1)}, f32[3,512]{1,0:T(4,128)}, u32[]{:S(2)}) copy-start(f32[3,512]{1,0:T(4,128)} %fusion.60) | copy-start | bytes 18436
  88.7 22.3 %copy-start.8 = (bf16[3,512,512]{1,2,0:T(8,128)(2,1)S(1)}, bf16[3,512,512]{1,2,0:T(8,128)(2,1)}, u32[]{:S(2)}) copy-start(bf16[3,512,512]{1,2,0:T(8,128)(2,1)} %get-tuple-element.15) | copy-start | bytes 4718596
  88.7 22.3 %copy-start.9 = (f32[3,512]{1,0:T(4,128)S(1)}, f32[3,512]{1,0:T(4,128)}, u32[]{:S(2)}) copy-start(f32[3,512]{1,0:T(4,128)} %get-tuple-element.14) | copy-start | bytes 18436
  109.4 9.4 %collective-permute-start.1 = (bf16[2,256,128]{2,1,0:T(8,128)(2,1)}, bf16[2,256,128]{2,1,0:T(8,128)(2,1)S(1)}, u32[]{:S(2)}, u32[]{:S(2)}) collective-permute-start(bf16[2,256,128]{2,1,0:T(8,128)(2,1)} %get-tuple-element.5), channel_id=1, source_target_pairs={{0,15},{1,14},{2,13},{3,12},{4,11},{5,10},{6,9},{7,8},{8,7},{9,6},... | collective-permute-start | bytes 393224 | tf_op jit(solution)/shard_map/ppermute | solution.py:108
  111.0 7.8 %copy-start.3 = (bf16[2,256,128]{2,1,0:T(8,128)(2,1)S(1)}, bf16[2,256,128]{2,1,0:T(8,128)(2,1)}, u32[]{:S(2)}) copy-start(bf16[2,256,128]{2,1,0:T(8,128)(2,1)} %get-tuple-element.4) | copy-start | bytes 393220
Sparse Core Ops, SparseCore 0:
  9.9 84.7 all-gather.1

commit v15 on v14

--- a/solution.py
+++ b/solution.py
@@ -9,7 +9,7 @@
 from jax.sharding import PartitionSpec as P
 
 NEGATIVE = -1e30
-KEY_BLOCK = 2048
+KEY_BLOCK = 4096
 TAIL_BLOCK = 512
 
 

time: 127 us -> 127 us (level)
  no operation moved by 1% of the time
where the time goes in v15:
time: 127 us; the launch traced here: 126 us
  waiting for transfers between devices  41.4 us (33%)
  blocking collectives  23.2 us (18%)
  starting transfers between devices  14.5 us (11%)
  between operations  14.2 us (11%)
  Pallas kernels  14.1 us (11%)
  other arithmetic  8.59 us (7%)
  matrix products  5.96 us (5%)
  local copies, waits for them, and re-layouts  4.24 us (3%)
    ppermute x1, waiting for transfers between devices, dense_heads(): lent = lax.ppermute(rows_first[:, half:], 'seq', swap)  29.3 us
    all_gather x1, blocking collectives, sparse_heads(): picked_kv = lax.all_gather(own, 'seq', axis=2, tiled=True)  23.2 us
    pallas_call x1, Pallas kernels, dense_flash(): pl.pallas_call(functools.partial(flash_kernel, scale=scale, block=block),...  14.1 us
    all_to_all x1, starting transfers between devices, sparse_heads(): arrived = lax.all_to_all(pieces, 'seq', 2, 2, tiled=True)  9.98 us
    ppermute x1, waiting for transfers between devices, dense_heads(): returned = lax.ppermute(theirs, 'seq', swap)  6.08 us
    all_gather x1, waiting for transfers between devices, dense_heads(): gathered = lax.all_gather(stacked, 'seq', axis=2, tiled=True)  5.97 us
    sub x1, other arithmetic, attend_ranked(): weights = jnp.where(visible, jnp.exp(scores - leading), 0.0)  4.69 us
    ppermute x1, starting transfers between devices, dense_heads(): lent = lax.ppermute(rows_first[:, half:], 'seq', swap)  2.93 us
  transfers between devices with their start and end apart: 4, of which 3 were waited for; matrix products, arithmetic and copies ran while one was open for 12% of the time, Pallas kernels for 0%

profile of v15, /device:TPU:1, one launch (start us, length us, event | category | flops | bytes accessed | tf_op | source)
XLA Modules:
  0.0 126.2 jit_solution(14551429128382897699)
XLA Ops:
  7.2 0.0 copy-start
  7.2 0.0 copy-start.4
  7.2 0.0 copy-start.6
  7.2 0.0 all-gather.2.cloned.1.call-start
  7.2 1.2 copy_bitcast_fusion
  8.4 0.9 pad_maximum_fusion.1
  9.3 0.0 all-gather.2.cloned.1.call-update
  9.3 1.7 %fusion.42 = bf16[3,512,128]{2,1,0:T(8,128)(2,1)S(1)} fusion(bf16[512,3,128]{2,0,1:T(8,128)(2,1)} %param.13, s32[512]{0:T(512)S(1)} %iota_add_fusion, s32[3,512]{1,0:T(4,128)} %param.15), kind=kOutput, calls=%fused_computation.34 | convolution fusion | flops 202309632 | bytes 794624 | tf_op jit(solution)/shard_map/ent,ted->end/dot_general | solution.py:137
  11.0 0.0 copy-done.4
  11.0 0.0 copy-done.6
  11.0 0.0 copy-start.2
  11.0 0.6 fusion.39
  11.7 0.0 copy-start.7
  11.7 0.1 pad_maximum_fusion
  11.8 1.1 copy.24
  12.8 10.0 %all-to-all-start = ((bf16[2,3,16,32,128]{4,3,1,0,2:T(8,128)(2,1)}), bf16[2,3,16,32,128]{4,3,1,0,2:T(8,128)(2,1)S(1)}, u32[]{:S(2)}, u32[]{:S(2)}) async-start(bf16[2,3,16,32,128]{4,3,1,0,2:T(8,128)(2,1)} %copy.24), calls=%async_computation | async-start | bytes 1572864 | tf_op jit(solution)/shard_map/all_to_all | solution.py:145
  22.8 0.0 copy-done.2
  22.9 2.9 %collective-permute-start = (bf16[2,256,128]{2,1,0:T(8,128)(2,1)S(1)}, bf16[2,256,128]{2,1,0:T(8,128)(2,1)S(1)}, u32[]{:S(2)}, u32[]{:S(2)}) collective-permute-start(bf16[2,256,128]{2,1,0:T(8,128)(2,1)S(1)} %get-tuple-element.13), channel_id=1, source_target_pairs={{0,15},{1,14},{2,13},{3,12},{4,11},{5,10},{6,9},{7,8},{8,7},{9,6},... | collective-permute-start | bytes 393224 | tf_op jit(solution)/shard_map/ppermute | solution.py:102
  25.8 0.1 multiply_subtract_fusion
  25.9 0.0 copy-done.7
  25.9 0.6 fusion.3
  26.6 0.6 fusion.60
  27.2 0.6 pad_add_fusion.1.info_ref
  27.8 0.8 iota_compare_fusion
  28.6 29.3 %collective-permute-done = bf16[2,256,128]{2,1,0:T(8,128)(2,1)S(1)} collective-permute-done((bf16[2,256,128]{2,1,0:T(8,128)(2,1)S(1)}, bf16[2,256,128]{2,1,0:T(8,128)(2,1)S(1)}, u32[]{:S(2)}, u32[]{:S(2)}) %collective-permute-start) | collective-permute-done | bytes 131104 | tf_op jit(solution)/shard_map/ppermute | solution.py:102
  57.9 0.7 pad_maximum_fusion.2.q_ref
  58.6 0.0 all-to-all-done
  58.6 0.1 reduce_sum.21
  58.8 23.2 %all_gather.7 = bf16[2,3,512,128]{3,2,1,0:T(8,128)(2,1)} all-gather(bf16[2,3,32,128]{3,2,1,0:T(8,128)(2,1)S(1)} %reduce_sum.21), channel_id=1, replica_groups=mesh['dp'=4,'head'=4,'seq'=16] {'seq'}, dimensions={2}, use_global_device_ids=true | all-gather | bytes 835584 | tf_op jit(solution)/shard_map/all_gather | solution.py:147
  82.0 0.0 copy-done
  82.0 2.1 %fusion.52 = f32[3,512,512]{1,2,0:T(8,128)S(1)} fusion(bf16[512,3,128]{2,0,1:T(8,128)(2,1)S(1)} %copy-done, s32[512]{0:T(512)S(1)} %iota_add_fusion, s32[3,512]{1,0:T(4,128)S(1)} %copy-done.4, bf16[2,3,512,128]{3,2,1,0:T(8,128)(2,1)} %all_gather.7), kind=kOutput, calls=%fused_computation.37 | convolution fusion | flops 403636224 | bytes 3940352 | tf_op jit(solution)/shard_map/erd,ekd->erk/dot_general | solution.py:117
  84.1 4.7 %fusion.64 = (f32[3,512]{1,0:T(4,128)}, bf16[3,512,512]{1,2,0:T(8,128)(2,1)}) fusion(f32[3,512,512]{1,2,0:T(8,128)S(1)} %fusion.52, pred[512,512]{0,1:T(8,128)(4,1)} %iota_compare_fusion), kind=kOutput, calls=%fused_computation.66 | output fusion | flops 6291967 | bytes 4986880 | tf_op jit(solution)/shard_map/sub | solution.py:121
  88.8 0.0 copy-start.1
  88.8 0.0 copy-start.5
  88.8 0.0 copy-start.8
  88.8 6.0 %all-gather.2.cloned.1.call-done.k_ref.v_ref = bf16[2,2,8192,128]{3,2,1,0:T(8,128)(2,1)} async-done(((bf16[2,2,512,128]{3,2,1,0:T(8,128)(2,1)}), bf16[2,2,8192,128]{3,2,1,0:T(8,128)(2,1)}) %all-gather.2.cloned.1.call-update) | async-done | bytes 8388624 | tf_op jit(solution)/shard_map/all_gather | solution.py:100
  94.7 14.1 %shard_map.95 = (bf16[2,256,128]{2,1,0:T(8,128)(2,1)}, bf16[2,256,128]{2,1,0:T(8,128)(2,1)}) custom-call(s32[4]{0:T(128)} %pad_add_fusion.1.info_ref, bf16[2,2,256,128]{3,2,1,0:T(8,128)(2,1)} %pad_maximum_fusion.2.q_ref, bf16[2,2,8192,128]{3,2,1,0:T(8,128)(2,1)} %all-gather.2.cloned.1.call-done.k_ref.v_ref, ...), custom_call_target="tpu_custom_call" | custom-call | flops 2147483648 | bytes 4718592 | tf_op jit(solution)/shard_map/pallas_call | solution.py:70
  108.8 1.6 %collective-permute-start.1 = (bf16[2,256,128]{2,1,0:T(8,128)(2,1)}, bf16[2,256,128]{2,1,0:T(8,128)(2,1)S(1)}, u32[]{:S(2)}, u32[]{:S(2)}) collective-permute-start(bf16[2,256,128]{2,1,0:T(8,128)(2,1)} %get-tuple-element.5), channel_id=1, source_target_pairs={{0,15},{1,14},{2,13},{3,12},{4,11},{5,10},{6,9},{7,8},{8,7},{9,6},... | collective-permute-start | bytes 393224 | tf_op jit(solution)/shard_map/ppermute | solution.py:108
  110.4 0.0 copy-done.1
  110.4 0.0 copy-done.5
  110.4 0.0 copy-done.8
  110.4 0.0 copy-done.9
  110.4 0.0 copy-start.3
  110.4 0.9 fusion.48
  111.4 0.9 copy.21
  112.3 6.1 %collective-permute-done.1 = bf16[2,256,128]{2,1,0:T(8,128)(2,1)S(1)} collective-permute-done((bf16[2,256,128]{2,1,0:T(8,128)(2,1)}, bf16[2,256,128]{2,1,0:T(8,128)(2,1)S(1)}, u32[]{:S(2)}, u32[]{:S(2)}) %collective-permute-start.1) | collective-permute-done | bytes 131104 | tf_op jit(solution)/shard_map/ppermute | solution.py:108
  118.4 0.0 copy-done.3
  118.4 1.0 copy.20
  (5 shorter events, 0.1 us)
Async XLA Ops:
  7.2 74.8 %copy-start = (bf16[512,3,128]{2,0,1:T(8,128)(2,1)S(1)}, bf16[512,3,128]{2,0,1:T(8,128)(2,1)}, u32[]{:S(2)}) copy-start(bf16[512,3,128]{2,0,1:T(8,128)(2,1)} %param.11) | copy-start | bytes 1179652
  7.2 3.8 %copy-start.4 = (s32[3,512]{1,0:T(4,128)S(1)}, s32[3,512]{1,0:T(4,128)}, u32[]{:S(2)}) copy-start(s32[3,512]{1,0:T(4,128)} %param.15) | copy-start | bytes 18436
  7.2 3.8 %copy-start.6 = (bf16[512,3,128]{2,0,1:T(8,128)(2,1)S(1)}, bf16[512,3,128]{2,0,1:T(8,128)(2,1)}, u32[]{:S(2)}) copy-start(bf16[512,3,128]{2,0,1:T(8,128)(2,1)} %param.12) | copy-start | bytes 1179652
  7.2 87.5 %all-gather.2.cloned.1.call-start = ((), (), s32[]{:S(2)}) async-start(), calls=%async_computation.1 | async-start | bytes 8912896 | tf_op jit(solution)/shard_map/all_gather | solution.py:100
  11.0 11.8 %copy-start.2 = (bf16[512,2,128]{2,1,0:T(2,128)(2,1)S(1)}, bf16[512,2,128]{2,1,0:T(2,128)(2,1)}, u32[]{:S(2)}) copy-start(bf16[512,2,128]{2,1,0:T(2,128)(2,1)} %param.8) | copy-start | bytes 786436
  11.7 14.2 %copy-start.7 = (bf16[3,512]{1,0:T(4,128)(2,1)S(1)}, bf16[3,512]{1,0:T(4,128)(2,1)}, u32[]{:S(2)}) copy-start(bf16[3,512]{1,0:T(4,128)(2,1)} %param.14) | copy-start | bytes 9220
  12.8 45.8 %all-to-all-start = ((bf16[2,3,16,32,128]{4,3,1,0,2:T(8,128)(2,1)}), bf16[2,3,16,32,128]{4,3,1,0,2:T(8,128)(2,1)S(1)}, u32[]{:S(2)}, u32[]{:S(2)}) async-start(bf16[2,3,16,32,128]{4,3,1,0,2:T(8,128)(2,1)} %copy.24), calls=%async_computation | async-start | bytes 1572864 | tf_op jit(solution)/shard_map/all_to_all | solution.py:145
  22.9 35.0 %collective-permute-start = (bf16[2,256,128]{2,1,0:T(8,128)(2,1)S(1)}, bf16[2,256,128]{2,1,0:T(8,128)(2,1)S(1)}, u32[]{:S(2)}, u32[]{:S(2)}) collective-permute-start(bf16[2,256,128]{2,1,0:T(8,128)(2,1)S(1)} %get-tuple-element.13), channel_id=1, source_target_pairs={{0,15},{1,14},{2,13},{3,12},{4,11},{5,10},{6,9},{7,8},{8,7},{9,6},... | collective-permute-start | bytes 393224 | tf_op jit(solution)/shard_map/ppermute | solution.py:102
  88.8 21.7 %copy-start.1 = (bf16[2,3,512,128]{3,2,1,0:T(8,128)(2,1)S(1)}, bf16[2,3,512,128]{3,2,1,0:T(8,128)(2,1)}, u32[]{:S(2)}) copy-start(bf16[2,3,512,128]{3,2,1,0:T(8,128)(2,1)} %all_gather.7) | copy-start | bytes 2359300
  88.8 21.7 %copy-start.5 = (f32[3,512]{1,0:T(4,128)S(1)}, f32[3,512]{1,0:T(4,128)}, u32[]{:S(2)}) copy-start(f32[3,512]{1,0:T(4,128)} %fusion.60) | copy-start | bytes 18436
  88.8 21.7 %copy-start.8 = (bf16[3,512,512]{1,2,0:T(8,128)(2,1)S(1)}, bf16[3,512,512]{1,2,0:T(8,128)(2,1)}, u32[]{:S(2)}) copy-start(bf16[3,512,512]{1,2,0:T(8,128)(2,1)} %get-tuple-element.15) | copy-start | bytes 4718596
  88.8 21.7 %copy-start.9 = (f32[3,512]{1,0:T(4,128)S(1)}, f32[3,512]{1,0:T(4,128)}, u32[]{:S(2)}) copy-start(f32[3,512]{1,0:T(4,128)} %get-tuple-element.14) | copy-start | bytes 18436
  108.8 9.5 %collective-permute-start.1 = (bf16[2,256,128]{2,1,0:T(8,128)(2,1)}, bf16[2,256,128]{2,1,0:T(8,128)(2,1)S(1)}, u32[]{:S(2)}, u32[]{:S(2)}) collective-permute-start(bf16[2,256,128]{2,1,0:T(8,128)(2,1)} %get-tuple-element.5), channel_id=1, source_target_pairs={{0,15},{1,14},{2,13},{3,12},{4,11},{5,10},{6,9},{7,8},{8,7},{9,6},... | collective-permute-start | bytes 393224 | tf_op jit(solution)/shard_map/ppermute | solution.py:108
  110.4 7.9 %copy-start.3 = (bf16[2,256,128]{2,1,0:T(8,128)(2,1)S(1)}, bf16[2,256,128]{2,1,0:T(8,128)(2,1)}, u32[]{:S(2)}) copy-start(bf16[2,256,128]{2,1,0:T(8,128)(2,1)} %get-tuple-element.4) | copy-start | bytes 393220
Sparse Core Ops, SparseCore 0:
  9.9 84.7 all-gather.1

commit v16 on v15

--- a/solution.py
+++ b/solution.py
@@ -11,6 +11,7 @@
 NEGATIVE = -1e30
 KEY_BLOCK = 4096
 TAIL_BLOCK = 512
+LOG2E = 1.4426950408889634
 
 
 def flash_kernel(info_ref, q_ref, k_ref, v_ref, own_ref, lent_ref, *, scale, block):
@@ -25,14 +26,14 @@
         scores = lax.dot_general(
             q_ref[0, 0], k_ref[0, pl.ds(first, wide), :], (((1,), (1,)), ((), ())),
             preferred_element_type=jnp.float32,
-        ) * scale
+        ) * (scale * LOG2E)
         if masked:
             rows = lax.broadcasted_iota(jnp.int32, scores.shape, 0) + offset
             cols = lax.broadcasted_iota(jnp.int32, scores.shape, 1)
             scores = jnp.where(cols <= rows, scores, NEGATIVE)
         m_new = jnp.maximum(m_prev, jnp.max(scores, axis=1, keepdims=True))
-        shrink = jnp.exp(m_prev - m_new)
-        weights = jnp.exp(scores - m_new)
+        shrink = jnp.exp2(m_prev - m_new)
+        weights = jnp.exp2(scores - m_new)
         l_new = l_prev * shrink + jnp.sum(weights, axis=1, keepdims=True)
         moved = jnp.dot(
             weights.astype(jnp.bfloat16), v_ref[0, pl.ds(first, wide), :],

time: 127 us -> 126 us (level)
  no operation moved by 1% of the time
where the time goes in v16:
time: 126 us
  waiting for transfers between devices  41.4 us (33%)
  blocking collectives  23.2 us (18%)
  starting transfers between devices  14.5 us (12%)
  between operations  14.2 us (11%)
  Pallas kernels  13.7 us (11%)
  other arithmetic  8.59 us (7%)
  matrix products  5.96 us (5%)
  local copies, waits for them, and re-layouts  4.24 us (3%)
    ppermute x1, waiting for transfers between devices, dense_heads(): lent = lax.ppermute(rows_first[:, half:], 'seq', swap)  29.3 us
    all_gather x1, blocking collectives, sparse_heads(): picked_kv = lax.all_gather(own, 'seq', axis=2, tiled=True)  23.2 us
    pallas_call x1, Pallas kernels, dense_flash(): pl.pallas_call(functools.partial(flash_kernel, scale=scale, block=block),...  13.7 us
    all_to_all x1, starting transfers between devices, sparse_heads(): arrived = lax.all_to_all(pieces, 'seq', 2, 2, tiled=True)  9.98 us
    ppermute x1, waiting for transfers between devices, dense_heads(): returned = lax.ppermute(theirs, 'seq', swap)  6.13 us
    all_gather x1, waiting for transfers between devices, dense_heads(): gathered = lax.all_gather(stacked, 'seq', axis=2, tiled=True)  5.97 us
    sub x1, other arithmetic, attend_ranked(): weights = jnp.where(visible, jnp.exp(scores - leading), 0.0)  4.69 us
    ppermute x1, starting transfers between devices, dense_heads(): lent = lax.ppermute(rows_first[:, half:], 'seq', swap)  2.93 us
  transfers between devices with their start and end apart: 4, of which 3 were waited for; matrix products, arithmetic and copies ran while one was open for 12% of the time, Pallas kernels for 0%

profile of v16, /device:TPU:1, one launch (start us, length us, event | category | flops | bytes accessed | tf_op | source)
XLA Modules:
  0.0 125.8 jit_solution(13102908737821105306)
XLA Ops:
  7.2 0.0 copy-start
  7.2 0.0 copy-start.4
  7.2 0.0 copy-start.6
  7.2 0.0 all-gather.2.cloned.1.call-start
  7.2 1.2 copy_bitcast_fusion
  8.4 0.9 pad_maximum_fusion.1
  9.3 0.0 all-gather.2.cloned.1.call-update
  9.3 1.7 %fusion.42 = bf16[3,512,128]{2,1,0:T(8,128)(2,1)S(1)} fusion(bf16[512,3,128]{2,0,1:T(8,128)(2,1)} %param.13, s32[512]{0:T(512)S(1)} %iota_add_fusion, s32[3,512]{1,0:T(4,128)} %param.15), kind=kOutput, calls=%fused_computation.34 | convolution fusion | flops 202309632 | bytes 794624 | tf_op jit(solution)/shard_map/ent,ted->end/dot_general | solution.py:138
  11.0 0.0 copy-done.4
  11.0 0.0 copy-done.6
  11.0 0.0 copy-start.2
  11.0 0.6 fusion.39
  11.7 0.0 copy-start.7
  11.7 0.1 pad_maximum_fusion
  11.8 1.1 copy.24
  12.8 10.0 %all-to-all-start = ((bf16[2,3,16,32,128]{4,3,1,0,2:T(8,128)(2,1)}), bf16[2,3,16,32,128]{4,3,1,0,2:T(8,128)(2,1)S(1)}, u32[]{:S(2)}, u32[]{:S(2)}) async-start(bf16[2,3,16,32,128]{4,3,1,0,2:T(8,128)(2,1)} %copy.24), calls=%async_computation | async-start | bytes 1572864 | tf_op jit(solution)/shard_map/all_to_all | solution.py:146
  22.8 0.0 copy-done.2
  22.9 2.9 %collective-permute-start = (bf16[2,256,128]{2,1,0:T(8,128)(2,1)S(1)}, bf16[2,256,128]{2,1,0:T(8,128)(2,1)S(1)}, u32[]{:S(2)}, u32[]{:S(2)}) collective-permute-start(bf16[2,256,128]{2,1,0:T(8,128)(2,1)S(1)} %get-tuple-element.13), channel_id=1, source_target_pairs={{0,15},{1,14},{2,13},{3,12},{4,11},{5,10},{6,9},{7,8},{8,7},{9,6},... | collective-permute-start | bytes 393224 | tf_op jit(solution)/shard_map/ppermute | solution.py:103
  25.8 0.1 multiply_subtract_fusion
  25.9 0.0 copy-done.7
  25.9 0.6 fusion.3
  26.6 0.6 fusion.60
  27.2 0.6 pad_add_fusion.1.info_ref
  27.8 0.8 iota_compare_fusion
  28.6 29.3 %collective-permute-done = bf16[2,256,128]{2,1,0:T(8,128)(2,1)S(1)} collective-permute-done((bf16[2,256,128]{2,1,0:T(8,128)(2,1)S(1)}, bf16[2,256,128]{2,1,0:T(8,128)(2,1)S(1)}, u32[]{:S(2)}, u32[]{:S(2)}) %collective-permute-start) | collective-permute-done | bytes 131104 | tf_op jit(solution)/shard_map/ppermute | solution.py:103
  57.9 0.7 pad_maximum_fusion.2.q_ref
  58.6 0.0 all-to-all-done
  58.6 0.1 reduce_sum.21
  58.8 23.2 %all_gather.7 = bf16[2,3,512,128]{3,2,1,0:T(8,128)(2,1)} all-gather(bf16[2,3,32,128]{3,2,1,0:T(8,128)(2,1)S(1)} %reduce_sum.21), channel_id=1, replica_groups=mesh['dp'=4,'head'=4,'seq'=16] {'seq'}, dimensions={2}, use_global_device_ids=true | all-gather | bytes 835584 | tf_op jit(solution)/shard_map/all_gather | solution.py:148
  82.0 0.0 copy-done
  82.0 2.1 %fusion.52 = f32[3,512,512]{1,2,0:T(8,128)S(1)} fusion(bf16[512,3,128]{2,0,1:T(8,128)(2,1)S(1)} %copy-done, s32[512]{0:T(512)S(1)} %iota_add_fusion, s32[3,512]{1,0:T(4,128)S(1)} %copy-done.4, bf16[2,3,512,128]{3,2,1,0:T(8,128)(2,1)} %all_gather.7), kind=kOutput, calls=%fused_computation.37 | convolution fusion | flops 403636224 | bytes 3940352 | tf_op jit(solution)/shard_map/erd,ekd->erk/dot_general | solution.py:118
  84.1 4.7 %fusion.64 = (f32[3,512]{1,0:T(4,128)}, bf16[3,512,512]{1,2,0:T(8,128)(2,1)}) fusion(f32[3,512,512]{1,2,0:T(8,128)S(1)} %fusion.52, pred[512,512]{0,1:T(8,128)(4,1)} %iota_compare_fusion), kind=kOutput, calls=%fused_computation.66 | output fusion | flops 6291967 | bytes 4986880 | tf_op jit(solution)/shard_map/sub | solution.py:122
  88.8 0.0 copy-start.1
  88.8 0.0 copy-start.5
  88.8 0.0 copy-start.8
  88.8 6.0 %all-gather.2.cloned.1.call-done.k_ref.v_ref = bf16[2,2,8192,128]{3,2,1,0:T(8,128)(2,1)} async-done(((bf16[2,2,512,128]{3,2,1,0:T(8,128)(2,1)}), bf16[2,2,8192,128]{3,2,1,0:T(8,128)(2,1)}) %all-gather.2.cloned.1.call-update) | async-done | bytes 8388624 | tf_op jit(solution)/shard_map/all_gather | solution.py:101
  94.7 13.7 %shard_map.95 = (bf16[2,256,128]{2,1,0:T(8,128)(2,1)}, bf16[2,256,128]{2,1,0:T(8,128)(2,1)}) custom-call(s32[4]{0:T(128)} %pad_add_fusion.1.info_ref, bf16[2,2,256,128]{3,2,1,0:T(8,128)(2,1)} %pad_maximum_fusion.2.q_ref, bf16[2,2,8192,128]{3,2,1,0:T(8,128)(2,1)} %all-gather.2.cloned.1.call-done.k_ref.v_ref, ...), custom_call_target="tpu_custom_call" | custom-call | flops 2147483648 | bytes 4718592 | tf_op jit(solution)/shard_map/pallas_call | solution.py:71
  108.4 1.6 %collective-permute-start.1 = (bf16[2,256,128]{2,1,0:T(8,128)(2,1)}, bf16[2,256,128]{2,1,0:T(8,128)(2,1)S(1)}, u32[]{:S(2)}, u32[]{:S(2)}) collective-permute-start(bf16[2,256,128]{2,1,0:T(8,128)(2,1)} %get-tuple-element.5), channel_id=1, source_target_pairs={{0,15},{1,14},{2,13},{3,12},{4,11},{5,10},{6,9},{7,8},{8,7},{9,6},... | collective-permute-start | bytes 393224 | tf_op jit(solution)/shard_map/ppermute | solution.py:109
  110.0 0.0 copy-done.1
  110.0 0.0 copy-done.5
  110.0 0.0 copy-done.8
  110.0 0.0 copy-done.9
  110.0 0.0 copy-start.3
  110.0 0.9 fusion.48
  110.9 0.9 copy.21
  111.9 6.1 %collective-permute-done.1 = bf16[2,256,128]{2,1,0:T(8,128)(2,1)S(1)} collective-permute-done((bf16[2,256,128]{2,1,0:T(8,128)(2,1)}, bf16[2,256,128]{2,1,0:T(8,128)(2,1)S(1)}, u32[]{:S(2)}, u32[]{:S(2)}) %collective-permute-start.1) | collective-permute-done | bytes 131104 | tf_op jit(solution)/shard_map/ppermute | solution.py:109
  118.0 0.0 copy-done.3
  118.0 1.0 copy.20
  (5 shorter events, 0.1 us)
Async XLA Ops:
  7.2 74.8 %copy-start = (bf16[512,3,128]{2,0,1:T(8,128)(2,1)S(1)}, bf16[512,3,128]{2,0,1:T(8,128)(2,1)}, u32[]{:S(2)}) copy-start(bf16[512,3,128]{2,0,1:T(8,128)(2,1)} %param.11) | copy-start | bytes 1179652
  7.2 3.8 %copy-start.4 = (s32[3,512]{1,0:T(4,128)S(1)}, s32[3,512]{1,0:T(4,128)}, u32[]{:S(2)}) copy-start(s32[3,512]{1,0:T(4,128)} %param.15) | copy-start | bytes 18436
  7.2 3.8 %copy-start.6 = (bf16[512,3,128]{2,0,1:T(8,128)(2,1)S(1)}, bf16[512,3,128]{2,0,1:T(8,128)(2,1)}, u32[]{:S(2)}) copy-start(bf16[512,3,128]{2,0,1:T(8,128)(2,1)} %param.12) | copy-start | bytes 1179652
  7.2 87.5 %all-gather.2.cloned.1.call-start = ((), (), s32[]{:S(2)}) async-start(), calls=%async_computation.1 | async-start | bytes 8912896 | tf_op jit(solution)/shard_map/all_gather | solution.py:101
  11.0 11.8 %copy-start.2 = (bf16[512,2,128]{2,1,0:T(2,128)(2,1)S(1)}, bf16[512,2,128]{2,1,0:T(2,128)(2,1)}, u32[]{:S(2)}) copy-start(bf16[512,2,128]{2,1,0:T(2,128)(2,1)} %param.8) | copy-start | bytes 786436
  11.7 14.2 %copy-start.7 = (bf16[3,512]{1,0:T(4,128)(2,1)S(1)}, bf16[3,512]{1,0:T(4,128)(2,1)}, u32[]{:S(2)}) copy-start(bf16[3,512]{1,0:T(4,128)(2,1)} %param.14) | copy-start | bytes 9220
  12.8 45.8 %all-to-all-start = ((bf16[2,3,16,32,128]{4,3,1,0,2:T(8,128)(2,1)}), bf16[2,3,16,32,128]{4,3,1,0,2:T(8,128)(2,1)S(1)}, u32[]{:S(2)}, u32[]{:S(2)}) async-start(bf16[2,3,16,32,128]{4,3,1,0,2:T(8,128)(2,1)} %copy.24), calls=%async_computation | async-start | bytes 1572864 | tf_op jit(solution)/shard_map/all_to_all | solution.py:146
  22.9 35.0 %collective-permute-start = (bf16[2,256,128]{2,1,0:T(8,128)(2,1)S(1)}, bf16[2,256,128]{2,1,0:T(8,128)(2,1)S(1)}, u32[]{:S(2)}, u32[]{:S(2)}) collective-permute-start(bf16[2,256,128]{2,1,0:T(8,128)(2,1)S(1)} %get-tuple-element.13), channel_id=1, source_target_pairs={{0,15},{1,14},{2,13},{3,12},{4,11},{5,10},{6,9},{7,8},{8,7},{9,6},... | collective-permute-start | bytes 393224 | tf_op jit(solution)/shard_map/ppermute | solution.py:103
  88.8 21.2 %copy-start.1 = (bf16[2,3,512,128]{3,2,1,0:T(8,128)(2,1)S(1)}, bf16[2,3,512,128]{3,2,1,0:T(8,128)(2,1)}, u32[]{:S(2)}) copy-start(bf16[2,3,512,128]{3,2,1,0:T(8,128)(2,1)} %all_gather.7) | copy-start | bytes 2359300
  88.8 21.2 %copy-start.5 = (f32[3,512]{1,0:T(4,128)S(1)}, f32[3,512]{1,0:T(4,128)}, u32[]{:S(2)}) copy-start(f32[3,512]{1,0:T(4,128)} %fusion.60) | copy-start | bytes 18436
  88.8 21.2 %copy-start.8 = (bf16[3,512,512]{1,2,0:T(8,128)(2,1)S(1)}, bf16[3,512,512]{1,2,0:T(8,128)(2,1)}, u32[]{:S(2)}) copy-start(bf16[3,512,512]{1,2,0:T(8,128)(2,1)} %get-tuple-element.15) | copy-start | bytes 4718596
  88.8 21.3 %copy-start.9 = (f32[3,512]{1,0:T(4,128)S(1)}, f32[3,512]{1,0:T(4,128)}, u32[]{:S(2)}) copy-start(f32[3,512]{1,0:T(4,128)} %get-tuple-element.14) | copy-start | bytes 18436
  108.4 9.6 %collective-permute-start.1 = (bf16[2,256,128]{2,1,0:T(8,128)(2,1)}, bf16[2,256,128]{2,1,0:T(8,128)(2,1)S(1)}, u32[]{:S(2)}, u32[]{:S(2)}) collective-permute-start(bf16[2,256,128]{2,1,0:T(8,128)(2,1)} %get-tuple-element.5), channel_id=1, source_target_pairs={{0,15},{1,14},{2,13},{3,12},{4,11},{5,10},{6,9},{7,8},{8,7},{9,6},... | collective-permute-start | bytes 393224 | tf_op jit(solution)/shard_map/ppermute | solution.py:109
  110.0 8.0 %copy-start.3 = (bf16[2,256,128]{2,1,0:T(8,128)(2,1)S(1)}, bf16[2,256,128]{2,1,0:T(8,128)(2,1)}, u32[]{:S(2)}) copy-start(bf16[2,256,128]{2,1,0:T(8,128)(2,1)} %get-tuple-element.4) | copy-start | bytes 393220
Sparse Core Ops, SparseCore 0:
  9.9 84.7 all-gather.1
